TPU v7x, 128 devices: a whole 4x4x4 slice. The times are simulated.
128 devices in a mesh: kv: 32 (over y, z, core), hd: 4 (over x).
Axes of the slice: x: 4, y: 4, z: 4, core: 2. Of those that a mesh axis runs over, the one named last changes fastest.
Arguments:
- kv_cache: bfloat16 [64, 16384, 256], P(None, 'kv'), may hold values from -6 to 6
- keep_lists: int32 [64, 16384], P(None, 'kv'), may hold values from 0 to 511, as said below
- kept_counts: int32 [64, 32], P(None, 'kv'), may hold values from 64 to 511
- drop_scores: float32 [64, 16384], P(None, 'kv'), may hold values from 0.01 to 10
- lengths: int32 [64], replicated, may hold values from 4096 to 16384, as said below
- offsets: int32 [64], replicated, may hold values from 0 to 31, as said below
- queries: bfloat16 [64, 2048], P(None, 'hd'), may hold values from -100 to 100
- out_weight: bfloat16 [2048, 2048], P('hd'), may hold values from -0.125 to 0.125
Outputs:
- projected: bfloat16 [64, 2048], P('kv', 'hd')
Inputs may be any that keep to these rules, and one draw needn't show every extreme that they name: `keep_lists`: each aligned run of 512 entries is an ordering of 0 to 511. `lengths`: some request has length exactly 16384. `offsets`: exactly 32 requests have a nonzero offset; no nonzero value is taken by more than 2 requests, and one by exactly 2.
All inputs are finite; a program needn't handle non-finite values.
Results may differ from a plain program's by a relative error of at most 0.006.
Values may be sent and summed in bfloat16 or wider, within the bound.
No kernel may reach another device: no remote copies, remote signals or barrier semaphores. Data moves between devices by JAX's collectives and lax.ppermute only.
A program may use at most 128 MiB of HBM per device.

v0:
```python
import math

import jax
import jax.numpy as jnp
from jax import lax
from jax.sharding import PartitionSpec as P


def combined_all(value, axis, join):
    pieces = jax.tree.map(lambda part: lax.all_gather(part, axis), value)
    head = jax.tree.map(lambda part: part[0], pieces)
    tail = jax.tree.map(lambda part: part[1:], pieces)
    total, _ = lax.scan(lambda total, piece: (join(total, piece), None), head, tail)
    return total


def codes_for(keep_block, count_block, score_block, lengths, block_index):
    requests, block_rows = keep_block.shape
    row_index = jnp.arange(requests, dtype=jnp.int32)[:, None]
    places = jnp.broadcast_to(
        jnp.arange(block_rows, dtype=jnp.int32)[None, :], (requests, block_rows)
    )
    rank_in_list = (
        jnp.zeros((requests, block_rows), jnp.int32).at[row_index, keep_block].set(places)
    )
    kept_rows = rank_in_list < count_block[:, None]
    position = block_index * block_rows + jnp.arange(block_rows, dtype=jnp.int32)
    valid_rows = position[None, :] < lengths[:, None]
    return jnp.where(valid_rows & kept_rows, -1.0, jnp.where(valid_rows, score_block, 0.0))


def block_partial(block_data, codes, queries_h):
    head_dim = queries_h.shape[-1]
    factor = 1.0 / math.sqrt(head_dim)
    kept_rows = codes < 0.0
    weight = jnp.maximum(codes, 0.0)
    totals = jnp.sum(weight, axis=1)
    has_merged = totals > 0.0
    floored = jnp.maximum(totals, 1.0)
    shares = (weight / floored[:, None]).astype(jnp.bfloat16)
    merged = jnp.einsum(
        "rb,rbc->rc", shares, block_data, preferred_element_type=jnp.float32
    ).astype(jnp.bfloat16)
    scores_qk = (
        jnp.einsum(
            "rhc,rbc->rhb",
            queries_h,
            block_data[..., :head_dim],
            preferred_element_type=jnp.float32,
        )
        * factor
    )
    merged_score = (
        jnp.einsum(
            "rhc,rc->rh", queries_h, merged[:, :head_dim], preferred_element_type=jnp.float32
        )
        * factor
    )
    merged_score = merged_score + jnp.log(floored)[:, None]
    scores_qk = jnp.where(kept_rows[:, None, :], scores_qk, -1e30)
    merged_score = jnp.where(has_merged[:, None], merged_score, -1e30)
    peaks = jnp.maximum(jnp.max(scores_qk, axis=-1), merged_score)
    probs = jnp.where(kept_rows[:, None, :], jnp.exp(scores_qk - peaks[..., None]), 0.0)
    merged_prob = jnp.where(has_merged[:, None], jnp.exp(merged_score - peaks), 0.0)
    mass = jnp.sum(probs, axis=-1) + merged_prob
    weighted = jnp.einsum(
        "rhb,rbc->rhc",
        probs.astype(jnp.bfloat16),
        block_data[..., head_dim:],
        preferred_element_type=jnp.float32,
    )
    merged_value = merged[:, head_dim:].astype(jnp.float32)
    weighted = (
        weighted
        + merged_prob.astype(jnp.bfloat16).astype(jnp.float32)[..., None] * merged_value[:, None, :]
    )
    return (peaks, mass, weighted)


def route_tables(offsets, devices, capacity):
    requests = offsets.shape[0]
    one_hot = (offsets[:, None] == jnp.arange(devices, dtype=jnp.int32)[None, :]).astype(jnp.int32)
    position = jnp.sum(jnp.cumsum(one_hot, axis=0) * one_hot, axis=1) - 1
    table = (
        jnp.zeros((devices, capacity), jnp.int32)
        .at[offsets, position]
        .set(jnp.arange(requests, dtype=jnp.int32), mode="drop")
    )
    filled = jnp.zeros((devices, capacity), jnp.bool_).at[offsets, position].set(True, mode="drop")
    return (table, filled, position)


def pack_slots(values, table, filled, device, devices, direction):
    targets = jnp.arange(devices, dtype=jnp.int32)
    amount = direction * (device - targets) % devices
    chosen = table[amount]
    live_slots = filled[amount] & (amount != 0)[:, None]
    gathered = values[chosen]
    live_slots = live_slots.reshape(live_slots.shape + (1,) * (values.ndim - 1))
    return jnp.where(live_slots, gathered, jnp.zeros((), values.dtype))


def unpack_slots(received, values, offsets, position, device, devices, capacity, direction):
    source = (device + direction * offsets) % devices
    slots = source * capacity + jnp.minimum(position, capacity - 1)
    stacked = received.reshape((devices * capacity,) + received.shape[2:])
    taken = stacked[slots]
    moving = (offsets != 0).reshape((-1,) + (1,) * (values.ndim - 1))
    return jnp.where(moving, taken, values)


def join_partials(first, second):
    peak_one, mass_one, sum_one = first
    peak_two, mass_two, sum_two = second
    largest = jnp.maximum(peak_one, peak_two)
    scale_one = jnp.exp(peak_one - largest)
    scale_two = jnp.exp(peak_two - largest)
    return (
        largest,
        mass_one * scale_one + mass_two * scale_two,
        sum_one * scale_one[..., None] + sum_two * scale_two[..., None],
    )


def body(kv_cache, keep_lists, kept_counts, drop_scores, lengths, offsets, queries, out_weight):
    devices = lax.axis_size("kv")
    device = lax.axis_index("kv")
    requests, block_rows, width = kv_cache.shape
    head_dim = width // 2
    capacity = (requests // 2 + devices - 2) // (devices - 1)
    per_device = requests // devices
    codes = codes_for(keep_lists, kept_counts[:, 0], drop_scores, lengths, device)
    table, filled, position = route_tables(offsets, devices, capacity)
    outgoing = pack_slots(kv_cache, table, filled, device, devices, 1)
    received = lax.all_to_all(outgoing, "kv", split_axis=0, concat_axis=0, tiled=True)
    block_data = unpack_slots(received, kv_cache, offsets, position, device, devices, capacity, 1)
    queries_h = queries.reshape(requests, -1, head_dim)
    peaks, mass, weighted = block_partial(block_data, codes, queries_h)
    peaks_all, mass_all, weighted_all = combined_all((peaks, mass, weighted), "kv", join_partials)
    mass_own = lax.dynamic_slice_in_dim(mass_all, device * per_device, per_device, 0)
    weighted_own = lax.dynamic_slice_in_dim(weighted_all, device * per_device, per_device, 0)
    attended = weighted_own / mass_own[..., None]
    attended = attended.astype(jnp.bfloat16).reshape(per_device, -1)
    partial_out = jnp.dot(attended, out_weight, preferred_element_type=jnp.float32)
    return lax.psum_scatter(partial_out, "hd", scatter_dimension=1, tiled=True).astype(jnp.bfloat16)


def solution(mesh):
    in_specs = (
        P(None, "kv", None),
        P(None, "kv"),
        P(None, "kv"),
        P(None, "kv"),
        P(),
        P(),
        P(None, "hd"),
        P("hd", None),
    )
    out_specs = P("kv", "hd")
    return jax.shard_map(body, mesh=mesh, in_specs=in_specs, out_specs=out_specs, check_vma=False)
```

profile of v0, /device:TPU:0, one launch (start us, length us, event | category | flops | bytes accessed | tf_op | source)
XLA Modules:
  0.0 496.2 jit_solution(9559754667904156106)
XLA Ops:
  9.1 3.6 scatter_fusion
  12.8 3.5 scatter_fusion.1
  17.9 13.1 %gather_fusion.2 = bf16[64,512,256]{2,1,0:T(8,128)(2,1)} fusion(bf16[64,512,256]{2,1,0:T(8,128)(2,1)} %param.10, s32[1024]{0:T(1024)S(1)} %pad_clamp_fusion.1), kind=kCustom, calls=%fused_computation.2 | custom fusion | bytes 33554688 | tf_op jit(solution)/shard_map/gather | solution.py:98
  31.1 14.0 %broadcast_select_fusion.1 = bf16[32,2,512,256]{3,2,1,0:T(8,128)(2,1)} fusion(bf16[32,2,512,256]{3,2,1,0:T(8,128)(2,1)} %bitcast.83, pred[32,2]{1,0:T(8,128)(4,1)S(1)} %broadcast_and_fusion), kind=kLoop, calls=%fused_computation.16 | loop fusion | flops 8388608 | bytes 33554496 | tf_op jit(solution)/shard_map/jit(_where)/select_n | solution.py:100
  45.1 8.7 %all-to-all-start = ((bf16[32,2,512,256]{3,2,1,0:T(8,128)(2,1)}), bf16[32,2,512,256]{3,2,1,0:T(8,128)(2,1)}, u32[]{:S(2)}, u32[]{:S(2)}) async-start(bf16[32,2,512,256]{3,2,1,0:T(8,128)(2,1)} %broadcast_select_fusion.1), calls=%async_computation | async-start | bytes 33554432 | tf_op jit(solution)/shard_map/all_to_all | solution.py:135
  54.3 120.1 %scatter_custom_fusion.2 = s32[32768]{0:T(1024)S(1)} fusion(s32[32768]{0:T(1024)S(1)} %bitcast.88, s32[32768]{0:T(1024)S(1)} %bitcast.89, s32[]{:T(128)} %copy.73), kind=kCustom, calls=%fused_computation.47 | custom fusion | bytes 131076
  175.5 119.2 %all-to-all-done = bf16[32,2,512,256]{3,2,1,0:T(8,128)(2,1)} async-done(((bf16[32,2,512,256]{3,2,1,0:T(8,128)(2,1)}), bf16[32,2,512,256]{3,2,1,0:T(8,128)(2,1)}, u32[]{:S(2)}, u32[]{:S(2)}) %all-to-all-start) | async-done | bytes 16777248 | tf_op jit(solution)/shard_map/all_to_all | solution.py:135
  294.7 13.2 %gather_fusion.3 = bf16[64,512,256]{2,1,0:T(8,128)(2,1)} fusion(bf16[64,512,256]{2,1,0:T(8,128)(2,1)} %bitcast.12, s32[1024]{0:T(1024)S(1)} %pad_clamp_fusion), kind=kCustom, calls=%fused_computation.3 | custom fusion | bytes 33554688 | tf_op jit(solution)/shard_map/gather | solution.py:107
  308.0 12.0 %broadcast_select_fusion = bf16[64,512,256]{2,1,0:T(8,128)(2,1)S(1)} fusion(bf16[64,512,256]{2,1,0:T(8,128)(2,1)} %gather_fusion.3, bf16[64,512,256]{2,1,0:T(8,128)(2,1)} %param.10, pred[64]{0:T(512)(128)(4,1)S(1)} %broadcast_compare_fusion.2), kind=kLoop, calls=%fused_computation.15 | loop fusion | flops 8388608 | bytes 50331712 | tf_op jit(solution)/shard_map/jit(_where)/select_n | solution.py:109
  319.9 2.3 fusion.27
  323.7 3.8 fusion.55
  328.9 2.8 fusion.10
  333.9 52.1 %all-gather.4 = f32[32,64,4]{1,2,0:T(4,128)S(1)} all-gather(f32[1,64,4]{1,2,0:T(4,128)S(1)} %copy.34), channel_id=3, replica_groups=mesh['kv'=32,'hd'=4] {'kv'}, dimensions={0}, use_global_device_ids=true | all-gather | bytes 33792 | tf_op jit(solution)/shard_map/all_gather | solution.py:10
  386.9 21.4 %all-gather.3 = f32[32,64,4]{1,2,0:T(4,128)S(1)} all-gather(f32[1,64,4]{1,2,0:T(4,128)S(1)} %copy.33), channel_id=2, replica_groups=mesh['kv'=32,'hd'=4] {'kv'}, dimensions={0}, use_global_device_ids=true | all-gather | bytes 33792 | tf_op jit(solution)/shard_map/all_gather | solution.py:10
  408.4 3.6 slice.71
  412.9 48.3 %while.14 = (s32[]{:T(128)}, f32[64,4]{0,1:T(4,128)S(1)}, f32[64,4]{0,1:T(4,128)S(1)}, f32[64,4,128]{2,1,0:T(4,128)S(1)}, f32[31,64,4]{1,2,0:T(4,128)S(1)}, /*in...) while((s32[]{:T(128)}, f32[64,4]{0,1:T(4,128)S(1)}, f32[64,4]{0,1:T(4,128)S(1)}, ...), condition=%wide.region_9.10_spmd, body=%wide.region_8.9_spmd.sunk | while | flops 99842 | bytes 407645 | solution.py:13
  413.2 1.3 fusion.63
  414.7 1.3 fusion.63
  416.3 1.3 fusion.63
  417.8 1.3 fusion.63
  419.4 1.3 fusion.63
  420.9 1.3 fusion.63
  422.5 1.3 fusion.63
  424.1 1.3 fusion.63
  425.6 1.3 fusion.63
  427.2 1.3 fusion.63
  428.7 1.3 fusion.63
  430.3 1.3 fusion.63
  431.8 1.3 fusion.63
  433.4 1.3 fusion.63
  435.0 1.3 fusion.63
  436.5 1.3 fusion.63
  438.1 1.3 fusion.63
  439.6 1.3 fusion.63
  441.2 1.3 fusion.63
  442.7 1.3 fusion.63
  444.3 1.3 fusion.63
  445.9 1.3 fusion.63
  447.4 1.3 fusion.63
  449.0 1.3 fusion.63
  450.5 1.3 fusion.63
  452.1 1.3 fusion.63
  453.6 1.3 fusion.63
  455.2 1.3 fusion.63
  456.8 1.3 fusion.63
  461.5 1.9 convolution_bitcast_fusion
  463.4 24.4 %reduce-scatter.4.cloned.1.call-done = f32[512,2]{1,0:T(8,128)} async-done(((f32[2048,2]{1,0:T(8,128)}), f32[512,2]{1,0:T(8,128)}) %reduce-scatter.4.cloned.1.call-update) | async-done | bytes 4112
  487.8 1.6 copy.41
  (178 shorter events, 22.2 us)
Async XLA Ops:
  6.5 454.9 %copy-start = (bf16[512,2048]{1,0:T(8,128)(2,1)S(1)}, bf16[512,2048]{1,0:T(8,128)(2,1)}, u32[]{:S(2)}) copy-start(bf16[512,2048]{1,0:T(8,128)(2,1)} %param.17) | copy-start | bytes 6291460
  45.1 8.8 %copy-start.2 = (s32[64,512]{1,0:T(8,128)S(1)}, s32[64,512]{1,0:T(8,128)}, u32[]{:S(2)}) copy-start(s32[64,512]{1,0:T(8,128)} %param.11) | copy-start | bytes 393220
  45.1 8.9 %copy-start.10 = (s32[2]{0:T(128)S(1)}, s32[2]{0:T(128)}, u32[]{:S(2)}) copy-start(s32[2]{0:T(128)} %constant.90) | copy-start | bytes 28
  45.1 9.0 %copy-start.9 = (s32[2]{0:T(128)S(1)}, s32[2]{0:T(128)}, u32[]{:S(2)}) copy-start(s32[2]{0:T(128)} %constant.93) | copy-start | bytes 28
  45.1 129.3 %copy-start.4 = (bf16[64,512]{1,0:T(8,128)(2,1)S(1)}, bf16[64,512]{1,0:T(8,128)(2,1)}, u32[]{:S(2)}) copy-start(bf16[64,512]{1,0:T(8,128)(2,1)} %param.16) | copy-start | bytes 196612
  45.1 129.4 %copy-start.6 = (s32[64]{0:T(128)S(1)}, s32[64]{0:T(128)}, u32[]{:S(2)}) copy-start(s32[64]{0:T(128)} %param.15) | copy-start | bytes 772
  45.1 129.4 %copy-start.3 = (f32[64,512]{1,0:T(8,128)S(1)}, f32[64,512]{1,0:T(8,128)}, u32[]{:S(2)}) copy-start(f32[64,512]{1,0:T(8,128)} %param.13) | copy-start | bytes 393220
  45.1 129.4 %copy-start.7 = (s32[64,1]{0,1:T(1,128)S(1)}, s32[64,1]{0,1:T(1,128)}, u32[]{:S(2)}) copy-start(s32[64,1]{0,1:T(1,128)} %param.12) | copy-start | bytes 772
  45.1 129.4 %copy-start.8 = (s32[64]{0:T(128)S(1)}, s32[64]{0:T(128)}, u32[]{:S(2)}) copy-start(s32[64]{0:T(128)} %param.14) | copy-start | bytes 772
  45.1 249.6 %all-to-all-start = ((bf16[32,2,512,256]{3,2,1,0:T(8,128)(2,1)}), bf16[32,2,512,256]{3,2,1,0:T(8,128)(2,1)}, u32[]{:S(2)}, u32[]{:S(2)}) async-start(bf16[32,2,512,256]{3,2,1,0:T(8,128)(2,1)} %broadcast_select_fusion.1), calls=%async_computation | async-start | bytes 33554432 | tf_op jit(solution)/shard_map/all_to_all | solution.py:135
  53.8 354.5 %all-gather.7.cloned.1.call-start = ((), (), s32[]{:S(2)}) async-start(), calls=%async_computation.2 | async-start | bytes 4325376 | tf_op jit(solution)/shard_map/all_gather | solution.py:10
  174.5 148.4 %copy-start.5 = (bf16[64,4,128]{2,1,0:T(4,128)(2,1)}, bf16[64,4,128]{2,1,0:T(4,128)(2,1)S(1)}, u32[]{:S(2)}) copy-start(bf16[64,4,128]{2,1,0:T(4,128)(2,1)S(1)} %reshape.139) | copy-start | bytes 196612
  328.3 0.6 copy-start.1
  331.7 156.0 %reduce-scatter.4.cloned.1.call-start = ((), (), s32[]{:S(2)}) async-start(), calls=%async_computation.3 | async-start | bytes 1310720
Sparse Core Ops, SparseCore 0:
  331.9 75.1 all-gather.6
  463.5 24.1 reduce-scatter.3
where the time goes:
time: 498 us; the launch traced here: 496 us
  local copies, waits for them, and re-layouts  169 us (34%)
  waiting for transfers between devices  144 us (29%)
  other arithmetic  75.3 us (15%)
  blocking collectives  73.6 us (15%)
  between operations  13.8 us (3%)
  matrix products  11.6 us (2%)
  starting transfers between devices  8.77 us (2%)
    unnamed x29, local copies, waits for them, and re-layouts  123 us
    all_to_all x1, waiting for transfers between devices, body(): lax.all_to_all(outgoing, 'kv', split_axis=0, concat_axis=0, tiled=True)  119 us
    all_gather x2, blocking collectives, combined_all(): pieces = jax.tree.map(lambda part: lax.all_gather(part, axis), value)  73.6 us
    add x31, other arithmetic, join_partials(): sum_one * scale_one[..., None] + sum_two * scale_two[..., None]  41 us
    unnamed x3, waiting for transfers between devices  24.4 us
    select_n x1, other arithmetic, pack_slots(): return jnp.where(live_slots, gathered, jnp.zeros((), values.dtype))  14 us
    gather x1, local copies, waits for them, and re-layouts, unpack_slots(): taken = stacked[slots]  13.2 us
    gather x1, local copies, waits for them, and re-layouts, pack_slots(): gathered = values[chosen]  13.1 us
  transfers between devices with their start and end apart: 3, of which 2 were waited for; matrix products, arithmetic and copies ran while one was open for 25% of the time, Pallas kernels for 0%

commit v1 on v0

--- a/solution.py
+++ b/solution.py
@@ -131,14 +131,17 @@
     per_device = requests // devices
     codes = codes_for(keep_lists, kept_counts[:, 0], drop_scores, lengths, device)
     table, filled, position = route_tables(offsets, devices, capacity)
-    outgoing = pack_slots(kv_cache, table, filled, device, devices, 1)
+    outgoing = pack_slots(codes, table, filled, device, devices, -1)
     received = lax.all_to_all(outgoing, "kv", split_axis=0, concat_axis=0, tiled=True)
-    block_data = unpack_slots(received, kv_cache, offsets, position, device, devices, capacity, 1)
+    held_codes = unpack_slots(received, codes, offsets, position, device, devices, capacity, -1)
     queries_h = queries.reshape(requests, -1, head_dim)
-    peaks, mass, weighted = block_partial(block_data, codes, queries_h)
-    peaks_all, mass_all, weighted_all = combined_all((peaks, mass, weighted), "kv", join_partials)
-    mass_own = lax.dynamic_slice_in_dim(mass_all, device * per_device, per_device, 0)
-    weighted_own = lax.dynamic_slice_in_dim(weighted_all, device * per_device, per_device, 0)
+    peaks, mass, weighted = block_partial(kv_cache, held_codes, queries_h)
+    largest = lax.pmax(peaks, "kv")
+    scale = jnp.exp(peaks - largest)
+    mass = mass * scale
+    weighted = weighted * scale[..., None]
+    mass_own = lax.psum_scatter(mass, "kv", scatter_dimension=0, tiled=True)
+    weighted_own = lax.psum_scatter(weighted, "kv", scatter_dimension=0, tiled=True)
     attended = weighted_own / mass_own[..., None]
     attended = attended.astype(jnp.bfloat16).reshape(per_device, -1)
     partial_out = jnp.dot(attended, out_weight, preferred_element_type=jnp.float32)

time: 498 us -> 561 us (1.13)
  blocking collectives: 73.6 us -> 249 us
  other arithmetic: 75.3 us -> 9.88 us
  local copies, waits for them, and re-layouts: 169 us -> 134 us
  waiting for transfers between devices: 144 us -> 123 us
  matrix products: 11.6 us -> 21.3 us
    pmax x0 -> x1, blocking collectives: none -> 125 us  [body(): largest = lax.pmax(peaks, 'kv')]
    unnamed x0 -> x1, blocking collectives: none -> 124 us
    all_to_all x1, waiting for transfers between devices: 119 us -> 3.7 us  [body(): lax.all_to_all(outgoing, 'kv', split_axis=0, concat_axis=0, tiled=True)]
    unnamed x3 -> x4, waiting for transfers between devices: 24.4 us -> 119 us
    all_gather x2 -> x0, blocking collectives: 73.6 us -> none  [combined_all(): pieces = jax.tree.map(lambda part: lax.all_gather(part, axis), value)]
    add x62 -> x0, other arithmetic: 41.9 us -> none  [the longest x31 41 us: join_partials(): sum_one * scale_one[..., None] + sum_two * scale_two[..., None]]
    select_n x1, other arithmetic: 14 us -> 0.77 us  [pack_slots(): return jnp.where(live_slots, gathered, jnp.zeros((), values.dtype))]
    gather x1, local copies, waits for them, and re-layouts: 13.2 us -> 0.65 us  [unpack_slots(): taken = stacked[slots]]
  transfers between devices with their start and end apart: 3 -> 3, of which waited for: 2 -> 3; matrix products, arithmetic and copies ran while one was open for 25% -> 1% of each run, Pallas kernels for 0% -> 0%
where the time goes in v1:
time: 561 us; the launch traced here: 560 us
  blocking collectives  249 us (44%)
  local copies, waits for them, and re-layouts  134 us (24%)
  waiting for transfers between devices  123 us (22%)
  matrix products  21.3 us (4%)
  between operations  14.3 us (3%)
  other arithmetic  9.88 us (2%)
  starting transfers between devices  8.5 us (2%)
    pmax x1, blocking collectives, body(): largest = lax.pmax(peaks, 'kv')  125 us
    unnamed x1, blocking collectives  124 us
    unnamed x9, local copies, waits for them, and re-layouts  123 us
    unnamed x4, waiting for transfers between devices  119 us
  transfers between devices with their start and end apart: 3, of which 3 were waited for; matrix products, arithmetic and copies ran while one was open for 1% of the time, Pallas kernels for 0%

profile of v1, /device:TPU:0, one launch (start us, length us, event | category | flops | bytes accessed | tf_op | source)
XLA Modules:
  0.0 560.2 jit_solution(17870855924349773127)
XLA Ops:
  6.6 0.9 fusion.29
  7.5 0.1 reduce_window_sum.11
  7.6 0.8 select_reduce_fusion
  8.4 0.7 fusion.46
  9.1 3.6 scatter_fusion
  12.7 0.1 copy.17
  12.8 3.5 scatter_fusion.1
  16.3 0.1 copy.18
  16.4 0.6 gather_fusion
  17.0 0.6 gather_fusion.1
  17.6 0.1 copy.19
  17.6 0.1 copy.20
  17.7 0.1 reshape.165
  17.9 0.9 fusion.23
  18.8 0.8 and_reduce_fusion
  19.6 0.8 multiply_reduce_fusion
  20.5 120.1 %scatter_custom_fusion.2 = s32[32768]{0:T(1024)S(1)} fusion(s32[32768]{0:T(1024)S(1)} %bitcast.58, s32[32768]{0:T(1024)S(1)} %bitcast.59, s32[]{:T(128)} %constant.21.clone.1), kind=kCustom, calls=%fused_computation.38 | custom fusion | bytes 131076
  140.6 1.0 fusion.22
  141.6 0.7 gather_fusion.2
  142.3 0.1 reshape.164
  142.3 0.1 broadcast_and_fusion
  142.4 0.8 broadcast_select_fusion
  143.2 8.4 %all-to-all-start = ((f32[32,2,512]{2,1,0:T(2,128)}), f32[32,2,512]{2,1,0:T(2,128)S(1)}, u32[]{:S(2)}, u32[]{:S(2)}) async-start(f32[32,2,512]{2,1,0:T(2,128)} %broadcast_select_fusion), calls=%async_computation | async-start | bytes 262144 | tf_op jit(solution)/shard_map/all_to_all | solution.py:135
  151.6 0.0 all-reduce.4.cloned.1.call-start
  151.6 0.7 compare_select_fusion.3
  152.3 0.7 broadcast_compare_fusion.2
  153.0 0.9 reshape.141
  153.8 1.2 dynamic-slice
  155.8 3.7 all-to-all-done
  159.5 0.1 reshape.140
  159.6 0.7 gather_fusion.3
  160.2 0.2 maximum_reduce_fusion
  160.5 0.1 fusion.28
  160.5 8.0 %fusion.24 = bf16[64,1,256]{2,1,0:T(2,128)(2,1)S(1)} fusion(bf16[64,512,256]{2,1,0:T(8,128)(2,1)} %param.8, bf16[64,512,1]{1,0,2:T(8,128)(2,1)S(1)} %fusion.28), kind=kOutput, calls=%fused_computation.30 | convolution fusion | flops 16777216 | bytes 16875520 | tf_op jit(solution)/shard_map/rb,rbc->rc/dot_general | solution.py:41
  168.6 0.2 fusion.30
  168.8 5.7 %fusion.50 = (f32[64,4]{1,0:T(8,128)S(1)}, f32[64,4,512]{2,1,0:T(4,128)S(1)}) fusion(bf16[64,4,128]{2,1,0:T(4,128)(2,1)S(1)} %reshape.141, bf16[64,512,256]{2,1,0:T(8,128)(2,1)} %param.8, pred[64,512]{1,0:T(8,128)(4,1)S(1)} %broadcast_compare_fusion), kind=kOutput, calls=%fused_computation.99 | convolution fusion | flops 33947392 | bytes 9012224 | tf_op jit(solution)/shard_map/rhc,rbc->rhb/dot_general | solution.py:45
  174.6 0.1 convert_convert_fusion
  174.7 125.3 %pmax.7 = f32[64,4]{1,0:T(8,128)S(1)} all-reduce(f32[64,4]{1,0:T(8,128)S(1)} %get-tuple-element.6), channel_id=1, replica_groups=mesh['kv'=32,'hd'=4] {'kv'}, use_global_device_ids=true, to_apply=%region_7.8 | all-reduce | flops 256 | bytes 2048 | tf_op jit(solution)/shard_map/pmax | solution.py:139
  299.9 0.4 fusion.16
  300.4 0.1 add_multiply_fusion
  300.5 123.8 %all-reduce.1 = f32[64,4]{1,0:T(8,128)S(1)} all-reduce(f32[64,4]{1,0:T(8,128)S(1)} %get-tuple-element.7), channel_id=3, replica_groups=mesh['kv'=32,'hd'=4] {'kv'}, use_global_device_ids=true, to_apply=%region_10.11.clone | all-reduce | flops 256 | bytes 2048
  424.2 5.4 fusion.10
  429.6 0.0 reduce-scatter.4.cloned.1.call-start
  429.7 96.3 %all-reduce.4.cloned.1.call-done = f32[64,4,128]{2,1,0:T(4,128)} async-done(((f32[64,4,128]{2,1,0:T(4,128)}), f32[64,4,128]{2,1,0:T(4,128)}) %all-reduce.4.cloned.1.call-update) | async-done | bytes 131088
  526.0 0.8 fusion.36
  526.8 1.9 convolution_bitcast_fusion
  528.7 23.0 %reduce-scatter.4.cloned.1.call-done = f32[512,2]{1,0:T(8,128)} async-done(((f32[2048,2]{1,0:T(8,128)}), f32[512,2]{1,0:T(8,128)}) %reduce-scatter.4.cloned.1.call-update) | async-done | bytes 4112
  551.7 1.6 copy.26
  (27 shorter events, 0.3 us)
Async XLA Ops:
  6.5 520.2 %copy-start = (bf16[512,2048]{1,0:T(8,128)(2,1)S(1)}, bf16[512,2048]{1,0:T(8,128)(2,1)}, u32[]{:S(2)}) copy-start(bf16[512,2048]{1,0:T(8,128)(2,1)} %param.15) | copy-start | bytes 6291460
  143.2 16.3 %all-to-all-start = ((f32[32,2,512]{2,1,0:T(2,128)}), f32[32,2,512]{2,1,0:T(2,128)S(1)}, u32[]{:S(2)}, u32[]{:S(2)}) async-start(f32[32,2,512]{2,1,0:T(2,128)} %broadcast_select_fusion), calls=%async_computation | async-start | bytes 262144 | tf_op jit(solution)/shard_map/all_to_all | solution.py:135
  151.6 374.4 %all-reduce.4.cloned.1.call-start = ((), (), s32[]{:S(2)}) async-start(), calls=%async_computation.3 | async-start | bytes 262144
  429.6 122.1 %reduce-scatter.4.cloned.1.call-start = ((), (), s32[]{:S(2)}) async-start(), calls=%async_computation.2 | async-start | bytes 1310720
Sparse Core Ops, SparseCore 0:
  429.8 96.2 all-reduce.3
  528.8 22.8 reduce-scatter.3

commit v2 on v1

--- a/solution.py
+++ b/solution.py
@@ -16,14 +16,16 @@
 
 def codes_for(keep_block, count_block, score_block, lengths, block_index):
     requests, block_rows = keep_block.shape
-    row_index = jnp.arange(requests, dtype=jnp.int32)[:, None]
-    places = jnp.broadcast_to(
-        jnp.arange(block_rows, dtype=jnp.int32)[None, :], (requests, block_rows)
-    )
-    rank_in_list = (
-        jnp.zeros((requests, block_rows), jnp.int32).at[row_index, keep_block].set(places)
-    )
-    kept_rows = rank_in_list < count_block[:, None]
+    low = 32
+    high = block_rows // low
+    places = jnp.arange(block_rows, dtype=jnp.int32)[None, :]
+    counted = (places < count_block[:, None]).astype(jnp.bfloat16)
+    upper = (keep_block // low)[..., None] == jnp.arange(high, dtype=jnp.int32)
+    lower = (keep_block % low)[..., None] == jnp.arange(low, dtype=jnp.int32)
+    upper = upper.astype(jnp.bfloat16) * counted[..., None]
+    lower = lower.astype(jnp.bfloat16)
+    kept = jnp.einsum("rpa,rpb->rab", upper, lower, preferred_element_type=jnp.float32)
+    kept_rows = kept.reshape(requests, block_rows) > 0.5
     position = block_index * block_rows + jnp.arange(block_rows, dtype=jnp.int32)
     valid_rows = position[None, :] < lengths[:, None]
     return jnp.where(valid_rows & kept_rows, -1.0, jnp.where(valid_rows, score_block, 0.0))
@@ -81,12 +83,12 @@
     requests = offsets.shape[0]
     one_hot = (offsets[:, None] == jnp.arange(devices, dtype=jnp.int32)[None, :]).astype(jnp.int32)
     position = jnp.sum(jnp.cumsum(one_hot, axis=0) * one_hot, axis=1) - 1
-    table = (
-        jnp.zeros((devices, capacity), jnp.int32)
-        .at[offsets, position]
-        .set(jnp.arange(requests, dtype=jnp.int32), mode="drop")
+    match = (offsets[:, None, None] == jnp.arange(devices, dtype=jnp.int32)[None, :, None]) & (
+        position[:, None, None] == jnp.arange(capacity, dtype=jnp.int32)[None, None, :]
     )
-    filled = jnp.zeros((devices, capacity), jnp.bool_).at[offsets, position].set(True, mode="drop")
+    index = jnp.arange(requests, dtype=jnp.int32)[:, None, None]
+    table = jnp.sum(jnp.where(match, index, 0), axis=0)
+    filled = jnp.any(match, axis=0)
     return (table, filled, position)
 
 
@@ -135,17 +137,26 @@
     received = lax.all_to_all(outgoing, "kv", split_axis=0, concat_axis=0, tiled=True)
     held_codes = unpack_slots(received, codes, offsets, position, device, devices, capacity, -1)
     queries_h = queries.reshape(requests, -1, head_dim)
+    heads = queries_h.shape[1]
     peaks, mass, weighted = block_partial(kv_cache, held_codes, queries_h)
-    largest = lax.pmax(peaks, "kv")
-    scale = jnp.exp(peaks - largest)
-    mass = mass * scale
-    weighted = weighted * scale[..., None]
-    mass_own = lax.psum_scatter(mass, "kv", scatter_dimension=0, tiled=True)
-    weighted_own = lax.psum_scatter(weighted, "kv", scatter_dimension=0, tiled=True)
-    attended = weighted_own / mass_own[..., None]
-    attended = attended.astype(jnp.bfloat16).reshape(per_device, -1)
+    stats = jnp.concatenate([peaks, mass], axis=1)
+    stats = jnp.pad(stats, ((0, 0), (0, head_dim - 2 * heads)))
+    payload = jnp.concatenate([weighted, stats[:, None, :]], axis=1)
+    gathered = lax.all_to_all(payload, "kv", split_axis=0, concat_axis=0, tiled=True)
+    gathered = gathered.reshape(devices, per_device, heads + 1, head_dim)
+    sums = gathered[:, :, :heads, :]
+    peaks_all = gathered[:, :, heads, :heads]
+    mass_all = gathered[:, :, heads, heads : 2 * heads]
+    largest = jnp.max(peaks_all, axis=0)
+    factors = jnp.exp(peaks_all - largest[None])
+    upper = jnp.sum(factors[..., None] * sums, axis=0)
+    lower = jnp.sum(factors * mass_all, axis=0)
+    attended = (upper / lower[..., None]).astype(jnp.bfloat16).reshape(per_device, -1)
     partial_out = jnp.dot(attended, out_weight, preferred_element_type=jnp.float32)
-    return lax.psum_scatter(partial_out, "hd", scatter_dimension=1, tiled=True).astype(jnp.bfloat16)
+    groups = lax.axis_size("hd")
+    pieces = partial_out.reshape(per_device, groups, -1).transpose(1, 0, 2)
+    pieces = lax.all_to_all(pieces, "hd", split_axis=0, concat_axis=0, tiled=True)
+    return jnp.sum(pieces, axis=0).astype(jnp.bfloat16)
 
 
 def solution(mesh):

time: 561 us -> 69.2 us (0.12)
  blocking collectives: 249 us -> 9.46 us
  local copies, waits for them, and re-layouts: 134 us -> 7.55 us
  waiting for transfers between devices: 123 us -> 12.4 us
  between operations: 14.3 us -> 0.26 us
    pmax x1 -> x0, blocking collectives: 125 us -> none  [body(): largest = lax.pmax(peaks, 'kv')]
    unnamed x1 -> x0, blocking collectives: 124 us -> none
    unnamed x9 -> x8, local copies, waits for them, and re-layouts: 123 us -> 0.03 us
    unnamed x4 -> x0, waiting for transfers between devices: 119 us -> none
    all_to_all x0 -> x1, blocking collectives: none -> 9.46 us  [body(): lax.all_to_all(pieces, 'hd', split_axis=0, concat_axis=0, tiled=True)]
    scatter x5 -> x0, local copies, waits for them, and re-layouts: 7.28 us -> none  [the longest x2 3.68 us: route_tables(): jnp.zeros((devices, capacity), jnp.bool_).at[offsets, position]]
    all_to_all x0 -> x1, waiting for transfers between devices: none -> 6.06 us  [body(): lax.all_to_all(payload, 'kv', split_axis=0, concat_axis=0, tiled=True)]
  transfers between devices with their start and end apart: 3 -> 2, of which waited for: 3 -> 2; matrix products, arithmetic and copies ran while one was open for 1% -> 6% of each run, Pallas kernels for 0% -> 0%
where the time goes in v2:
time: 69.2 us; the launch traced here: 68.7 us
  matrix products  17.2 us (25%)
  waiting for transfers between devices  12.4 us (18%)
  starting transfers between devices  12.3 us (18%)
  other arithmetic  9.57 us (14%)
  blocking collectives  9.46 us (14%)
  local copies, waits for them, and re-layouts  7.55 us (11%)
    all_to_all x1, blocking collectives, body(): lax.all_to_all(pieces, 'hd', split_axis=0, concat_axis=0, tiled=True)  9.46 us
    all_to_all x1, starting transfers between devices, body(): lax.all_to_all(outgoing, 'kv', split_axis=0, concat_axis=0, tiled=True)  8.42 us
    dot_general x1, matrix products, block_partial(): jnp.einsum('rb,rbc->rc', shares, block_data, preferred_element_type=jnp.f...  8.19 us
    all_to_all x1, waiting for transfers between devices, body(): lax.all_to_all(outgoing, 'kv', split_axis=0, concat_axis=0, tiled=True)  6.32 us
    all_to_all x1, waiting for transfers between devices, body(): lax.all_to_all(payload, 'kv', split_axis=0, concat_axis=0, tiled=True)  6.06 us
    dot_general x1, matrix products, block_partial(): jnp.einsum('rhc,rbc->rhb', queries_h, block_data[..., :head_dim], preferr...  5.89 us
    all_to_all x1, starting transfers between devices, body(): lax.all_to_all(payload, 'kv', split_axis=0, concat_axis=0, tiled=True)  3.87 us
    dot_general x1, local copies, waits for them, and re-layouts, body(): jnp.dot(attended, out_weight, preferred_element_type=jnp.float32)  2.87 us
  transfers between devices with their start and end apart: 2, of which 2 were waited for; matrix products, arithmetic and copies ran while one was open for 6% of the time, Pallas kernels for 0%

profile of v2, /device:TPU:0, one launch (start us, length us, event | category | flops | bytes accessed | tf_op | source)
XLA Modules:
  0.0 68.7 jit_solution(7120563482130544100)
XLA Ops:
  0.0 0.7 %iota_compare_fusion.7 = (pred[64,32]{1,0:T(8,128)(4,1)S(1)}, s32[64,32]{1,0:T(8,128)S(1)}) fusion(s32[64]{0:T(128)} %param.13), kind=kLoop, calls=%fused_computation.62 | loop fusion | flops 4096 | bytes 10496 | tf_op jit(solution)/shard_map/eq | solution.py:86
  0.8 0.1 copy.37
  0.9 0.1 reduce_window_sum.11
  0.9 0.8 %select_reduce_fusion = s32[64]{0:T(128)S(1)} fusion(s32[64,32]{1,0:T(8,128)S(1)} %reduce_window_sum.11, s32[64]{0:T(128)} %param.13), kind=kLoop, calls=%fused_computation.61 | loop fusion | flops 6080 | bytes 8704 | tf_op jit(solution)/shard_map/reduce_sum | solution.py:85
  1.8 0.7 compare_select_fusion.2
  2.5 0.1 and_reduce_fusion
  2.6 0.1 fusion.35
  2.7 0.1 copy.38
  2.9 0.1 copy.41
  2.9 0.6 gather_fusion
  3.5 0.6 gather_fusion.1
  4.1 0.1 copy.42
  4.2 0.1 copy.43
  4.3 0.1 reshape.238
  4.4 0.7 %fusion.32 = bf16[64,512]{1,0:T(8,128)(2,1)S(1)} fusion(s32[64]{0:T(128)} %bitcast.46), kind=kLoop, calls=%fused_computation.44 | loop fusion | flops 65536 | bytes 65792 | tf_op jit(solution)/shard_map/convert_element_type | solution.py:22
  5.1 1.0 %add_select_fusion.1 = (s32[64,512]{1,0:T(8,128)S(1)}, s32[64,512]{1,0:T(8,128)S(1)}) fusion(s32[64,512]{1,0:T(8,128)} %param.9), kind=kLoop, calls=%fused_computation.29 | loop fusion | flops 622592 | bytes 393216 | tf_op jit(solution)/shard_map/jit(floor_divide)/jit(_where)/select_n | solution.py:23
  6.2 0.9 %fusion.7 = pred[64,16,32]{2,1,0:T(8,128)(4,1)S(1)} fusion(s32[64,512]{1,0:T(8,128)S(1)} %get-tuple-element.12, s32[64,512]{1,0:T(8,128)S(1)} %get-tuple-element.11, bf16[64,512]{1,0:T(8,128)(2,1)S(1)} %fusion.32), kind=kOutput, calls=%fused_computation.13 | convolution fusion | flops 35684352 | bytes 360448 | tf_op jit(solution)/shard_map/rpa,rpb->rab/dot_general | solution.py:27
  7.1 0.3 copy.39
  7.4 0.1 copy.40
  7.6 1.0 %fusion.27 = f32[64,512]{1,0:T(8,128)S(1)} fusion(f32[64,512]{1,0:T(8,128)} %param.11, pred[64,512]{1,0:T(8,128)(4,1)S(1)} %copy.40, s32[512]{0:T(512)S(1)} %iota_add_fusion, s32[64]{0:T(128)} %param.12), kind=kLoop, calls=%fused_computation.35 | loop fusion | flops 131072 | bytes 297216 | tf_op jit(solution)/shard_map/jit(_where)/select_n | solution.py:31
  8.6 0.7 gather_fusion.2
  9.4 0.8 %broadcast_select_fusion = f32[32,2,512]{2,1,0:T(2,128)} fusion(f32[32,2,512]{2,1,0:T(2,128)S(1)} %reshape.237, pred[32,2]{1,0:T(8,128)(4,1)S(1)} %broadcast_and_fusion), kind=kLoop, calls=%fused_computation.45 | loop fusion | flops 32768 | bytes 262208 | tf_op jit(solution)/shard_map/jit(_where)/select_n | solution.py:102
  10.1 8.4 %all-to-all-start = ((f32[32,2,512]{2,1,0:T(2,128)}), f32[32,2,512]{2,1,0:T(2,128)S(1)}, u32[]{:S(2)}, u32[]{:S(2)}) async-start(f32[32,2,512]{2,1,0:T(2,128)} %broadcast_select_fusion), calls=%async_computation | async-start | bytes 262144 | tf_op jit(solution)/shard_map/all_to_all | solution.py:137
  18.6 0.7 broadcast_compare_fusion.2
  19.2 0.9 %reshape.218 = bf16[64,4,128]{2,1,0:T(4,128)(2,1)S(1)} reshape(bf16[64,512]{1,0:T(8,128)(2,1)} %param.14) | data formatting | bytes 131072 | tf_op jit(solution)/shard_map/reshape | solution.py:139
  20.1 6.3 %all-to-all-done = f32[32,2,512]{2,1,0:T(2,128)S(1)} async-done(((f32[32,2,512]{2,1,0:T(2,128)}), f32[32,2,512]{2,1,0:T(2,128)S(1)}, u32[]{:S(2)}, u32[]{:S(2)}) %all-to-all-start) | async-done | bytes 131104 | tf_op jit(solution)/shard_map/all_to_all | solution.py:137
  26.4 0.1 reshape.217
  26.5 0.7 gather_fusion.3
  27.2 0.2 maximum_reduce_fusion
  27.4 0.1 fusion.34
  27.5 8.2 %fusion.29 = bf16[64,1,256]{2,1,0:T(2,128)(2,1)S(1)} fusion(bf16[64,512,256]{2,1,0:T(8,128)(2,1)} %param.8, bf16[64,512,1]{1,0,2:T(8,128)(2,1)S(1)} %fusion.34), kind=kOutput, calls=%fused_computation.38 | convolution fusion | flops 16777216 | bytes 16875520 | tf_op jit(solution)/shard_map/rb,rbc->rc/dot_general | solution.py:43
  35.8 0.2 fusion.36
  36.0 5.9 %fusion.52 = (f32[64,4]{1,0:T(8,128)S(1)}, f32[64,4,512]{2,1,0:T(4,128)S(1)}) fusion(bf16[64,4,128]{2,1,0:T(4,128)(2,1)S(1)} %reshape.218, bf16[64,512,256]{2,1,0:T(8,128)(2,1)} %param.8, pred[64,512]{1,0:T(8,128)(4,1)S(1)} %broadcast_compare_fusion), kind=kOutput, calls=%fused_computation.105 | convolution fusion | flops 33947392 | bytes 9012224 | tf_op jit(solution)/shard_map/rhc,rbc->rhb/dot_general | solution.py:47
  41.9 0.1 fusion.38
  42.0 0.4 fusion.21
  42.4 0.1 convert_convert_fusion
  42.5 0.1 select_maximum_fusion
  42.6 1.3 %fusion.11 = f32[64,4,128]{2,1,0:T(4,128)S(1)} fusion(bf16[64,512,256]{2,1,0:T(8,128)(2,1)S(1)} %bitcast.33, f32[64,4,512]{2,1,0:T(4,128)S(1)} %get-tuple-element.24, f32[64,4]{1,0:T(8,128)S(1)} %fusion.38, pred[64,512]{1,0:T(8,128)(4,1)S(1)} %broadcast_compare_fusion, f32[64,128]{1,0:T(8,128)S(1)} %get-tuple-element.15, f32[64,4]{1,0:T(8,128)S(1)} %get-tuple-element.13), kind=kOutput, calls=%fused_computation.15 | convolution fusion | flops 34013184 | bytes 9175040 | tf_op jit(solution)/shard_map/rhb,rbc->rhc/dot_general | solution.py:68
  43.9 0.8 %pad_maximum_fusion = f32[64,5,128]{2,1,0:T(8,128)} fusion(f32[64,1,128]{2,1,0:T(1,128)S(1)} %bitcast.45, f32[64,4,128]{2,1,0:T(4,128)S(1)} %fusion.11), kind=kLoop, calls=%fused_computation.24 | loop fusion | flops 40960 | bytes 327680 | tf_op jit(solution)/shard_map/concatenate | solution.py:144
  44.7 3.9 %all-to-all-start.1 = ((f32[64,5,128]{2,1,0:T(8,128)}), f32[64,5,128]{2,1,0:T(8,128)S(1)}, u32[]{:S(2)}, u32[]{:S(2)}) async-start(f32[64,5,128]{2,1,0:T(8,128)} %pad_maximum_fusion), calls=%async_computation.1 | async-start | bytes 524288 | tf_op jit(solution)/shard_map/all_to_all | solution.py:145
  48.6 2.9 %copy.50 = bf16[2048,512]{1,0:T(8,128)(2,1)S(1)} copy(bf16[2048,512]{0,1:T(8,128)(2,1)} %bitcast.35) | data formatting | bytes 4194304 | tf_op jit(solution)/shard_map/dot_general | solution.py:155
  51.5 6.1 %all-to-all-done.1 = f32[64,5,128]{2,1,0:T(8,128)S(1)} async-done(((f32[64,5,128]{2,1,0:T(8,128)}), f32[64,5,128]{2,1,0:T(8,128)S(1)}, u32[]{:S(2)}, u32[]{:S(2)}) %all-to-all-start.1) | async-done | bytes 163872 | tf_op jit(solution)/shard_map/all_to_all | solution.py:145
  57.5 0.1 fusion.51
  57.8 0.1 fusion.28
  57.9 0.1 divide_convert_fusion.1
  58.0 0.6 convolution_bitcast_fusion
  58.6 9.5 %all_to_all.15 = f32[4,2,512]{2,1,0:T(2,128)S(1)} all-to-all(f32[4,2,512]{2,1,0:T(2,128)S(1)} %convolution_bitcast_fusion), channel_id=1, replica_groups=mesh['kv'=32,'hd'=4] {'hd'}, dimensions={0} | all-to-all | bytes 32768 | tf_op jit(solution)/shard_map/all_to_all | solution.py:158
  68.1 0.6 reduce_sum.69
  (27 shorter events, 0.4 us)
Async XLA Ops:
  10.1 16.3 %all-to-all-start = ((f32[32,2,512]{2,1,0:T(2,128)}), f32[32,2,512]{2,1,0:T(2,128)S(1)}, u32[]{:S(2)}, u32[]{:S(2)}) async-start(f32[32,2,512]{2,1,0:T(2,128)} %broadcast_select_fusion), calls=%async_computation | async-start | bytes 262144 | tf_op jit(solution)/shard_map/all_to_all | solution.py:137
  27.5 15.1 %slice-start = ((s8[16777216]{0:T(1024)(128)(4,1)}), s8[4194304]{0:T(1024)(128)(4,1)S(1)}, s32[]{:S(2)}) async-start(s8[16777216]{0:T(1024)(128)(4,1)} %bitcast.32), calls=%async_computation.3 | async-start | bytes 8388608
  27.5 15.1 %slice-start.1 = ((s8[16777216]{0:T(1024)(128)(4,1)}), s8[4194304]{0:T(1024)(128)(4,1)S(1)}, s32[]{:S(2)}) async-start(s8[16777216]{0:T(1024)(128)(4,1)} %bitcast.32), calls=%async_computation.4 | async-start | bytes 8388608
  27.5 15.1 %slice-start.2 = ((s8[16777216]{0:T(1024)(128)(4,1)}), s8[4194304]{0:T(1024)(128)(4,1)S(1)}, s32[]{:S(2)}) async-start(s8[16777216]{0:T(1024)(128)(4,1)} %bitcast.32), calls=%async_computation.5 | async-start | bytes 8388608
  36.0 6.6 %slice-start.3 = ((s8[16777216]{0:T(1024)(128)(4,1)}), s8[4194304]{0:T(1024)(128)(4,1)S(1)}, s32[]{:S(2)}) async-start(s8[16777216]{0:T(1024)(128)(4,1)} %bitcast.32), calls=%async_computation.6 | async-start | bytes 8388608
  44.7 12.8 %all-to-all-start.1 = ((f32[64,5,128]{2,1,0:T(8,128)}), f32[64,5,128]{2,1,0:T(8,128)S(1)}, u32[]{:S(2)}, u32[]{:S(2)}) async-start(f32[64,5,128]{2,1,0:T(8,128)} %pad_maximum_fusion), calls=%async_computation.1 | async-start | bytes 524288 | tf_op jit(solution)/shard_map/all_to_all | solution.py:145

commit v3 on v2

--- a/solution.py
+++ b/solution.py
@@ -19,10 +19,10 @@
     low = 32
     high = block_rows // low
     places = jnp.arange(block_rows, dtype=jnp.int32)[None, :]
-    counted = (places < count_block[:, None]).astype(jnp.bfloat16)
-    upper = (keep_block // low)[..., None] == jnp.arange(high, dtype=jnp.int32)
-    lower = (keep_block % low)[..., None] == jnp.arange(low, dtype=jnp.int32)
-    upper = upper.astype(jnp.bfloat16) * counted[..., None]
+    counted = places < count_block[:, None]
+    upper = (keep_block >> 5)[..., None] == jnp.arange(high, dtype=jnp.int32)
+    lower = (keep_block & (low - 1))[..., None] == jnp.arange(low, dtype=jnp.int32)
+    upper = (upper & counted[..., None]).astype(jnp.bfloat16)
     lower = lower.astype(jnp.bfloat16)
     kept = jnp.einsum("rpa,rpb->rab", upper, lower, preferred_element_type=jnp.float32)
     kept_rows = kept.reshape(requests, block_rows) > 0.5
@@ -31,7 +31,19 @@
     return jnp.where(valid_rows & kept_rows, -1.0, jnp.where(valid_rows, score_block, 0.0))
 
 
-def block_partial(block_data, codes, queries_h):
+def raw_scores(block_data, queries_h):
+    head_dim = queries_h.shape[-1]
+    factor = 1.0 / math.sqrt(head_dim)
+    scores_qk = jnp.einsum(
+        "rhc,rbc->rhb",
+        queries_h,
+        block_data[..., :head_dim],
+        preferred_element_type=jnp.float32,
+    )
+    return lax.optimization_barrier(scores_qk * factor)
+
+
+def block_partial(block_data, codes, queries_h, scores_qk):
     head_dim = queries_h.shape[-1]
     factor = 1.0 / math.sqrt(head_dim)
     kept_rows = codes < 0.0
@@ -43,15 +55,6 @@
     merged = jnp.einsum(
         "rb,rbc->rc", shares, block_data, preferred_element_type=jnp.float32
     ).astype(jnp.bfloat16)
-    scores_qk = (
-        jnp.einsum(
-            "rhc,rbc->rhb",
-            queries_h,
-            block_data[..., :head_dim],
-            preferred_element_type=jnp.float32,
-        )
-        * factor
-    )
     merged_score = (
         jnp.einsum(
             "rhc,rc->rh", queries_h, merged[:, :head_dim], preferred_element_type=jnp.float32
@@ -81,33 +84,33 @@
 
 def route_tables(offsets, devices, capacity):
     requests = offsets.shape[0]
-    one_hot = (offsets[:, None] == jnp.arange(devices, dtype=jnp.int32)[None, :]).astype(jnp.int32)
-    position = jnp.sum(jnp.cumsum(one_hot, axis=0) * one_hot, axis=1) - 1
-    match = (offsets[:, None, None] == jnp.arange(devices, dtype=jnp.int32)[None, :, None]) & (
-        position[:, None, None] == jnp.arange(capacity, dtype=jnp.int32)[None, None, :]
-    )
-    index = jnp.arange(requests, dtype=jnp.int32)[:, None, None]
-    table = jnp.sum(jnp.where(match, index, 0), axis=0)
-    filled = jnp.any(match, axis=0)
-    return (table, filled, position)
+    index = jnp.arange(requests, dtype=jnp.int32)
+    same = offsets[:, None] == offsets[None, :]
+    position = jnp.sum((same & (index[None, :] < index[:, None])).astype(jnp.int32), axis=1)
+    return position
 
 
-def pack_slots(values, table, filled, device, devices, direction):
-    targets = jnp.arange(devices, dtype=jnp.int32)
-    amount = direction * (device - targets) % devices
-    chosen = table[amount]
-    live_slots = filled[amount] & (amount != 0)[:, None]
+def pack_slots(values, offsets, position, device, devices, capacity):
+    requests = offsets.shape[0]
+    index = jnp.arange(requests, dtype=jnp.int32)
+    amount = (jnp.arange(devices, dtype=jnp.int32) - device) % devices
+    match = (
+        (offsets[None, None, :] == amount[:, None, None])
+        & (position[None, None, :] == jnp.arange(capacity, dtype=jnp.int32)[None, :, None])
+        & (amount != 0)[:, None, None]
+    )
+    chosen = jnp.sum(jnp.where(match, index, 0), axis=2)
+    live = jnp.any(match, axis=2)
     gathered = values[chosen]
-    live_slots = live_slots.reshape(live_slots.shape + (1,) * (values.ndim - 1))
-    return jnp.where(live_slots, gathered, jnp.zeros((), values.dtype))
+    return jnp.where(live[..., None], gathered, jnp.zeros((), values.dtype))
 
 
-def unpack_slots(received, values, offsets, position, device, devices, capacity, direction):
-    source = (device + direction * offsets) % devices
+def unpack_slots(received, values, offsets, position, device, devices, capacity):
+    source = (device - offsets) % devices
     slots = source * capacity + jnp.minimum(position, capacity - 1)
     stacked = received.reshape((devices * capacity,) + received.shape[2:])
     taken = stacked[slots]
-    moving = (offsets != 0).reshape((-1,) + (1,) * (values.ndim - 1))
+    moving = (offsets != 0)[:, None]
     return jnp.where(moving, taken, values)
 
 
@@ -132,13 +135,14 @@
     capacity = (requests // 2 + devices - 2) // (devices - 1)
     per_device = requests // devices
     codes = codes_for(keep_lists, kept_counts[:, 0], drop_scores, lengths, device)
-    table, filled, position = route_tables(offsets, devices, capacity)
-    outgoing = pack_slots(codes, table, filled, device, devices, -1)
+    position = route_tables(offsets, devices, capacity)
+    outgoing = pack_slots(codes, offsets, position, device, devices, capacity)
     received = lax.all_to_all(outgoing, "kv", split_axis=0, concat_axis=0, tiled=True)
-    held_codes = unpack_slots(received, codes, offsets, position, device, devices, capacity, -1)
+    held_codes = unpack_slots(received, codes, offsets, position, device, devices, capacity)
     queries_h = queries.reshape(requests, -1, head_dim)
     heads = queries_h.shape[1]
-    peaks, mass, weighted = block_partial(kv_cache, held_codes, queries_h)
+    scores_qk = raw_scores(kv_cache, queries_h)
+    peaks, mass, weighted = block_partial(kv_cache, held_codes, queries_h, scores_qk)
     stats = jnp.concatenate([peaks, mass], axis=1)
     stats = jnp.pad(stats, ((0, 0), (0, head_dim - 2 * heads)))
     payload = jnp.concatenate([weighted, stats[:, None, :]], axis=1)

time: 69.2 us -> 67.9 us (0.981)
  waiting for transfers between devices: 12.4 us -> 6.7 us
  matrix products: 17.2 us -> 20.4 us
  starting transfers between devices: 12.3 us -> 15.2 us
  local copies, waits for them, and re-layouts: 7.55 us -> 6.1 us
    all_to_all x1, waiting for transfers between devices: 6.32 us -> 0.64 us  [body(): lax.all_to_all(outgoing, 'kv', split_axis=0, concat_axis=0, tiled=True)]
    dot_general x1, matrix products: 1.32 us -> 4.74 us  [block_partial(): jnp.einsum('rhb,rbc->rhc', probs.astype(jnp.bfloat16), block_data[..., he...]
    all_to_all x1, starting transfers between devices: 3.87 us -> 6.76 us  [body(): lax.all_to_all(payload, 'kv', split_axis=0, concat_axis=0, tiled=True)]
    gather x3 -> x0, local copies, waits for them, and re-layouts: 1.24 us -> none  [the longest x2 0.65 us: pack_slots(): chosen = table[amount]]
    select_n x3 -> x2, other arithmetic: 1.8 us -> 0.77 us  [the longest x1 0.76 us: pack_slots(): return jnp.where(live[..., None], gathered, jnp.zeros((), values.dtype))]
    shift_right_arithmetic x0 -> x1, other arithmetic: none -> 0.93 us  [codes_for(): upper = (keep_block >> 5)[..., None] == jnp.arange(high, dtype=jnp.int32)]
    lt x0 -> x1, other arithmetic: none -> 0.74 us  [codes_for(): counted = places < count_block[:, None]]
    convert_element_type x1 -> x0, other arithmetic: 0.73 us -> none  [codes_for(): counted = (places < count_block[:, None]).astype(jnp.bfloat16)]
  transfers between devices with their start and end apart: 2 -> 2, of which waited for: 2 -> 2; matrix products, arithmetic and copies ran while one was open for 6% -> 15% of each run, Pallas kernels for 0% -> 0%
where the time goes in v3:
time: 67.9 us; the launch traced here: 67.3 us
  matrix products  20.4 us (30%)
  starting transfers between devices  15.2 us (22%)
  blocking collectives  9.46 us (14%)
  other arithmetic  9.23 us (14%)
  waiting for transfers between devices  6.7 us (10%)
  local copies, waits for them, and re-layouts  6.1 us (9%)
    all_to_all x1, blocking collectives, body(): lax.all_to_all(pieces, 'hd', split_axis=0, concat_axis=0, tiled=True)  9.46 us
    all_to_all x1, starting transfers between devices, body(): lax.all_to_all(outgoing, 'kv', split_axis=0, concat_axis=0, tiled=True)  8.42 us
    dot_general x1, matrix products, block_partial(): jnp.einsum('rb,rbc->rc', shares, block_data, preferred_element_type=jnp.f...  8.04 us
    all_to_all x1, starting transfers between devices, body(): lax.all_to_all(payload, 'kv', split_axis=0, concat_axis=0, tiled=True)  6.76 us
    all_to_all x1, waiting for transfers between devices, body(): lax.all_to_all(payload, 'kv', split_axis=0, concat_axis=0, tiled=True)  6.06 us
    dot_general x1, matrix products, raw_scores(): jnp.einsum('rhc,rbc->rhb', queries_h, block_data[..., :head_dim], preferr...  5.65 us
    dot_general x1, matrix products, block_partial(): jnp.einsum('rhb,rbc->rhc', probs.astype(jnp.bfloat16), block_data[..., he...  4.74 us
    dot_general x1, local copies, waits for them, and re-layouts, body(): jnp.dot(attended, out_weight, preferred_element_type=jnp.float32)  2.87 us
  transfers between devices with their start and end apart: 2, of which 2 were waited for; matrix products, arithmetic and copies ran while one was open for 15% of the time, Pallas kernels for 0%

profile of v3, /device:TPU:0, one launch (start us, length us, event | category | flops | bytes accessed | tf_op | source)
XLA Modules:
  0.0 67.3 jit_solution(16311394874316190965)
XLA Ops:
  0.0 0.0 copy-start
  0.0 0.9 %convert_reduce_fusion = s32[64]{0:T(128)S(1)} fusion(s32[64]{0:T(128)} %param.13), kind=kLoop, calls=%fused_computation.50 | loop fusion | flops 20416 | bytes 512 | tf_op jit(solution)/shard_map/reduce_sum | solution.py:89
  1.0 0.7 %broadcast_compare_fusion.1 = pred[32,64]{1,0:T(8,128)(4,1)S(1)} fusion(s32[64]{0:T(128)} %param.13, s32[32]{0:T(128)S(1)} %and_select_fusion.1), kind=kLoop, calls=%fused_computation.61 | loop fusion | flops 2048 | bytes 2432 | tf_op jit(solution)/shard_map/eq | solution.py:98
  1.7 0.2 fusion.32
  1.9 0.2 select_reduce_fusion.1
  2.1 0.1 copy.33
  2.2 0.1 copy.36
  2.3 0.1 reshape.171
  2.4 0.7 %iota_compare_fusion.5 = pred[64,512]{1,0:T(8,128)(4,1)S(1)} fusion(s32[64]{0:T(128)} %bitcast.42), kind=kLoop, calls=%fused_computation.34 | loop fusion | flops 32768 | bytes 33024 | tf_op jit(solution)/shard_map/lt | solution.py:22
  3.1 0.9 %broadcast_shift-right-arithmetic_fusion = (s32[64,512]{1,0:T(8,128)S(1)}, s32[64,512]{1,0:T(8,128)S(1)}) fusion(s32[64,512]{1,0:T(8,128)} %param.9), kind=kLoop, calls=%fused_computation.40 | loop fusion | flops 65536 | bytes 393216 | tf_op jit(solution)/shard_map/shift_right_arithmetic | solution.py:23
  4.1 1.2 %fusion.8 = pred[64,16,32]{2,1,0:T(8,128)(4,1)S(1)} fusion(s32[64,512]{1,0:T(8,128)S(1)} %get-tuple-element.12, s32[64,512]{1,0:T(8,128)S(1)} %get-tuple-element.11, pred[64,512]{1,0:T(8,128)(4,1)S(1)} %iota_compare_fusion.5), kind=kOutput, calls=%fused_computation.11 | convolution fusion | flops 35684352 | bytes 327680 | tf_op jit(solution)/shard_map/rpa,rpb->rab/dot_general | solution.py:27
  5.2 0.3 copy.34
  5.6 0.1 copy.35
  5.7 1.0 %fusion.26 = f32[64,512]{1,0:T(8,128)S(1)} fusion(f32[64,512]{1,0:T(8,128)} %param.11, pred[64,512]{1,0:T(8,128)(4,1)S(1)} %copy.35, s32[512]{0:T(512)S(1)} %iota_add_fusion, s32[64]{0:T(128)} %param.12), kind=kLoop, calls=%fused_computation.28 | loop fusion | flops 131072 | bytes 297216 | tf_op jit(solution)/shard_map/jit(_where)/select_n | solution.py:31
  6.7 0.7 gather_fusion
  7.4 0.1 reshape.170
  7.4 0.8 %broadcast_select_fusion = f32[32,2,512]{2,1,0:T(2,128)} fusion(f32[32,2,512]{2,1,0:T(2,128)S(1)} %reshape.170, pred[32,2]{1,0:T(8,128)(4,1)S(1)} %copy.33), kind=kLoop, calls=%fused_computation.35 | loop fusion | flops 32768 | bytes 262208 | tf_op jit(solution)/shard_map/jit(_where)/select_n | solution.py:105
  8.2 8.4 %all-to-all-start = ((f32[32,2,512]{2,1,0:T(2,128)}), f32[32,2,512]{2,1,0:T(2,128)S(1)}, u32[]{:S(2)}, u32[]{:S(2)}) async-start(f32[32,2,512]{2,1,0:T(2,128)} %broadcast_select_fusion), calls=%async_computation | async-start | bytes 262144 | tf_op jit(solution)/shard_map/all_to_all | solution.py:140
  16.6 0.7 compare_select_fusion.2
  17.3 0.9 %reshape.167 = bf16[64,4,128]{2,1,0:T(4,128)(2,1)S(1)} reshape(bf16[64,512]{1,0:T(8,128)(2,1)} %param.14) | data formatting | bytes 131072 | tf_op jit(solution)/shard_map/reshape | solution.py:142
  18.2 5.6 %fusion.11 = f32[64,4,512]{2,1,0:T(4,128)S(1)} fusion(bf16[64,4,128]{2,1,0:T(4,128)(2,1)S(1)} %reshape.167, bf16[64,512,256]{2,1,0:T(8,128)(2,1)} %param.8), kind=kOutput, calls=%fused_computation.12 | convolution fusion | flops 33685504 | bytes 8978432 | tf_op jit(solution)/shard_map/rhc,rbc->rhb/dot_general | solution.py:37
  23.8 0.0 copy-done
  23.9 0.6 all-to-all-done
  24.5 0.1 reshape.166
  24.6 0.7 gather_fusion.1
  25.2 0.2 maximum_reduce_fusion
  25.5 0.1 fusion.30
  25.6 8.0 %fusion.28 = bf16[64,1,256]{2,1,0:T(2,128)(2,1)S(1)} fusion(bf16[64,512,256]{2,1,0:T(8,128)(2,1)} %param.8, bf16[64,512,1]{1,0,2:T(8,128)(2,1)S(1)} %fusion.30), kind=kOutput, calls=%fused_computation.31 | convolution fusion | flops 16777216 | bytes 16875520 | tf_op jit(solution)/shard_map/rb,rbc->rc/dot_general | solution.py:55
  33.7 0.2 fusion.33
  33.9 0.3 select_reduce_fusion
  34.1 0.1 fusion.35
  34.2 0.5 fusion.19
  34.8 0.1 convert_convert_fusion
  34.9 0.1 select_maximum_fusion
  34.9 4.7 %fusion.14 = f32[64,4,128]{2,1,0:T(4,128)S(1)} fusion(bf16[64,512,256]{2,1,0:T(8,128)(2,1)} %param.8, f32[64,4,512]{2,1,0:T(4,128)S(1)} %fusion.11, f32[64,4]{1,0:T(8,128)S(1)} %fusion.35, pred[64,512]{1,0:T(8,128)(4,1)S(1)} %broadcast_compare_fusion, f32[64,128]{1,0:T(8,128)S(1)} %get-tuple-element.15, f32[64,4]{1,0:T(8,128)S(1)} %get-tuple-element.13), kind=kOutput, calls=%fused_computation.13 | convolution fusion | flops 34144256 | bytes 9111552 | tf_op jit(solution)/shard_map/rhb,rbc->rhc/dot_general | solution.py:71
  39.7 0.8 %pad_maximum_fusion = f32[64,5,128]{2,1,0:T(8,128)} fusion(f32[64,1,128]{2,1,0:T(1,128)S(1)} %bitcast.41, f32[64,4,128]{2,1,0:T(4,128)S(1)} %fusion.14), kind=kLoop, calls=%fused_computation.21 | loop fusion | flops 40960 | bytes 327680 | tf_op jit(solution)/shard_map/concatenate | solution.py:148
  40.4 6.8 %all-to-all-start.1 = ((f32[64,5,128]{2,1,0:T(8,128)}), f32[64,5,128]{2,1,0:T(8,128)S(1)}, u32[]{:S(2)}, u32[]{:S(2)}) async-start(f32[64,5,128]{2,1,0:T(8,128)} %pad_maximum_fusion), calls=%async_computation.1 | async-start | bytes 524288 | tf_op jit(solution)/shard_map/all_to_all | solution.py:149
  47.2 2.9 %copy.43 = bf16[2048,512]{1,0:T(8,128)(2,1)S(1)} copy(bf16[2048,512]{0,1:T(8,128)(2,1)} %bitcast.31) | data formatting | bytes 4194304 | tf_op jit(solution)/shard_map/dot_general | solution.py:159
  50.1 6.1 %all-to-all-done.1 = f32[64,5,128]{2,1,0:T(8,128)S(1)} async-done(((f32[64,5,128]{2,1,0:T(8,128)}), f32[64,5,128]{2,1,0:T(8,128)S(1)}, u32[]{:S(2)}, u32[]{:S(2)}) %all-to-all-start.1) | async-done | bytes 163872 | tf_op jit(solution)/shard_map/all_to_all | solution.py:149
  56.1 0.1 fusion.44
  56.3 0.1 multiply_reduce_fusion
  56.4 0.1 fusion.27
  56.5 0.1 divide_convert_fusion.1
  56.6 0.6 convolution_bitcast_fusion
  57.3 9.5 %all_to_all.15 = f32[4,2,512]{2,1,0:T(2,128)S(1)} all-to-all(f32[4,2,512]{2,1,0:T(2,128)S(1)} %convolution_bitcast_fusion), channel_id=1, replica_groups=mesh['kv'=32,'hd'=4] {'hd'}, dimensions={0} | all-to-all | bytes 32768 | tf_op jit(solution)/shard_map/all_to_all | solution.py:162
  66.7 0.6 reduce_sum.72
  (15 shorter events, 0.2 us)
Async XLA Ops:
  0.0 23.8 %copy-start = (s32[64]{0:T(128)S(1)}, s32[64]{0:T(128)}, u32[]{:S(2)}) copy-start(s32[64]{0:T(128)} %param.13) | copy-start | bytes 772
  8.2 16.3 %all-to-all-start = ((f32[32,2,512]{2,1,0:T(2,128)}), f32[32,2,512]{2,1,0:T(2,128)S(1)}, u32[]{:S(2)}, u32[]{:S(2)}) async-start(f32[32,2,512]{2,1,0:T(2,128)} %broadcast_select_fusion), calls=%async_computation | async-start | bytes 262144 | tf_op jit(solution)/shard_map/all_to_all | solution.py:140
  40.4 15.7 %all-to-all-start.1 = ((f32[64,5,128]{2,1,0:T(8,128)}), f32[64,5,128]{2,1,0:T(8,128)S(1)}, u32[]{:S(2)}, u32[]{:S(2)}) async-start(f32[64,5,128]{2,1,0:T(8,128)} %pad_maximum_fusion), calls=%async_computation.1 | async-start | bytes 524288 | tf_op jit(solution)/shard_map/all_to_all | solution.py:149

commit v4 on v3

--- a/solution.py
+++ b/solution.py
@@ -52,9 +52,16 @@
     has_merged = totals > 0.0
     floored = jnp.maximum(totals, 1.0)
     shares = (weight / floored[:, None]).astype(jnp.bfloat16)
-    merged = jnp.einsum(
-        "rb,rbc->rc", shares, block_data, preferred_element_type=jnp.float32
-    ).astype(jnp.bfloat16)
+    scores_qk = jnp.where(kept_rows[:, None, :], scores_qk, -1e30)
+    kept_peaks = jnp.max(scores_qk, axis=-1)
+    kept_probs = jnp.where(
+        kept_rows[:, None, :], jnp.exp(scores_qk - kept_peaks[..., None]), 0.0
+    )
+    kept_mass = jnp.sum(kept_probs, axis=-1)
+    rows = jnp.concatenate([shares[:, None, :], kept_probs.astype(jnp.bfloat16)], axis=1)
+    products = jnp.einsum("rkb,rbc->rkc", rows, block_data, preferred_element_type=jnp.float32)
+    merged = products[:, 0, :].astype(jnp.bfloat16)
+    kept_weighted = products[:, 1:, head_dim:]
     merged_score = (
         jnp.einsum(
             "rhc,rc->rh", queries_h, merged[:, :head_dim], preferred_element_type=jnp.float32
@@ -62,21 +69,14 @@
         * factor
     )
     merged_score = merged_score + jnp.log(floored)[:, None]
-    scores_qk = jnp.where(kept_rows[:, None, :], scores_qk, -1e30)
     merged_score = jnp.where(has_merged[:, None], merged_score, -1e30)
-    peaks = jnp.maximum(jnp.max(scores_qk, axis=-1), merged_score)
-    probs = jnp.where(kept_rows[:, None, :], jnp.exp(scores_qk - peaks[..., None]), 0.0)
+    peaks = jnp.maximum(kept_peaks, merged_score)
+    rescale = jnp.exp(kept_peaks - peaks)
     merged_prob = jnp.where(has_merged[:, None], jnp.exp(merged_score - peaks), 0.0)
-    mass = jnp.sum(probs, axis=-1) + merged_prob
-    weighted = jnp.einsum(
-        "rhb,rbc->rhc",
-        probs.astype(jnp.bfloat16),
-        block_data[..., head_dim:],
-        preferred_element_type=jnp.float32,
-    )
+    mass = kept_mass * rescale + merged_prob
     merged_value = merged[:, head_dim:].astype(jnp.float32)
     weighted = (
-        weighted
+        kept_weighted * rescale[..., None]
         + merged_prob.astype(jnp.bfloat16).astype(jnp.float32)[..., None] * merged_value[:, None, :]
     )
     return (peaks, mass, weighted)

time: 67.9 us -> 61.1 us (0.90)
  matrix products: 20.4 us -> 15.7 us
  starting transfers between devices: 15.2 us -> 13.7 us
  waiting for transfers between devices: 6.7 us -> 8.18 us
  other arithmetic: 9.23 us -> 7.92 us
    dot_general x2 -> x1, matrix products: 12.8 us -> 8.06 us  [block_partial(): jnp.einsum('rkb,rbc->rkc', rows, block_data, preferred_element_type=jnp.f...]
    all_to_all x1, waiting for transfers between devices: 0.64 us -> 2.12 us  [body(): lax.all_to_all(outgoing, 'kv', split_axis=0, concat_axis=0, tiled=True)]
    all_to_all x1, starting transfers between devices: 6.76 us -> 5.28 us  [body(): lax.all_to_all(payload, 'kv', split_axis=0, concat_axis=0, tiled=True)]
    select_n x1, other arithmetic: 1 us -> 0.1 us  [codes_for(): jnp.where(valid_rows & kept_rows, -1.0, jnp.where(valid_rows, score_block...]
    reshape x1, local copies, waits for them, and re-layouts: 0.86 us -> 0.02 us  [body(): queries_h = queries.reshape(requests, -1, head_dim)]
  transfers between devices with their start and end apart: 2 -> 2, of which waited for: 2 -> 2; matrix products, arithmetic and copies ran while one was open for 15% -> 14% of each run, Pallas kernels for 0% -> 0%
where the time goes in v4:
time: 61.1 us; the launch traced here: 60.7 us
  matrix products  15.7 us (26%)
  starting transfers between devices  13.7 us (22%)
  blocking collectives  9.46 us (15%)
  waiting for transfers between devices  8.18 us (13%)
  other arithmetic  7.92 us (13%)
  local copies, waits for them, and re-layouts  5.43 us (9%)
    all_to_all x1, blocking collectives, body(): lax.all_to_all(pieces, 'hd', split_axis=0, concat_axis=0, tiled=True)  9.46 us
    all_to_all x1, starting transfers between devices, body(): lax.all_to_all(outgoing, 'kv', split_axis=0, concat_axis=0, tiled=True)  8.41 us
    dot_general x1, matrix products, block_partial(): jnp.einsum('rkb,rbc->rkc', rows, block_data, preferred_element_type=jnp.f...  8.06 us
    all_to_all x1, waiting for transfers between devices, body(): lax.all_to_all(payload, 'kv', split_axis=0, concat_axis=0, tiled=True)  6.06 us
    dot_general x1, matrix products, raw_scores(): jnp.einsum('rhc,rbc->rhb', queries_h, block_data[..., :head_dim], preferr...  5.65 us
    all_to_all x1, starting transfers between devices, body(): lax.all_to_all(payload, 'kv', split_axis=0, concat_axis=0, tiled=True)  5.28 us
    dot_general x1, local copies, waits for them, and re-layouts, body(): jnp.dot(attended, out_weight, preferred_element_type=jnp.float32)  2.87 us
    all_to_all x1, waiting for transfers between devices, body(): lax.all_to_all(outgoing, 'kv', split_axis=0, concat_axis=0, tiled=True)  2.12 us
  transfers between devices with their start and end apart: 2, of which 2 were waited for; matrix products, arithmetic and copies ran while one was open for 14% of the time, Pallas kernels for 0%

profile of v4, /device:TPU:0, one launch (start us, length us, event | category | flops | bytes accessed | tf_op | source)
XLA Modules:
  0.0 60.7 jit_solution(1827000031276999537)
XLA Ops:
  0.0 0.9 %convert_reduce_fusion = s32[64]{0:T(128)S(1)} fusion(s32[64]{0:T(128)} %param.13), kind=kLoop, calls=%fused_computation.50 | loop fusion | flops 20416 | bytes 512 | tf_op jit(solution)/shard_map/reduce_sum | solution.py:89
  1.0 0.7 %broadcast_compare_fusion.1 = pred[32,64]{1,0:T(8,128)(4,1)S(1)} fusion(s32[64]{0:T(128)} %param.13, s32[32]{0:T(128)S(1)} %and_select_fusion.1), kind=kLoop, calls=%fused_computation.61 | loop fusion | flops 2048 | bytes 2432 | tf_op jit(solution)/shard_map/eq | solution.py:98
  1.7 0.2 fusion.25
  1.9 0.2 select_reduce_fusion.1
  2.1 0.1 copy.37
  2.2 0.1 copy.40
  2.3 0.1 reshape.173
  2.4 0.7 %iota_compare_fusion.5 = pred[64,512]{1,0:T(8,128)(4,1)S(1)} fusion(s32[64]{0:T(128)} %bitcast.42), kind=kLoop, calls=%fused_computation.31 | loop fusion | flops 32768 | bytes 33024 | tf_op jit(solution)/shard_map/lt | solution.py:22
  3.2 0.9 %broadcast_shift-right-arithmetic_fusion = (s32[64,512]{1,0:T(8,128)S(1)}, s32[64,512]{1,0:T(8,128)S(1)}) fusion(s32[64,512]{1,0:T(8,128)} %param.9), kind=kLoop, calls=%fused_computation.37 | loop fusion | flops 65536 | bytes 393216 | tf_op jit(solution)/shard_map/shift_right_arithmetic | solution.py:23
  4.1 1.2 %fusion.6 = pred[64,16,32]{2,1,0:T(8,128)(4,1)S(1)} fusion(s32[64,512]{1,0:T(8,128)S(1)} %get-tuple-element.18, s32[64,512]{1,0:T(8,128)S(1)} %get-tuple-element.17, pred[64,512]{1,0:T(8,128)(4,1)S(1)} %iota_compare_fusion.5), kind=kOutput, calls=%fused_computation.9 | convolution fusion | flops 35684352 | bytes 327680 | tf_op jit(solution)/shard_map/rpa,rpb->rab/dot_general | solution.py:27
  5.3 0.3 copy.38
  5.6 0.1 copy.39
  5.7 0.0 copy-done.3
  5.7 0.0 copy-done
  5.8 0.1 fusion.20
  5.9 0.7 %gather_fusion = f32[64,512]{1,0:T(8,128)S(1)} fusion(f32[64,512]{1,0:T(8,128)S(1)} %fusion.20, s32[1024]{0:T(1024)S(1)} %pad_clamp_fusion.1), kind=kCustom, calls=%fused_computation | custom fusion | bytes 262400 | tf_op jit(solution)/shard_map/gather | solution.py:104
  6.5 0.1 reshape.172
  6.6 0.8 %broadcast_select_fusion = f32[32,2,512]{2,1,0:T(2,128)} fusion(f32[32,2,512]{2,1,0:T(2,128)S(1)} %reshape.172, pred[32,2]{1,0:T(8,128)(4,1)S(1)} %copy.37), kind=kLoop, calls=%fused_computation.32 | loop fusion | flops 32768 | bytes 262208 | tf_op jit(solution)/shard_map/jit(_where)/select_n | solution.py:105
  7.4 8.4 %all-to-all-start = ((f32[32,2,512]{2,1,0:T(2,128)}), f32[32,2,512]{2,1,0:T(2,128)S(1)}, u32[]{:S(2)}, u32[]{:S(2)}) async-start(f32[32,2,512]{2,1,0:T(2,128)} %broadcast_select_fusion), calls=%async_computation | async-start | bytes 262144 | tf_op jit(solution)/shard_map/all_to_all | solution.py:140
  15.8 0.0 copy-done.2
  15.8 0.0 copy-done.1
  15.8 5.6 %fusion.9 = f32[64,4,512]{2,1,0:T(4,128)S(1)} fusion(bf16[64,4,128]{2,1,0:T(4,128)(2,1)S(1)} %reshape.169, bf16[64,512,256]{2,1,0:T(8,128)(2,1)} %param.8), kind=kOutput, calls=%fused_computation.10 | convolution fusion | flops 33685504 | bytes 8978432 | tf_op jit(solution)/shard_map/rhc,rbc->rhb/dot_general | solution.py:37
  21.5 2.1 %all-to-all-done = f32[32,2,512]{2,1,0:T(2,128)S(1)} async-done(((f32[32,2,512]{2,1,0:T(2,128)}), f32[32,2,512]{2,1,0:T(2,128)S(1)}, u32[]{:S(2)}, u32[]{:S(2)}) %all-to-all-start) | async-done | bytes 131104 | tf_op jit(solution)/shard_map/all_to_all | solution.py:140
  23.6 0.1 reshape.168
  23.7 0.7 %gather_fusion.1 = f32[64,512]{1,0:T(8,128)S(1)} fusion(f32[64,512]{1,0:T(8,128)S(1)} %reshape.168, s32[1024]{0:T(1024)S(1)} %pad_clamp_fusion), kind=kCustom, calls=%fused_computation.1 | custom fusion | bytes 262400 | tf_op jit(solution)/shard_map/gather | solution.py:112
  24.4 0.2 maximum_reduce_fusion
  24.6 0.1 fusion.23
  24.7 0.1 copy.41
  24.8 0.3 select_reduce_fusion
  25.1 0.6 fusion.19
  25.7 8.1 %fusion.14 = f32[64,5,256]{2,1,0:T(8,128)S(1)} fusion(bf16[64,512,256]{2,1,0:T(8,128)(2,1)} %param.8, bf16[64,4,512]{2,1,0:T(4,128)(2,1)S(1)} %get-tuple-element.13, bf16[64,1,512]{2,1,0:T(2,128)(2,1)S(1)} %copy.41), kind=kOutput, calls=%fused_computation.14 | convolution fusion | flops 84541440 | bytes 17432576 | tf_op jit(solution)/shard_map/rkb,rbc->rkc/dot_general | solution.py:62
  33.7 0.1 slice.57
  33.8 0.2 fusion.26
  34.0 0.1 convert_convert_fusion
  34.1 0.1 multiply_add_fusion
  34.2 0.1 select_maximum_fusion
  34.3 0.2 fusion.22
  34.5 0.7 %pad_maximum_fusion = f32[64,5,128]{2,1,0:T(8,128)} fusion(f32[64,1,128]{2,1,0:T(1,128)S(1)} %bitcast.41, f32[64,4,128]{2,1,0:T(4,128)S(1)} %fusion.22), kind=kLoop, calls=%fused_computation.22 | loop fusion | flops 40960 | bytes 327680 | tf_op jit(solution)/shard_map/concatenate | solution.py:148
  35.3 5.3 %all-to-all-start.1 = ((f32[64,5,128]{2,1,0:T(8,128)}), f32[64,5,128]{2,1,0:T(8,128)S(1)}, u32[]{:S(2)}, u32[]{:S(2)}) async-start(f32[64,5,128]{2,1,0:T(8,128)} %pad_maximum_fusion), calls=%async_computation.1 | async-start | bytes 524288 | tf_op jit(solution)/shard_map/all_to_all | solution.py:149
  40.6 2.9 %copy.46 = bf16[2048,512]{1,0:T(8,128)(2,1)S(1)} copy(bf16[2048,512]{0,1:T(8,128)(2,1)} %bitcast.31) | data formatting | bytes 4194304 | tf_op jit(solution)/shard_map/dot_general | solution.py:159
  43.4 6.1 %all-to-all-done.1 = f32[64,5,128]{2,1,0:T(8,128)S(1)} async-done(((f32[64,5,128]{2,1,0:T(8,128)}), f32[64,5,128]{2,1,0:T(8,128)S(1)}, u32[]{:S(2)}, u32[]{:S(2)}) %all-to-all-start.1) | async-done | bytes 163872 | tf_op jit(solution)/shard_map/all_to_all | solution.py:149
  49.5 0.1 fusion.36
  49.7 0.1 multiply_reduce_fusion
  49.7 0.1 fusion.21
  49.9 0.1 divide_convert_fusion.1
  50.0 0.6 %convolution_bitcast_fusion = f32[4,2,512]{2,1,0:T(2,128)S(1)} fusion(bf16[2,512,1]{1,0,2:T(2,128)(2,1)S(1)} %reshape.191, bf16[4,512,512]{2,1,0:T(8,128)(2,1)S(1)} %bitcast.30), kind=kOutput, calls=%fused_computation.11 | convolution fusion | flops 4194304 | bytes 2115584 | tf_op jit(solution)/shard_map/dot_general | solution.py:159
  50.6 9.5 %all_to_all.15 = f32[4,2,512]{2,1,0:T(2,128)S(1)} all-to-all(f32[4,2,512]{2,1,0:T(2,128)S(1)} %convolution_bitcast_fusion), channel_id=1, replica_groups=mesh['kv'=32,'hd'=4] {'hd'}, dimensions={0} | all-to-all | bytes 32768 | tf_op jit(solution)/shard_map/all_to_all | solution.py:162
  60.1 0.6 reduce_sum.72
  (21 shorter events, 0.2 us)
Async XLA Ops:
  0.0 15.8 %copy-start.2 = (s32[64]{0:T(128)S(1)}, s32[64]{0:T(128)}, u32[]{:S(2)}) copy-start(s32[64]{0:T(128)} %param.13) | copy-start | bytes 772
  0.0 5.7 %copy-start.3 = (s32[64]{0:T(128)S(1)}, s32[64]{0:T(128)}, u32[]{:S(2)}) copy-start(s32[64]{0:T(128)} %param.12) | copy-start | bytes 772
  0.0 5.7 %copy-start = (f32[64,512]{1,0:T(8,128)S(1)}, f32[64,512]{1,0:T(8,128)}, u32[]{:S(2)}) copy-start(f32[64,512]{1,0:T(8,128)} %param.11) | copy-start | bytes 393220
  0.0 15.8 %copy-start.1 = (bf16[64,512]{1,0:T(8,128)(2,1)S(1)}, bf16[64,512]{1,0:T(8,128)(2,1)}, u32[]{:S(2)}) copy-start(bf16[64,512]{1,0:T(8,128)(2,1)} %param.14) | copy-start | bytes 196612
  7.4 16.3 %all-to-all-start = ((f32[32,2,512]{2,1,0:T(2,128)}), f32[32,2,512]{2,1,0:T(2,128)S(1)}, u32[]{:S(2)}, u32[]{:S(2)}) async-start(f32[32,2,512]{2,1,0:T(2,128)} %broadcast_select_fusion), calls=%async_computation | async-start | bytes 262144 | tf_op jit(solution)/shard_map/all_to_all | solution.py:140
  35.3 14.2 %all-to-all-start.1 = ((f32[64,5,128]{2,1,0:T(8,128)}), f32[64,5,128]{2,1,0:T(8,128)S(1)}, u32[]{:S(2)}, u32[]{:S(2)}) async-start(f32[64,5,128]{2,1,0:T(8,128)} %pad_maximum_fusion), calls=%async_computation.1 | async-start | bytes 524288 | tf_op jit(solution)/shard_map/all_to_all | solution.py:149

commit v5 on v4

--- a/solution.py
+++ b/solution.py
@@ -90,19 +90,17 @@
     return position
 
 
-def pack_slots(values, offsets, position, device, devices, capacity):
+def pack_slots(values, offsets, device, devices):
     requests = offsets.shape[0]
     index = jnp.arange(requests, dtype=jnp.int32)
     amount = (jnp.arange(devices, dtype=jnp.int32) - device) % devices
-    match = (
-        (offsets[None, None, :] == amount[:, None, None])
-        & (position[None, None, :] == jnp.arange(capacity, dtype=jnp.int32)[None, :, None])
-        & (amount != 0)[:, None, None]
-    )
-    chosen = jnp.sum(jnp.where(match, index, 0), axis=2)
-    live = jnp.any(match, axis=2)
-    gathered = values[chosen]
-    return jnp.where(live[..., None], gathered, jnp.zeros((), values.dtype))
+    match = (offsets[None, :] == amount[:, None]) & (amount != 0)[:, None]
+    first = jnp.min(jnp.where(match, index, requests), axis=1)
+    last = jnp.max(jnp.where(match, index, -1), axis=1)
+    zero = jnp.zeros((), values.dtype)
+    lower = jnp.where((first < requests)[:, None], values[jnp.minimum(first, requests - 1)], zero)
+    upper = jnp.where((last > first)[:, None], values[jnp.maximum(last, 0)], zero)
+    return jnp.stack([lower, upper], axis=1)
 
 
 def unpack_slots(received, values, offsets, position, device, devices, capacity):
@@ -135,9 +133,9 @@
     capacity = (requests // 2 + devices - 2) // (devices - 1)
     per_device = requests // devices
     codes = codes_for(keep_lists, kept_counts[:, 0], drop_scores, lengths, device)
+    outgoing = pack_slots(codes, offsets, device, devices)
+    received = lax.all_to_all(outgoing, "kv", split_axis=0, concat_axis=0, tiled=True)
     position = route_tables(offsets, devices, capacity)
-    outgoing = pack_slots(codes, offsets, position, device, devices, capacity)
-    received = lax.all_to_all(outgoing, "kv", split_axis=0, concat_axis=0, tiled=True)
     held_codes = unpack_slots(received, codes, offsets, position, device, devices, capacity)
     queries_h = queries.reshape(requests, -1, head_dim)
     heads = queries_h.shape[1]

time: 61.1 us -> 60.4 us (0.989)
  other arithmetic: 7.92 us -> 6.3 us
  local copies, waits for them, and re-layouts: 5.43 us -> 6.35 us
    reduce_min x0 -> x1, other arithmetic: none -> 0.9 us  [pack_slots(): first = jnp.min(jnp.where(match, index, requests), axis=1)]
    reduce_sum x1, other arithmetic: 0.94 us -> 0.17 us  [route_tables(): jnp.sum((same & (index[None, :] < index[:, None])).astype(jnp.int32), axi...]
    eq x2 -> x0, other arithmetic: 0.74 us -> none  [the longest x1 0.73 us: pack_slots(): offsets[None, None, :] == amount[:, None, None]]
    another operation x0 -> x1, local copies, waits for them, and re-layouts: none -> 0.74 us  [pack_slots(): return jnp.stack([lower, upper], axis=1)]
    select_n x2, other arithmetic: 0.77 us -> 0.09 us  [the longest x1 0.08 us: pack_slots(): jnp.where((last > first)[:, None], values[jnp.maximum(last, 0)], zero)]
  transfers between devices with their start and end apart: 2 -> 2, of which waited for: 2 -> 2; matrix products, arithmetic and copies ran while one was open for 14% -> 15% of each run, Pallas kernels for 0% -> 0%
where the time goes in v5:
time: 60.4 us; the launch traced here: 60 us
  matrix products  15.7 us (26%)
  starting transfers between devices  13.9 us (23%)
  blocking collectives  9.46 us (16%)
  waiting for transfers between devices  8 us (13%)
  local copies, waits for them, and re-layouts  6.35 us (11%)
  other arithmetic  6.3 us (10%)
    all_to_all x1, blocking collectives, body(): lax.all_to_all(pieces, 'hd', split_axis=0, concat_axis=0, tiled=True)  9.46 us
    all_to_all x1, starting transfers between devices, body(): lax.all_to_all(outgoing, 'kv', split_axis=0, concat_axis=0, tiled=True)  8.42 us
    dot_general x1, matrix products, block_partial(): jnp.einsum('rkb,rbc->rkc', rows, block_data, preferred_element_type=jnp.f...  8.06 us
    all_to_all x1, waiting for transfers between devices, body(): lax.all_to_all(payload, 'kv', split_axis=0, concat_axis=0, tiled=True)  6.06 us
    dot_general x1, matrix products, raw_scores(): jnp.einsum('rhc,rbc->rhb', queries_h, block_data[..., :head_dim], preferr...  5.65 us
    all_to_all x1, starting transfers between devices, body(): lax.all_to_all(payload, 'kv', split_axis=0, concat_axis=0, tiled=True)  5.45 us
    dot_general x1, local copies, waits for them, and re-layouts, body(): jnp.dot(attended, out_weight, preferred_element_type=jnp.float32)  2.87 us
    all_to_all x1, waiting for transfers between devices, body(): lax.all_to_all(outgoing, 'kv', split_axis=0, concat_axis=0, tiled=True)  1.94 us
  transfers between devices with their start and end apart: 2, of which 2 were waited for; matrix products, arithmetic and copies ran while one was open for 15% of the time, Pallas kernels for 0%

profile of v5, /device:TPU:0, one launch (start us, length us, event | category | flops | bytes accessed | tf_op | source)
XLA Modules:
  0.0 60.0 jit_solution(1926312848253879644)
XLA Ops:
  0.0 0.0 copy-start.2
  0.0 0.0 copy-start.3
  0.0 0.0 copy-start
  0.0 0.0 copy-start.1
  0.0 0.9 %select_reduce_fusion.2 = (s32[32]{0:T(128)S(1)}, s32[32]{0:T(128)S(1)}) fusion(s32[64]{0:T(128)} %param.13, s32[32]{0:T(128)S(1)} %and_select_fusion.1, pred[32]{0:T(512)(128)(4,1)S(1)} %broadcast_compare_fusion.3), kind=kLoop, calls=%fused_computation.62 | loop fusion | flops 12224 | bytes 672 | tf_op jit(solution)/shard_map/reduce_min | solution.py:98
  1.0 0.7 %iota_compare_fusion.5 = pred[64,512]{1,0:T(8,128)(4,1)S(1)} fusion(s32[64]{0:T(128)} %bitcast.46), kind=kLoop, calls=%fused_computation.33 | loop fusion | flops 32768 | bytes 33024 | tf_op jit(solution)/shard_map/lt | solution.py:22
  1.8 0.9 %broadcast_shift-right-arithmetic_fusion = (s32[64,512]{1,0:T(8,128)S(1)}, s32[64,512]{1,0:T(8,128)S(1)}) fusion(s32[64,512]{1,0:T(8,128)} %param.9), kind=kLoop, calls=%fused_computation.40 | loop fusion | flops 65536 | bytes 393216 | tf_op jit(solution)/shard_map/shift_right_arithmetic | solution.py:23
  2.7 1.2 %fusion.6 = pred[64,16,32]{2,1,0:T(8,128)(4,1)S(1)} fusion(s32[64,512]{1,0:T(8,128)S(1)} %get-tuple-element.20, s32[64,512]{1,0:T(8,128)S(1)} %get-tuple-element.19, pred[64,512]{1,0:T(8,128)(4,1)S(1)} %iota_compare_fusion.5), kind=kOutput, calls=%fused_computation.10 | convolution fusion | flops 35684352 | bytes 327680 | tf_op jit(solution)/shard_map/rpa,rpb->rab/dot_general | solution.py:27
  3.9 0.3 copy.36
  4.2 0.1 copy.37
  4.3 0.0 copy-done.3
  4.3 0.0 copy-done
  4.3 0.1 fusion.20
  4.4 0.6 %gather_fusion.1 = f32[32,512]{1,0:T(8,128)S(1)} fusion(f32[64,512]{1,0:T(8,128)S(1)} %fusion.20, s32[1024]{0:T(1024)S(1)} %pad_clamp_fusion.1), kind=kCustom, calls=%fused_computation.1 | custom fusion | bytes 131200 | tf_op jit(solution)/shard_map/gather | solution.py:102
  5.0 0.6 %gather_fusion = f32[32,512]{1,0:T(8,128)S(1)} fusion(f32[64,512]{1,0:T(8,128)S(1)} %fusion.20, s32[1024]{0:T(1024)S(1)} %pad_clamp_fusion.2), kind=kCustom, calls=%fused_computation | custom fusion | bytes 131200 | tf_op jit(solution)/shard_map/gather | solution.py:101
  5.7 0.1 bitcast_select_fusion
  5.8 0.7 %copy.38 = f32[32,2,512]{2,1,0:T(2,128)} copy(f32[32,2,512]{2,0,1:T(8,128)S(1)} %pad_maximum_fusion.1) | data formatting | bytes 262144 | tf_op jit(solution)/shard_map/stack | solution.py:103
  6.5 8.4 %all-to-all-start = ((f32[32,2,512]{2,1,0:T(2,128)}), f32[32,2,512]{2,1,0:T(2,128)S(1)}, u32[]{:S(2)}, u32[]{:S(2)}) async-start(f32[32,2,512]{2,1,0:T(2,128)} %copy.38), calls=%async_computation | async-start | bytes 262144 | tf_op jit(solution)/shard_map/all_to_all | solution.py:137
  14.9 0.0 copy-done.2
  14.9 0.2 convert_reduce_fusion
  15.1 0.0 copy-done.1
  15.2 5.6 %fusion.9 = f32[64,4,512]{2,1,0:T(4,128)S(1)} fusion(bf16[64,4,128]{2,1,0:T(4,128)(2,1)S(1)} %reshape.186, bf16[64,512,256]{2,1,0:T(8,128)(2,1)} %param.8), kind=kOutput, calls=%fused_computation.11 | convolution fusion | flops 33685504 | bytes 8978432 | tf_op jit(solution)/shard_map/rhc,rbc->rhb/dot_general | solution.py:37
  20.8 1.9 %all-to-all-done = f32[32,2,512]{2,1,0:T(2,128)S(1)} async-done(((f32[32,2,512]{2,1,0:T(2,128)}), f32[32,2,512]{2,1,0:T(2,128)S(1)}, u32[]{:S(2)}, u32[]{:S(2)}) %all-to-all-start) | async-done | bytes 131104 | tf_op jit(solution)/shard_map/all_to_all | solution.py:137
  22.8 0.1 reshape.185
  22.9 0.7 %gather_fusion.2 = f32[64,512]{1,0:T(8,128)S(1)} fusion(f32[64,512]{1,0:T(8,128)S(1)} %reshape.185, s32[1024]{0:T(1024)S(1)} %pad_clamp_fusion), kind=kCustom, calls=%fused_computation.2 | custom fusion | bytes 262400 | tf_op jit(solution)/shard_map/gather | solution.py:110
  23.5 0.2 maximum_reduce_fusion
  23.8 0.1 fusion.23
  23.9 0.1 copy.39
  24.0 0.3 select_reduce_fusion
  24.3 0.6 fusion.19
  24.8 8.1 %fusion.14 = f32[64,5,256]{2,1,0:T(8,128)S(1)} fusion(bf16[64,512,256]{2,1,0:T(8,128)(2,1)} %param.8, bf16[64,4,512]{2,1,0:T(4,128)(2,1)S(1)} %get-tuple-element.15, bf16[64,1,512]{2,1,0:T(2,128)(2,1)S(1)} %copy.39), kind=kOutput, calls=%fused_computation.15 | convolution fusion | flops 84541440 | bytes 17432576 | tf_op jit(solution)/shard_map/rkb,rbc->rkc/dot_general | solution.py:62
  32.9 0.1 slice.59
  33.0 0.2 fusion.25
  33.2 0.1 convert_convert_fusion
  33.3 0.1 multiply_add_fusion
  33.4 0.1 select_maximum_fusion
  33.5 0.2 fusion.22
  33.7 0.7 %pad_maximum_fusion = f32[64,5,128]{2,1,0:T(8,128)} fusion(f32[64,1,128]{2,1,0:T(1,128)S(1)} %bitcast.45, f32[64,4,128]{2,1,0:T(4,128)S(1)} %fusion.22), kind=kLoop, calls=%fused_computation.23 | loop fusion | flops 40960 | bytes 327680 | tf_op jit(solution)/shard_map/concatenate | solution.py:146
  34.4 5.5 %all-to-all-start.1 = ((f32[64,5,128]{2,1,0:T(8,128)}), f32[64,5,128]{2,1,0:T(8,128)S(1)}, u32[]{:S(2)}, u32[]{:S(2)}) async-start(f32[64,5,128]{2,1,0:T(8,128)} %pad_maximum_fusion), calls=%async_computation.1 | async-start | bytes 524288 | tf_op jit(solution)/shard_map/all_to_all | solution.py:147
  39.9 2.9 %copy.44 = bf16[2048,512]{1,0:T(8,128)(2,1)S(1)} copy(bf16[2048,512]{0,1:T(8,128)(2,1)} %bitcast.35) | data formatting | bytes 4194304 | tf_op jit(solution)/shard_map/dot_general | solution.py:157
  42.7 6.1 %all-to-all-done.1 = f32[64,5,128]{2,1,0:T(8,128)S(1)} async-done(((f32[64,5,128]{2,1,0:T(8,128)}), f32[64,5,128]{2,1,0:T(8,128)S(1)}, u32[]{:S(2)}, u32[]{:S(2)}) %all-to-all-start.1) | async-done | bytes 163872 | tf_op jit(solution)/shard_map/all_to_all | solution.py:147
  48.8 0.1 fusion.36
  49.0 0.1 multiply_reduce_fusion
  49.0 0.1 fusion.21
  49.2 0.1 divide_convert_fusion.1
  49.3 0.6 %convolution_bitcast_fusion = f32[4,2,512]{2,1,0:T(2,128)S(1)} fusion(bf16[2,512,1]{1,0,2:T(2,128)(2,1)S(1)} %reshape.216, bf16[4,512,512]{2,1,0:T(8,128)(2,1)S(1)} %bitcast.34), kind=kOutput, calls=%fused_computation.12 | convolution fusion | flops 4194304 | bytes 2115584 | tf_op jit(solution)/shard_map/dot_general | solution.py:157
  49.9 9.5 %all_to_all.15 = f32[4,2,512]{2,1,0:T(2,128)S(1)} all-to-all(f32[4,2,512]{2,1,0:T(2,128)S(1)} %convolution_bitcast_fusion), channel_id=1, replica_groups=mesh['kv'=32,'hd'=4] {'hd'}, dimensions={0} | all-to-all | bytes 32768 | tf_op jit(solution)/shard_map/all_to_all | solution.py:160
  59.4 0.6 reduce_sum.59
  (20 shorter events, 0.2 us)
Async XLA Ops:
  0.0 14.9 %copy-start.2 = (s32[64]{0:T(128)S(1)}, s32[64]{0:T(128)}, u32[]{:S(2)}) copy-start(s32[64]{0:T(128)} %param.13) | copy-start | bytes 772
  0.0 4.3 %copy-start.3 = (s32[64]{0:T(128)S(1)}, s32[64]{0:T(128)}, u32[]{:S(2)}) copy-start(s32[64]{0:T(128)} %param.12) | copy-start | bytes 772
  0.0 4.3 %copy-start = (f32[64,512]{1,0:T(8,128)S(1)}, f32[64,512]{1,0:T(8,128)}, u32[]{:S(2)}) copy-start(f32[64,512]{1,0:T(8,128)} %param.11) | copy-start | bytes 393220
  0.0 15.1 %copy-start.1 = (bf16[64,512]{1,0:T(8,128)(2,1)S(1)}, bf16[64,512]{1,0:T(8,128)(2,1)}, u32[]{:S(2)}) copy-start(bf16[64,512]{1,0:T(8,128)(2,1)} %param.14) | copy-start | bytes 196612
  6.5 16.3 %all-to-all-start = ((f32[32,2,512]{2,1,0:T(2,128)}), f32[32,2,512]{2,1,0:T(2,128)S(1)}, u32[]{:S(2)}, u32[]{:S(2)}) async-start(f32[32,2,512]{2,1,0:T(2,128)} %copy.38), calls=%async_computation | async-start | bytes 262144 | tf_op jit(solution)/shard_map/all_to_all | solution.py:137
  34.4 14.4 %all-to-all-start.1 = ((f32[64,5,128]{2,1,0:T(8,128)}), f32[64,5,128]{2,1,0:T(8,128)S(1)}, u32[]{:S(2)}, u32[]{:S(2)}) async-start(f32[64,5,128]{2,1,0:T(8,128)} %pad_maximum_fusion), calls=%async_computation.1 | async-start | bytes 524288 | tf_op jit(solution)/shard_map/all_to_all | solution.py:147

commit v6 on v5

--- a/solution.py
+++ b/solution.py
@@ -90,24 +90,24 @@
     return position
 
 
-def pack_slots(values, offsets, device, devices):
+def pack_slots(values, offsets, device, devices, capacity):
     requests = offsets.shape[0]
     index = jnp.arange(requests, dtype=jnp.int32)
-    amount = (jnp.arange(devices, dtype=jnp.int32) - device) % devices
+    slot_ids = jnp.arange(devices * capacity, dtype=jnp.int32)
+    amount = (slot_ids // capacity - device) % devices
+    second = (slot_ids % capacity) == 1
     match = (offsets[None, :] == amount[:, None]) & (amount != 0)[:, None]
     first = jnp.min(jnp.where(match, index, requests), axis=1)
     last = jnp.max(jnp.where(match, index, -1), axis=1)
-    zero = jnp.zeros((), values.dtype)
-    lower = jnp.where((first < requests)[:, None], values[jnp.minimum(first, requests - 1)], zero)
-    upper = jnp.where((last > first)[:, None], values[jnp.maximum(last, 0)], zero)
-    return jnp.stack([lower, upper], axis=1)
+    chosen = jnp.clip(jnp.where(second, last, first), 0, requests - 1)
+    live = jnp.where(second, last > first, first < requests)
+    return jnp.where(live[:, None], values[chosen], jnp.zeros((), values.dtype))
 
 
 def unpack_slots(received, values, offsets, position, device, devices, capacity):
     source = (device - offsets) % devices
     slots = source * capacity + jnp.minimum(position, capacity - 1)
-    stacked = received.reshape((devices * capacity,) + received.shape[2:])
-    taken = stacked[slots]
+    taken = received[slots]
     moving = (offsets != 0)[:, None]
     return jnp.where(moving, taken, values)
 
@@ -133,7 +133,7 @@
     capacity = (requests // 2 + devices - 2) // (devices - 1)
     per_device = requests // devices
     codes = codes_for(keep_lists, kept_counts[:, 0], drop_scores, lengths, device)
-    outgoing = pack_slots(codes, offsets, device, devices)
+    outgoing = pack_slots(codes, offsets, device, devices, capacity)
     received = lax.all_to_all(outgoing, "kv", split_axis=0, concat_axis=0, tiled=True)
     position = route_tables(offsets, devices, capacity)
     held_codes = unpack_slots(received, codes, offsets, position, device, devices, capacity)

time: 60.4 us -> 60 us (level)
  local copies, waits for them, and re-layouts: 6.35 us -> 5.35 us
  other arithmetic: 6.3 us -> 6.91 us
    reduce_max x0 -> x1, other arithmetic: none -> 1 us  [pack_slots(): last = jnp.max(jnp.where(match, index, -1), axis=1)]
    reduce_min x1 -> x0, other arithmetic: 0.9 us -> none  [pack_slots(): first = jnp.min(jnp.where(match, index, requests), axis=1)]
    another operation x1 -> x0, local copies, waits for them, and re-layouts: 0.74 us -> none  [pack_slots(): return jnp.stack([lower, upper], axis=1)]
    select_n x4 -> x5, other arithmetic: 0.11 us -> 0.81 us  [the longest x2 0.77 us: pack_slots(): return jnp.where(live[:, None], values[chosen], jnp.zeros((), values.dtype))]
  transfers between devices with their start and end apart: 2 -> 2, of which waited for: 2 -> 2; matrix products, arithmetic and copies ran while one was open for 15% -> 14% of each run, Pallas kernels for 0% -> 0%
where the time goes in v6:
time: 60 us; the launch traced here: 59.6 us
  matrix products  15.7 us (26%)
  starting transfers between devices  13.7 us (23%)
  blocking collectives  9.46 us (16%)
  waiting for transfers between devices  8.18 us (14%)
  other arithmetic  6.91 us (12%)
  local copies, waits for them, and re-layouts  5.35 us (9%)
    all_to_all x1, blocking collectives, body(): lax.all_to_all(pieces, 'hd', split_axis=0, concat_axis=0, tiled=True)  9.46 us
    all_to_all x1, starting transfers between devices, body(): lax.all_to_all(outgoing, 'kv', split_axis=0, concat_axis=0, tiled=True)  8.42 us
    dot_general x1, matrix products, block_partial(): jnp.einsum('rkb,rbc->rkc', rows, block_data, preferred_element_type=jnp.f...  8.06 us
    all_to_all x1, waiting for transfers between devices, body(): lax.all_to_all(payload, 'kv', split_axis=0, concat_axis=0, tiled=True)  6.06 us
    dot_general x1, matrix products, raw_scores(): jnp.einsum('rhc,rbc->rhb', queries_h, block_data[..., :head_dim], preferr...  5.65 us
    all_to_all x1, starting transfers between devices, body(): lax.all_to_all(payload, 'kv', split_axis=0, concat_axis=0, tiled=True)  5.28 us
    dot_general x1, local copies, waits for them, and re-layouts, body(): jnp.dot(attended, out_weight, preferred_element_type=jnp.float32)  2.87 us
    all_to_all x1, waiting for transfers between devices, body(): lax.all_to_all(outgoing, 'kv', split_axis=0, concat_axis=0, tiled=True)  2.12 us
  transfers between devices with their start and end apart: 2, of which 2 were waited for; matrix products, arithmetic and copies ran while one was open for 14% of the time, Pallas kernels for 0%

profile of v6, /device:TPU:0, one launch (start us, length us, event | category | flops | bytes accessed | tf_op | source)
XLA Modules:
  0.0 59.6 jit_solution(8421671878613511389)
XLA Ops:
  0.0 0.0 copy-start.2
  0.0 0.0 copy-start.3
  0.0 0.0 copy-start
  0.0 0.0 copy-start.1
  0.0 1.0 %select_reduce_fusion.2 = (s32[64]{0:T(128)S(1)}, s32[64]{0:T(128)S(1)}, s32[64]{0:T(128)S(1)}) fusion(s32[64]{0:T(128)} %param.13, s32[64]{0:T(128)S(1)} %and_select_fusion.2, pred[64]{0:T(512)(128)(4,1)S(1)} %broadcast_compare_fusion.3), kind=kLoop, calls=%fused_computation.52 | loop fusion | flops 44864 | bytes 1344 | tf_op jit(solution)/shard_map/reduce_max | solution.py:101
  1.1 0.1 lt.88
  1.2 0.1 gt.30
  1.3 0.7 %iota_compare_fusion.5 = pred[64,512]{1,0:T(8,128)(4,1)S(1)} fusion(s32[64]{0:T(128)} %bitcast.48), kind=kLoop, calls=%fused_computation.31 | loop fusion | flops 32768 | bytes 33024 | tf_op jit(solution)/shard_map/lt | solution.py:22
  2.1 0.9 %broadcast_shift-right-arithmetic_fusion = (s32[64,512]{1,0:T(8,128)S(1)}, s32[64,512]{1,0:T(8,128)S(1)}) fusion(s32[64,512]{1,0:T(8,128)} %param.9), kind=kLoop, calls=%fused_computation.37 | loop fusion | flops 65536 | bytes 393216 | tf_op jit(solution)/shard_map/shift_right_arithmetic | solution.py:23
  3.0 1.2 %fusion.6 = pred[64,16,32]{2,1,0:T(8,128)(4,1)S(1)} fusion(s32[64,512]{1,0:T(8,128)S(1)} %get-tuple-element.21, s32[64,512]{1,0:T(8,128)S(1)} %get-tuple-element.20, pred[64,512]{1,0:T(8,128)(4,1)S(1)} %iota_compare_fusion.5), kind=kOutput, calls=%fused_computation.9 | convolution fusion | flops 35684352 | bytes 327680 | tf_op jit(solution)/shard_map/rpa,rpb->rab/dot_general | solution.py:27
  4.2 0.3 copy.33
  4.5 0.1 copy.34
  4.6 0.0 copy-done.3
  4.6 0.0 copy-done
  4.6 0.1 fusion.20
  4.8 0.7 %gather_fusion = f32[64,512]{1,0:T(8,128)S(1)} fusion(f32[64,512]{1,0:T(8,128)S(1)} %fusion.20, s32[1024]{0:T(1024)S(1)} %pad_clamp_fusion.1), kind=kCustom, calls=%fused_computation | custom fusion | bytes 262400 | tf_op jit(solution)/shard_map/gather | solution.py:104
  5.4 0.1 gather.9
  5.5 0.8 %broadcast_select_fusion = f32[32,2,512]{2,1,0:T(2,128)} fusion(f32[32,2,512]{2,1,0:T(2,128)S(1)} %gather.9, pred[32,2]{1,0:T(8,128)(4,1)S(1)} %fusion.32), kind=kLoop, calls=%fused_computation.32 | loop fusion | flops 32768 | bytes 262208 | tf_op jit(solution)/shard_map/jit(_where)/select_n | solution.py:104
  6.3 8.4 %all-to-all-start = ((f32[32,2,512]{2,1,0:T(2,128)}), f32[32,2,512]{2,1,0:T(2,128)S(1)}, u32[]{:S(2)}, u32[]{:S(2)}) async-start(f32[32,2,512]{2,1,0:T(2,128)} %broadcast_select_fusion), calls=%async_computation | async-start | bytes 262144 | tf_op jit(solution)/shard_map/all_to_all | solution.py:137
  14.7 0.0 copy-done.2
  14.7 0.0 copy-done.1
  14.8 5.6 %fusion.9 = f32[64,4,512]{2,1,0:T(4,128)S(1)} fusion(bf16[64,4,128]{2,1,0:T(4,128)(2,1)S(1)} %reshape.177, bf16[64,512,256]{2,1,0:T(8,128)(2,1)} %param.8), kind=kOutput, calls=%fused_computation.10 | convolution fusion | flops 33685504 | bytes 8978432 | tf_op jit(solution)/shard_map/rhc,rbc->rhb/dot_general | solution.py:37
  20.4 2.1 %all-to-all-done = f32[32,2,512]{2,1,0:T(2,128)S(1)} async-done(((f32[32,2,512]{2,1,0:T(2,128)}), f32[32,2,512]{2,1,0:T(2,128)S(1)}, u32[]{:S(2)}, u32[]{:S(2)}) %all-to-all-start) | async-done | bytes 131104 | tf_op jit(solution)/shard_map/all_to_all | solution.py:137
  22.6 0.1 all_to_all.13
  22.7 0.7 %gather_fusion.1 = f32[64,512]{1,0:T(8,128)S(1)} fusion(f32[64,512]{1,0:T(8,128)S(1)} %all_to_all.13, s32[1024]{0:T(1024)S(1)} %pad_clamp_fusion), kind=kCustom, calls=%fused_computation.1 | custom fusion | bytes 262400 | tf_op jit(solution)/shard_map/gather | solution.py:110
  23.3 0.2 maximum_reduce_fusion
  23.6 0.1 fusion.23
  23.6 0.1 copy.35
  23.8 0.3 select_reduce_fusion
  24.0 0.6 fusion.19
  24.6 8.1 %fusion.14 = f32[64,5,256]{2,1,0:T(8,128)S(1)} fusion(bf16[64,512,256]{2,1,0:T(8,128)(2,1)} %param.8, bf16[64,4,512]{2,1,0:T(4,128)(2,1)S(1)} %get-tuple-element.16, bf16[64,1,512]{2,1,0:T(2,128)(2,1)S(1)} %copy.35), kind=kOutput, calls=%fused_computation.14 | convolution fusion | flops 84541440 | bytes 17432576 | tf_op jit(solution)/shard_map/rkb,rbc->rkc/dot_general | solution.py:62
  32.6 0.1 slice.57
  32.7 0.2 fusion.25
  32.9 0.1 convert_convert_fusion
  33.0 0.1 multiply_add_fusion
  33.1 0.1 select_maximum_fusion
  33.2 0.2 fusion.22
  33.4 0.7 %pad_maximum_fusion = f32[64,5,128]{2,1,0:T(8,128)} fusion(f32[64,1,128]{2,1,0:T(1,128)S(1)} %bitcast.47, f32[64,4,128]{2,1,0:T(4,128)S(1)} %fusion.22), kind=kLoop, calls=%fused_computation.22 | loop fusion | flops 40960 | bytes 327680 | tf_op jit(solution)/shard_map/concatenate | solution.py:146
  34.2 5.3 %all-to-all-start.1 = ((f32[64,5,128]{2,1,0:T(8,128)}), f32[64,5,128]{2,1,0:T(8,128)S(1)}, u32[]{:S(2)}, u32[]{:S(2)}) async-start(f32[64,5,128]{2,1,0:T(8,128)} %pad_maximum_fusion), calls=%async_computation.1 | async-start | bytes 524288 | tf_op jit(solution)/shard_map/all_to_all | solution.py:147
  39.5 2.9 %copy.40 = bf16[2048,512]{1,0:T(8,128)(2,1)S(1)} copy(bf16[2048,512]{0,1:T(8,128)(2,1)} %bitcast.37) | data formatting | bytes 4194304 | tf_op jit(solution)/shard_map/dot_general | solution.py:157
  42.3 6.1 %all-to-all-done.1 = f32[64,5,128]{2,1,0:T(8,128)S(1)} async-done(((f32[64,5,128]{2,1,0:T(8,128)}), f32[64,5,128]{2,1,0:T(8,128)S(1)}, u32[]{:S(2)}, u32[]{:S(2)}) %all-to-all-start.1) | async-done | bytes 163872 | tf_op jit(solution)/shard_map/all_to_all | solution.py:147
  48.4 0.1 fusion.42
  48.6 0.1 multiply_reduce_fusion
  48.6 0.1 fusion.21
  48.8 0.1 divide_convert_fusion.1
  48.9 0.6 %convolution_bitcast_fusion = f32[4,2,512]{2,1,0:T(2,128)S(1)} fusion(bf16[2,512,1]{1,0,2:T(2,128)(2,1)S(1)} %reshape.198, bf16[4,512,512]{2,1,0:T(8,128)(2,1)S(1)} %bitcast.36), kind=kOutput, calls=%fused_computation.11 | convolution fusion | flops 4194304 | bytes 2115584 | tf_op jit(solution)/shard_map/dot_general | solution.py:157
  49.5 9.5 %all_to_all.19 = f32[4,2,512]{2,1,0:T(2,128)S(1)} all-to-all(f32[4,2,512]{2,1,0:T(2,128)S(1)} %convolution_bitcast_fusion), channel_id=1, replica_groups=mesh['kv'=32,'hd'=4] {'hd'}, dimensions={0} | all-to-all | bytes 32768 | tf_op jit(solution)/shard_map/all_to_all | solution.py:160
  59.0 0.6 reduce_sum.59
  (18 shorter events, 0.2 us)
Async XLA Ops:
  0.0 14.7 %copy-start.2 = (s32[64]{0:T(128)S(1)}, s32[64]{0:T(128)}, u32[]{:S(2)}) copy-start(s32[64]{0:T(128)} %param.13) | copy-start | bytes 772
  0.0 4.6 %copy-start.3 = (s32[64]{0:T(128)S(1)}, s32[64]{0:T(128)}, u32[]{:S(2)}) copy-start(s32[64]{0:T(128)} %param.12) | copy-start | bytes 772
  0.0 4.6 %copy-start = (f32[64,512]{1,0:T(8,128)S(1)}, f32[64,512]{1,0:T(8,128)}, u32[]{:S(2)}) copy-start(f32[64,512]{1,0:T(8,128)} %param.11) | copy-start | bytes 393220
  0.0 14.7 %copy-start.1 = (bf16[64,512]{1,0:T(8,128)(2,1)S(1)}, bf16[64,512]{1,0:T(8,128)(2,1)}, u32[]{:S(2)}) copy-start(bf16[64,512]{1,0:T(8,128)(2,1)} %param.14) | copy-start | bytes 196612
  6.3 16.3 %all-to-all-start = ((f32[32,2,512]{2,1,0:T(2,128)}), f32[32,2,512]{2,1,0:T(2,128)S(1)}, u32[]{:S(2)}, u32[]{:S(2)}) async-start(f32[32,2,512]{2,1,0:T(2,128)} %broadcast_select_fusion), calls=%async_computation | async-start | bytes 262144 | tf_op jit(solution)/shard_map/all_to_all | solution.py:137
  34.2 14.2 %all-to-all-start.1 = ((f32[64,5,128]{2,1,0:T(8,128)}), f32[64,5,128]{2,1,0:T(8,128)S(1)}, u32[]{:S(2)}, u32[]{:S(2)}) async-start(f32[64,5,128]{2,1,0:T(8,128)} %pad_maximum_fusion), calls=%async_computation.1 | async-start | bytes 524288 | tf_op jit(solution)/shard_map/all_to_all | solution.py:147

commit v7 on v6

--- a/solution.py
+++ b/solution.py
@@ -19,11 +19,11 @@
     low = 32
     high = block_rows // low
     places = jnp.arange(block_rows, dtype=jnp.int32)[None, :]
-    counted = places < count_block[:, None]
-    upper = (keep_block >> 5)[..., None] == jnp.arange(high, dtype=jnp.int32)
-    lower = (keep_block & (low - 1))[..., None] == jnp.arange(low, dtype=jnp.int32)
-    upper = (upper & counted[..., None]).astype(jnp.bfloat16)
-    lower = lower.astype(jnp.bfloat16)
+    counted_hi = jnp.where(places < count_block[:, None], keep_block >> 5, -1)
+    upper = (counted_hi[..., None] == jnp.arange(high, dtype=jnp.int32)).astype(jnp.bfloat16)
+    lower = ((keep_block & (low - 1))[..., None] == jnp.arange(low, dtype=jnp.int32)).astype(
+        jnp.bfloat16
+    )
     kept = jnp.einsum("rpa,rpb->rab", upper, lower, preferred_element_type=jnp.float32)
     kept_rows = kept.reshape(requests, block_rows) > 0.5
     position = block_index * block_rows + jnp.arange(block_rows, dtype=jnp.int32)

time: 60 us -> 60.1 us (level)
    select_n x0 -> x1, other arithmetic: none -> 0.99 us  [codes_for(): counted_hi = jnp.where(places < count_block[:, None], keep_block >> 5, -1)]
    shift_right_arithmetic x1 -> x0, other arithmetic: 0.93 us -> none  [codes_for(): upper = (keep_block >> 5)[..., None] == jnp.arange(high, dtype=jnp.int32)]
    select_n x1, other arithmetic: 0.1 us -> 1 us  [codes_for(): jnp.where(valid_rows & kept_rows, -1.0, jnp.where(valid_rows, score_block...]
    lt x1 -> x0, other arithmetic: 0.75 us -> none  [codes_for(): counted = places < count_block[:, None]]
where the time goes in v7:
time: 60.1 us; the launch traced here: 59.6 us
  matrix products  15.6 us (26%)
  starting transfers between devices  13.7 us (23%)
  blocking collectives  9.46 us (16%)
  waiting for transfers between devices  8.18 us (14%)
  other arithmetic  7.1 us (12%)
  local copies, waits for them, and re-layouts  5.34 us (9%)
    all_to_all x1, blocking collectives, body(): lax.all_to_all(pieces, 'hd', split_axis=0, concat_axis=0, tiled=True)  9.46 us
    all_to_all x1, starting transfers between devices, body(): lax.all_to_all(outgoing, 'kv', split_axis=0, concat_axis=0, tiled=True)  8.42 us
    dot_general x1, matrix products, block_partial(): jnp.einsum('rkb,rbc->rkc', rows, block_data, preferred_element_type=jnp.f...  8.06 us
    all_to_all x1, waiting for transfers between devices, body(): lax.all_to_all(payload, 'kv', split_axis=0, concat_axis=0, tiled=True)  6.06 us
    dot_general x1, matrix products, raw_scores(): jnp.einsum('rhc,rbc->rhb', queries_h, block_data[..., :head_dim], preferr...  5.65 us
    all_to_all x1, starting transfers between devices, body(): lax.all_to_all(payload, 'kv', split_axis=0, concat_axis=0, tiled=True)  5.28 us
    dot_general x1, local copies, waits for them, and re-layouts, body(): jnp.dot(attended, out_weight, preferred_element_type=jnp.float32)  2.87 us
    all_to_all x1, waiting for transfers between devices, body(): lax.all_to_all(outgoing, 'kv', split_axis=0, concat_axis=0, tiled=True)  2.12 us
  transfers between devices with their start and end apart: 2, of which 2 were waited for; matrix products, arithmetic and copies ran while one was open for 14% of the time, Pallas kernels for 0%

profile of v7, /device:TPU:0, one launch (start us, length us, event | category | flops | bytes accessed | tf_op | source)
XLA Modules:
  0.0 59.6 jit_solution(17794612312508876663)
XLA Ops:
  0.0 0.0 copy-start.1
  0.0 0.0 copy-start
  0.0 1.0 %select_reduce_fusion.2 = (s32[64]{0:T(128)S(1)}, s32[64]{0:T(128)S(1)}, s32[64]{0:T(128)S(1)}) fusion(s32[64]{0:T(128)} %param.13, s32[64]{0:T(128)S(1)} %and_select_fusion.2, pred[64]{0:T(512)(128)(4,1)S(1)} %broadcast_compare_fusion.3), kind=kLoop, calls=%fused_computation.50 | loop fusion | flops 44864 | bytes 1344 | tf_op jit(solution)/shard_map/reduce_max | solution.py:101
  1.0 0.1 lt.86
  1.2 0.1 gt.30
  1.3 1.0 %shift-right-arithmetic_select_fusion = (s32[64,512]{1,0:T(8,128)S(1)}, s32[64,512]{1,0:T(8,128)S(1)}) fusion(s32[64,512]{1,0:T(8,128)} %param.9, s32[64]{0:T(128)} %bitcast.48), kind=kLoop, calls=%fused_computation.29 | loop fusion | flops 131072 | bytes 393472 | tf_op jit(solution)/shard_map/jit(_where)/select_n | solution.py:22
  2.3 1.1 %fusion.4 = pred[64,16,32]{2,1,0:T(8,128)(4,1)S(1)} fusion(s32[64,512]{1,0:T(8,128)S(1)} %get-tuple-element.21, s32[64,512]{1,0:T(8,128)S(1)} %get-tuple-element.20), kind=kOutput, calls=%fused_computation.8 | convolution fusion | flops 35160064 | bytes 294912 | tf_op jit(solution)/shard_map/rpa,rpb->rab/dot_general | solution.py:27
  3.3 0.3 copy.33
  3.6 0.1 copy.34
  3.8 1.0 %fusion.15 = f32[64,512]{1,0:T(8,128)S(1)} fusion(f32[64,512]{1,0:T(8,128)} %param.11, pred[64,512]{1,0:T(8,128)(4,1)S(1)} %copy.34, s32[512]{0:T(512)S(1)} %iota_add_fusion, s32[64]{0:T(128)} %param.12), kind=kLoop, calls=%fused_computation.23 | loop fusion | flops 131072 | bytes 297216 | tf_op jit(solution)/shard_map/jit(_where)/select_n | solution.py:31
  4.8 0.7 %gather_fusion = f32[64,512]{1,0:T(8,128)S(1)} fusion(f32[64,512]{1,0:T(8,128)S(1)} %fusion.15, s32[1024]{0:T(1024)S(1)} %pad_clamp_fusion.1), kind=kCustom, calls=%fused_computation | custom fusion | bytes 262400 | tf_op jit(solution)/shard_map/gather | solution.py:104
  5.4 0.1 gather.9
  5.6 0.8 %broadcast_select_fusion = f32[32,2,512]{2,1,0:T(2,128)} fusion(f32[32,2,512]{2,1,0:T(2,128)S(1)} %gather.9, pred[32,2]{1,0:T(8,128)(4,1)S(1)} %fusion.27), kind=kLoop, calls=%fused_computation.31 | loop fusion | flops 32768 | bytes 262208 | tf_op jit(solution)/shard_map/jit(_where)/select_n | solution.py:104
  6.3 8.4 %all-to-all-start = ((f32[32,2,512]{2,1,0:T(2,128)}), f32[32,2,512]{2,1,0:T(2,128)S(1)}, u32[]{:S(2)}, u32[]{:S(2)}) async-start(f32[32,2,512]{2,1,0:T(2,128)} %broadcast_select_fusion), calls=%async_computation | async-start | bytes 262144 | tf_op jit(solution)/shard_map/all_to_all | solution.py:137
  14.7 0.0 copy-done.1
  14.8 0.0 copy-done
  14.8 5.6 %fusion.5 = f32[64,4,512]{2,1,0:T(4,128)S(1)} fusion(bf16[64,4,128]{2,1,0:T(4,128)(2,1)S(1)} %reshape.155, bf16[64,512,256]{2,1,0:T(8,128)(2,1)} %param.8), kind=kOutput, calls=%fused_computation.9 | convolution fusion | flops 33685504 | bytes 8978432 | tf_op jit(solution)/shard_map/rhc,rbc->rhb/dot_general | solution.py:37
  20.5 2.1 %all-to-all-done = f32[32,2,512]{2,1,0:T(2,128)S(1)} async-done(((f32[32,2,512]{2,1,0:T(2,128)}), f32[32,2,512]{2,1,0:T(2,128)S(1)}, u32[]{:S(2)}, u32[]{:S(2)}) %all-to-all-start) | async-done | bytes 131104 | tf_op jit(solution)/shard_map/all_to_all | solution.py:137
  22.6 0.1 all_to_all.13
  22.7 0.7 %gather_fusion.1 = f32[64,512]{1,0:T(8,128)S(1)} fusion(f32[64,512]{1,0:T(8,128)S(1)} %all_to_all.13, s32[1024]{0:T(1024)S(1)} %pad_clamp_fusion), kind=kCustom, calls=%fused_computation.1 | custom fusion | bytes 262400 | tf_op jit(solution)/shard_map/gather | solution.py:110
  23.3 0.2 maximum_reduce_fusion
  23.6 0.1 fusion.18
  23.7 0.1 copy.35
  23.8 0.3 select_reduce_fusion
  24.1 0.6 fusion.14
  24.6 8.1 %fusion.9 = f32[64,5,256]{2,1,0:T(8,128)S(1)} fusion(bf16[64,512,256]{2,1,0:T(8,128)(2,1)} %param.8, bf16[64,4,512]{2,1,0:T(4,128)(2,1)S(1)} %get-tuple-element.16, bf16[64,1,512]{2,1,0:T(2,128)(2,1)S(1)} %copy.35), kind=kOutput, calls=%fused_computation.12 | convolution fusion | flops 84541440 | bytes 17432576 | tf_op jit(solution)/shard_map/rkb,rbc->rkc/dot_general | solution.py:62
  32.7 0.1 slice.57
  32.8 0.2 fusion.20
  33.0 0.1 convert_convert_fusion
  33.1 0.1 multiply_add_fusion
  33.2 0.1 select_maximum_fusion
  33.3 0.2 fusion.17
  33.5 0.7 %pad_maximum_fusion = f32[64,5,128]{2,1,0:T(8,128)} fusion(f32[64,1,128]{2,1,0:T(1,128)S(1)} %bitcast.47, f32[64,4,128]{2,1,0:T(4,128)S(1)} %fusion.17), kind=kLoop, calls=%fused_computation.20 | loop fusion | flops 40960 | bytes 327680 | tf_op jit(solution)/shard_map/concatenate | solution.py:146
  34.2 5.3 %all-to-all-start.1 = ((f32[64,5,128]{2,1,0:T(8,128)}), f32[64,5,128]{2,1,0:T(8,128)S(1)}, u32[]{:S(2)}, u32[]{:S(2)}) async-start(f32[64,5,128]{2,1,0:T(8,128)} %pad_maximum_fusion), calls=%async_computation.1 | async-start | bytes 524288 | tf_op jit(solution)/shard_map/all_to_all | solution.py:147
  39.5 2.9 %copy.40 = bf16[2048,512]{1,0:T(8,128)(2,1)S(1)} copy(bf16[2048,512]{0,1:T(8,128)(2,1)} %bitcast.37) | data formatting | bytes 4194304 | tf_op jit(solution)/shard_map/dot_general | solution.py:157
  42.4 6.1 %all-to-all-done.1 = f32[64,5,128]{2,1,0:T(8,128)S(1)} async-done(((f32[64,5,128]{2,1,0:T(8,128)}), f32[64,5,128]{2,1,0:T(8,128)S(1)}, u32[]{:S(2)}, u32[]{:S(2)}) %all-to-all-start.1) | async-done | bytes 163872 | tf_op jit(solution)/shard_map/all_to_all | solution.py:147
  48.4 0.1 fusion.37
  48.6 0.1 multiply_reduce_fusion
  48.7 0.1 fusion.16
  48.8 0.1 divide_convert_fusion.1
  48.9 0.6 %convolution_bitcast_fusion = f32[4,2,512]{2,1,0:T(2,128)S(1)} fusion(bf16[2,512,1]{1,0,2:T(2,128)(2,1)S(1)} %reshape.176, bf16[4,512,512]{2,1,0:T(8,128)(2,1)S(1)} %bitcast.36), kind=kOutput, calls=%fused_computation.10 | convolution fusion | flops 4194304 | bytes 2115584 | tf_op jit(solution)/shard_map/dot_general | solution.py:157
  49.6 9.5 %all_to_all.19 = f32[4,2,512]{2,1,0:T(2,128)S(1)} all-to-all(f32[4,2,512]{2,1,0:T(2,128)S(1)} %convolution_bitcast_fusion), channel_id=1, replica_groups=mesh['kv'=32,'hd'=4] {'hd'}, dimensions={0} | all-to-all | bytes 32768 | tf_op jit(solution)/shard_map/all_to_all | solution.py:160
  59.0 0.6 reduce_sum.59
  (18 shorter events, 0.2 us)
Async XLA Ops:
  0.0 14.7 %copy-start.1 = (s32[64]{0:T(128)S(1)}, s32[64]{0:T(128)}, u32[]{:S(2)}) copy-start(s32[64]{0:T(128)} %param.13) | copy-start | bytes 772
  0.0 14.8 %copy-start = (bf16[64,512]{1,0:T(8,128)(2,1)S(1)}, bf16[64,512]{1,0:T(8,128)(2,1)}, u32[]{:S(2)}) copy-start(bf16[64,512]{1,0:T(8,128)(2,1)} %param.14) | copy-start | bytes 196612
  6.3 16.3 %all-to-all-start = ((f32[32,2,512]{2,1,0:T(2,128)}), f32[32,2,512]{2,1,0:T(2,128)S(1)}, u32[]{:S(2)}, u32[]{:S(2)}) async-start(f32[32,2,512]{2,1,0:T(2,128)} %broadcast_select_fusion), calls=%async_computation | async-start | bytes 262144 | tf_op jit(solution)/shard_map/all_to_all | solution.py:137
  34.2 14.2 %all-to-all-start.1 = ((f32[64,5,128]{2,1,0:T(8,128)}), f32[64,5,128]{2,1,0:T(8,128)S(1)}, u32[]{:S(2)}, u32[]{:S(2)}) async-start(f32[64,5,128]{2,1,0:T(8,128)} %pad_maximum_fusion), calls=%async_computation.1 | async-start | bytes 524288 | tf_op jit(solution)/shard_map/all_to_all | solution.py:147

commit v8 on v7

--- a/solution.py
+++ b/solution.py
@@ -96,12 +96,14 @@
     slot_ids = jnp.arange(devices * capacity, dtype=jnp.int32)
     amount = (slot_ids // capacity - device) % devices
     second = (slot_ids % capacity) == 1
-    match = (offsets[None, :] == amount[:, None]) & (amount != 0)[:, None]
-    first = jnp.min(jnp.where(match, index, requests), axis=1)
-    last = jnp.max(jnp.where(match, index, -1), axis=1)
-    chosen = jnp.clip(jnp.where(second, last, first), 0, requests - 1)
-    live = jnp.where(second, last > first, first < requests)
-    return jnp.where(live[:, None], values[chosen], jnp.zeros((), values.dtype))
+    same = offsets[:, None] == offsets[None, :]
+    earlier = jnp.sum((same & (index[None, :] < index[:, None])).astype(jnp.int32), axis=1)
+    match = (
+        (offsets[None, :] == amount[:, None])
+        & (amount != 0)[:, None]
+        & ((earlier[None, :] == 1) == second[:, None])
+    )
+    return jnp.dot(match.astype(values.dtype), values, precision=lax.Precision.HIGHEST)
 
 
 def unpack_slots(received, values, offsets, position, device, devices, capacity):

time: 60.1 us -> 59.3 us (0.987)
  other arithmetic: 7.1 us -> 5.27 us
  matrix products: 15.6 us -> 16.9 us
    select_n x4 -> x0, other arithmetic: 1.79 us -> none  [the longest x1 1 us: codes_for(): jnp.where(valid_rows & kept_rows, -1.0, jnp.where(valid_rows, score_block...]
    dot_general x0 -> x1, matrix products: none -> 1.21 us  [pack_slots(): jnp.dot(match.astype(values.dtype), values, precision=lax.Precision.HIGHEST)]
    reduce_max x1 -> x0, other arithmetic: 0.97 us -> none  [pack_slots(): last = jnp.max(jnp.where(match, index, -1), axis=1)]
    reduce_sum x0 -> x1, other arithmetic: none -> 0.91 us  [pack_slots(): jnp.sum((same & (index[None, :] < index[:, None])).astype(jnp.int32), axi...]
    gather x2 -> x0, local copies, waits for them, and re-layouts: 0.73 us -> none  [pack_slots(): return jnp.where(live[:, None], values[chosen], jnp.zeros((), values.dtype))]
    all_to_all x1 -> x2, local copies, waits for them, and re-layouts: 0.09 us -> 0.8 us  [body(): lax.all_to_all(outgoing, 'kv', split_axis=0, concat_axis=0, tiled=True)]
  transfers between devices with their start and end apart: 2 -> 2, of which waited for: 2 -> 2; matrix products, arithmetic and copies ran while one was open for 14% -> 15% of each run, Pallas kernels for 0% -> 0%
where the time goes in v8:
time: 59.3 us; the launch traced here: 58.8 us
  matrix products  16.9 us (28%)
  starting transfers between devices  13.8 us (23%)
  blocking collectives  9.46 us (16%)
  waiting for transfers between devices  8.12 us (14%)
  other arithmetic  5.27 us (9%)
  local copies, waits for them, and re-layouts  5.1 us (9%)
    all_to_all x1, blocking collectives, body(): lax.all_to_all(pieces, 'hd', split_axis=0, concat_axis=0, tiled=True)  9.46 us
    all_to_all x1, starting transfers between devices, body(): lax.all_to_all(outgoing, 'kv', split_axis=0, concat_axis=0, tiled=True)  8.42 us
    dot_general x1, matrix products, block_partial(): jnp.einsum('rkb,rbc->rkc', rows, block_data, preferred_element_type=jnp.f...  8.06 us
    all_to_all x1, waiting for transfers between devices, body(): lax.all_to_all(payload, 'kv', split_axis=0, concat_axis=0, tiled=True)  6.06 us
    dot_general x1, matrix products, raw_scores(): jnp.einsum('rhc,rbc->rhb', queries_h, block_data[..., :head_dim], preferr...  5.68 us
    all_to_all x1, starting transfers between devices, body(): lax.all_to_all(payload, 'kv', split_axis=0, concat_axis=0, tiled=True)  5.33 us
    dot_general x1, local copies, waits for them, and re-layouts, body(): jnp.dot(attended, out_weight, preferred_element_type=jnp.float32)  2.87 us
    all_to_all x1, waiting for transfers between devices, body(): lax.all_to_all(outgoing, 'kv', split_axis=0, concat_axis=0, tiled=True)  2.06 us
  transfers between devices with their start and end apart: 2, of which 2 were waited for; matrix products, arithmetic and copies ran while one was open for 15% of the time, Pallas kernels for 0%

profile of v8, /device:TPU:0, one launch (start us, length us, event | category | flops | bytes accessed | tf_op | source)
XLA Modules:
  0.0 58.8 jit_solution(8364244257538836834)
XLA Ops:
  0.0 0.0 copy-start.3
  0.0 0.0 copy-start.1
  0.0 0.9 %convert_reduce_fusion = s32[64]{0:T(128)S(1)} fusion(s32[64]{0:T(128)} %param.13), kind=kLoop, calls=%fused_computation.50 | loop fusion | flops 20416 | bytes 512 | tf_op jit(solution)/shard_map/reduce_sum | solution.py:100
  1.0 1.0 %shift-right-arithmetic_select_fusion = (s32[64,512]{1,0:T(8,128)S(1)}, s32[64,512]{1,0:T(8,128)S(1)}) fusion(s32[64,512]{1,0:T(8,128)} %param.9, s32[64]{0:T(128)} %bitcast.38), kind=kLoop, calls=%fused_computation.28 | loop fusion | flops 131072 | bytes 393472 | tf_op jit(solution)/shard_map/jit(_where)/select_n | solution.py:22
  2.0 1.1 %fusion.4 = pred[64,16,32]{2,1,0:T(8,128)(4,1)S(1)} fusion(s32[64,512]{1,0:T(8,128)S(1)} %get-tuple-element.18, s32[64,512]{1,0:T(8,128)S(1)} %get-tuple-element.17), kind=kOutput, calls=%fused_computation.7 | convolution fusion | flops 35160064 | bytes 294912 | tf_op jit(solution)/shard_map/rpa,rpb->rab/dot_general | solution.py:27
  3.0 0.3 copy.33
  3.3 0.1 copy.34
  3.5 1.2 %fusion.19 = f32[64,512]{1,0:T(8,128)S(1)} fusion(f32[64,512]{1,0:T(8,128)} %param.11, pred[64,512]{1,0:T(32,128)(4,1)S(1)} %copy.34, s32[512]{0:T(512)S(1)} %iota_add_fusion, s32[64]{0:T(128)} %param.12, s32[64]{0:T(128)} %param.13, s32[64]{0:T(128)S(1)} %and_select_fusion.2, pred[64]{0:T(512)(128)(4,1)S(1)} %broadcast_compare_fusion.3, ...), kind=kOutput, calls=%fused_computation.32 | convolution fusion | flops 25313280 | bytes 297920 | tf_op jit(solution)/shard_map/dot_general | solution.py:106
  4.7 0.7 %all_to_all.14 = f32[32,2,512]{2,1,0:T(2,128)} reshape(f32[64,512]{1,0:T(8,128)S(1)} %fusion.19) | data formatting | bytes 262144 | tf_op jit(solution)/shard_map/all_to_all | solution.py:139
  5.4 8.4 %all-to-all-start = ((f32[32,2,512]{2,1,0:T(2,128)}), f32[32,2,512]{2,1,0:T(2,128)S(1)}, u32[]{:S(2)}, u32[]{:S(2)}) async-start(f32[32,2,512]{2,1,0:T(2,128)} %all_to_all.14), calls=%async_computation | async-start | bytes 262144 | tf_op jit(solution)/shard_map/all_to_all | solution.py:139
  13.8 0.0 copy-done.3
  13.8 0.0 copy-done.1
  13.9 0.0 copy-start
  13.9 0.0 copy-start.2
  13.9 5.7 %fusion.5 = f32[64,4,512]{2,1,0:T(4,128)S(1)} fusion(bf16[64,4,128]{2,1,0:T(4,128)(2,1)S(1)} %reshape.101, bf16[64,512,256]{2,1,0:T(8,128)(2,1)} %param.8), kind=kOutput, calls=%fused_computation.8 | convolution fusion | flops 33685504 | bytes 8978432 | tf_op jit(solution)/shard_map/rhc,rbc->rhb/dot_general | solution.py:37
  19.6 2.1 %all-to-all-done = f32[32,2,512]{2,1,0:T(2,128)S(1)} async-done(((f32[32,2,512]{2,1,0:T(2,128)}), f32[32,2,512]{2,1,0:T(2,128)S(1)}, u32[]{:S(2)}, u32[]{:S(2)}) %all-to-all-start) | async-done | bytes 131104 | tf_op jit(solution)/shard_map/all_to_all | solution.py:139
  21.7 0.1 all_to_all.16
  21.8 0.7 %gather_fusion = f32[64,512]{1,0:T(8,128)S(1)} fusion(f32[64,512]{1,0:T(8,128)S(1)} %all_to_all.16, s32[1024]{0:T(1024)S(1)} %pad_clamp_fusion), kind=kCustom, calls=%fused_computation | custom fusion | bytes 262400 | tf_op jit(solution)/shard_map/gather | solution.py:112
  22.4 0.0 copy-done
  22.4 0.0 copy-done.2
  22.4 0.2 maximum_reduce_fusion
  22.7 0.1 fusion.25
  22.8 0.1 copy.35
  22.9 0.3 select_reduce_fusion
  23.2 0.6 fusion.14
  23.7 8.1 %fusion.9 = f32[64,5,256]{2,1,0:T(8,128)S(1)} fusion(bf16[64,512,256]{2,1,0:T(8,128)(2,1)} %param.8, bf16[64,4,512]{2,1,0:T(4,128)(2,1)S(1)} %get-tuple-element.13, bf16[64,1,512]{2,1,0:T(2,128)(2,1)S(1)} %copy.35), kind=kOutput, calls=%fused_computation.11 | convolution fusion | flops 84541440 | bytes 17432576 | tf_op jit(solution)/shard_map/rkb,rbc->rkc/dot_general | solution.py:62
  31.8 0.1 slice.55
  31.9 0.2 fusion.31
  32.1 0.1 convert_convert_fusion
  32.2 0.1 multiply_add_fusion
  32.3 0.1 select_maximum_fusion
  32.4 0.2 fusion.17
  32.6 0.7 %pad_maximum_fusion = f32[64,5,128]{2,1,0:T(8,128)} fusion(f32[64,1,128]{2,1,0:T(1,128)S(1)} %bitcast.37, f32[64,4,128]{2,1,0:T(4,128)S(1)} %fusion.17), kind=kLoop, calls=%fused_computation.19 | loop fusion | flops 40960 | bytes 327680 | tf_op jit(solution)/shard_map/concatenate | solution.py:148
  33.3 5.3 %all-to-all-start.1 = ((f32[64,5,128]{2,1,0:T(8,128)}), f32[64,5,128]{2,1,0:T(8,128)S(1)}, u32[]{:S(2)}, u32[]{:S(2)}) async-start(f32[64,5,128]{2,1,0:T(8,128)} %pad_maximum_fusion), calls=%async_computation.1 | async-start | bytes 524288 | tf_op jit(solution)/shard_map/all_to_all | solution.py:149
  38.7 2.9 %copy.40 = bf16[2048,512]{1,0:T(8,128)(2,1)S(1)} copy(bf16[2048,512]{0,1:T(8,128)(2,1)} %bitcast.27) | data formatting | bytes 4194304 | tf_op jit(solution)/shard_map/dot_general | solution.py:159
  41.6 6.1 %all-to-all-done.1 = f32[64,5,128]{2,1,0:T(8,128)S(1)} async-done(((f32[64,5,128]{2,1,0:T(8,128)}), f32[64,5,128]{2,1,0:T(8,128)S(1)}, u32[]{:S(2)}, u32[]{:S(2)}) %all-to-all-start.1) | async-done | bytes 163872 | tf_op jit(solution)/shard_map/all_to_all | solution.py:149
  47.6 0.1 fusion.51
  47.8 0.1 multiply_reduce_fusion
  47.9 0.1 fusion.16
  48.0 0.1 divide_convert_fusion.1
  48.1 0.6 %convolution_bitcast_fusion = f32[4,2,512]{2,1,0:T(2,128)S(1)} fusion(bf16[2,512,1]{1,0,2:T(2,128)(2,1)S(1)} %reshape.114, bf16[4,512,512]{2,1,0:T(8,128)(2,1)S(1)} %bitcast.26), kind=kOutput, calls=%fused_computation.9 | convolution fusion | flops 4194304 | bytes 2115584 | tf_op jit(solution)/shard_map/dot_general | solution.py:159
  48.7 9.5 %all_to_all.22 = f32[4,2,512]{2,1,0:T(2,128)S(1)} all-to-all(f32[4,2,512]{2,1,0:T(2,128)S(1)} %convolution_bitcast_fusion), channel_id=1, replica_groups=mesh['kv'=32,'hd'=4] {'hd'}, dimensions={0} | all-to-all | bytes 32768 | tf_op jit(solution)/shard_map/all_to_all | solution.py:162
  58.2 0.6 %reduce_sum.63 = bf16[2,512]{1,0:T(2,128)(2,1)} reduce(f32[4,2,512]{2,1,0:T(2,128)S(1)} %all_to_all.22, f32[]{:T(128)} %constant.78.clone.1), dimensions={0}, to_apply=%region_7.8 | reduce | flops 3072 | bytes 18436 | tf_op jit(solution)/shard_map/reduce_sum | solution.py:163
  (15 shorter events, 0.2 us)
Async XLA Ops:
  0.0 13.8 %copy-start.3 = (s32[64]{0:T(128)S(1)}, s32[64]{0:T(128)}, u32[]{:S(2)}) copy-start(s32[64]{0:T(128)} %param.13) | copy-start | bytes 772
  0.0 13.8 %copy-start.1 = (bf16[64,512]{1,0:T(8,128)(2,1)S(1)}, bf16[64,512]{1,0:T(8,128)(2,1)}, u32[]{:S(2)}) copy-start(bf16[64,512]{1,0:T(8,128)(2,1)} %param.14) | copy-start | bytes 196612
  5.4 16.3 %all-to-all-start = ((f32[32,2,512]{2,1,0:T(2,128)}), f32[32,2,512]{2,1,0:T(2,128)S(1)}, u32[]{:S(2)}, u32[]{:S(2)}) async-start(f32[32,2,512]{2,1,0:T(2,128)} %all_to_all.14), calls=%async_computation | async-start | bytes 262144 | tf_op jit(solution)/shard_map/all_to_all | solution.py:139
  13.9 8.6 %copy-start = (f32[64,512]{1,0:T(8,128)S(1)}, f32[64,512]{1,0:T(8,128)}, u32[]{:S(2)}) copy-start(f32[64,512]{1,0:T(8,128)} %param.11) | copy-start | bytes 393220
  13.9 8.5 %copy-start.2 = (s32[64]{0:T(128)S(1)}, s32[64]{0:T(128)}, u32[]{:S(2)}) copy-start(s32[64]{0:T(128)} %param.12) | copy-start | bytes 772
  33.3 14.3 %all-to-all-start.1 = ((f32[64,5,128]{2,1,0:T(8,128)}), f32[64,5,128]{2,1,0:T(8,128)S(1)}, u32[]{:S(2)}, u32[]{:S(2)}) async-start(f32[64,5,128]{2,1,0:T(8,128)} %pad_maximum_fusion), calls=%async_computation.1 | async-start | bytes 524288 | tf_op jit(solution)/shard_map/all_to_all | solution.py:149

commit v9 on v8

--- a/solution.py
+++ b/solution.py
@@ -109,9 +109,11 @@
 def unpack_slots(received, values, offsets, position, device, devices, capacity):
     source = (device - offsets) % devices
     slots = source * capacity + jnp.minimum(position, capacity - 1)
-    taken = received[slots]
-    moving = (offsets != 0)[:, None]
-    return jnp.where(moving, taken, values)
+    moving = offsets != 0
+    flat = received.reshape(devices * capacity, -1)
+    picks = (slots[:, None] == jnp.arange(devices * capacity, dtype=jnp.int32)[None, :]) & moving[:, None]
+    taken = jnp.dot(picks.astype(values.dtype), flat, precision=lax.Precision.HIGHEST)
+    return taken + jnp.where(moving[:, None], jnp.zeros((), values.dtype), values)
 
 
 def join_partials(first, second):

time: 59.3 us -> 58.7 us (0.990)
  local copies, waits for them, and re-layouts: 5.1 us -> 4.45 us
    gather x1 -> x0, local copies, waits for them, and re-layouts: 0.65 us -> none  [unpack_slots(): taken = received[slots]]
where the time goes in v9:
time: 58.7 us; the launch traced here: 58.3 us
  matrix products  17.1 us (29%)
  starting transfers between devices  13.7 us (23%)
  blocking collectives  9.46 us (16%)
  waiting for transfers between devices  8.15 us (14%)
  other arithmetic  5.13 us (9%)
  local copies, waits for them, and re-layouts  4.45 us (8%)
    all_to_all x1, blocking collectives, body(): lax.all_to_all(pieces, 'hd', split_axis=0, concat_axis=0, tiled=True)  9.46 us
    all_to_all x1, starting transfers between devices, body(): lax.all_to_all(outgoing, 'kv', split_axis=0, concat_axis=0, tiled=True)  8.42 us
    dot_general x1, matrix products, block_partial(): jnp.einsum('rkb,rbc->rkc', rows, block_data, preferred_element_type=jnp.f...  8.06 us
    all_to_all x1, waiting for transfers between devices, body(): lax.all_to_all(payload, 'kv', split_axis=0, concat_axis=0, tiled=True)  6.06 us
    dot_general x1, matrix products, raw_scores(): jnp.einsum('rhc,rbc->rhb', queries_h, block_data[..., :head_dim], preferr...  5.68 us
    all_to_all x1, starting transfers between devices, body(): lax.all_to_all(payload, 'kv', split_axis=0, concat_axis=0, tiled=True)  5.32 us
    dot_general x1, local copies, waits for them, and re-layouts, body(): jnp.dot(attended, out_weight, preferred_element_type=jnp.float32)  2.87 us
    all_to_all x1, waiting for transfers between devices, body(): lax.all_to_all(outgoing, 'kv', split_axis=0, concat_axis=0, tiled=True)  2.09 us
  transfers between devices with their start and end apart: 2, of which 2 were waited for; matrix products, arithmetic and copies ran while one was open for 15% of the time, Pallas kernels for 0%

profile of v9, /device:TPU:0, one launch (start us, length us, event | category | flops | bytes accessed | tf_op | source)
XLA Modules:
  0.0 58.3 jit_solution(2262463231806222334)
XLA Ops:
  0.0 0.0 copy-start.2
  0.0 0.0 copy-start.1
  0.0 0.9 %convert_reduce_fusion = s32[64]{0:T(128)S(1)} fusion(s32[64]{0:T(128)} %param.13), kind=kLoop, calls=%fused_computation.50 | loop fusion | flops 20416 | bytes 512 | tf_op jit(solution)/shard_map/reduce_sum | solution.py:89
  1.0 1.0 %shift-right-arithmetic_select_fusion = (s32[64,512]{1,0:T(8,128)S(1)}, s32[64,512]{1,0:T(8,128)S(1)}) fusion(s32[64,512]{1,0:T(8,128)} %param.9, s32[64]{0:T(128)} %bitcast.39), kind=kLoop, calls=%fused_computation.28 | loop fusion | flops 131072 | bytes 393472 | tf_op jit(solution)/shard_map/jit(_where)/select_n | solution.py:22
  2.0 1.1 %fusion.4 = pred[64,16,32]{2,1,0:T(8,128)(4,1)S(1)} fusion(s32[64,512]{1,0:T(8,128)S(1)} %get-tuple-element.16, s32[64,512]{1,0:T(8,128)S(1)} %get-tuple-element.15), kind=kOutput, calls=%fused_computation.6 | convolution fusion | flops 35160064 | bytes 294912 | tf_op jit(solution)/shard_map/rpa,rpb->rab/dot_general | solution.py:27
  3.0 0.3 copy.34
  3.3 0.1 copy.35
  3.5 1.2 %fusion.18 = f32[64,512]{1,0:T(8,128)S(1)} fusion(f32[64,512]{1,0:T(8,128)} %param.11, pred[64,512]{1,0:T(32,128)(4,1)S(1)} %copy.35, s32[512]{0:T(512)S(1)} %iota_add_fusion, s32[64]{0:T(128)} %param.12, s32[64]{0:T(128)} %param.13, s32[64]{0:T(128)S(1)} %and_select_fusion.1, pred[64]{0:T(512)(128)(4,1)S(1)} %broadcast_compare_fusion.3, ...), kind=kOutput, calls=%fused_computation.31 | convolution fusion | flops 25313280 | bytes 297920 | tf_op jit(solution)/shard_map/dot_general | solution.py:106
  4.7 0.7 %all_to_all.14 = f32[32,2,512]{2,1,0:T(2,128)} reshape(f32[64,512]{1,0:T(8,128)S(1)} %fusion.18) | data formatting | bytes 262144 | tf_op jit(solution)/shard_map/all_to_all | solution.py:141
  5.4 8.4 %all-to-all-start = ((f32[32,2,512]{2,1,0:T(2,128)}), f32[32,2,512]{2,1,0:T(2,128)S(1)}, u32[]{:S(2)}, u32[]{:S(2)}) async-start(f32[32,2,512]{2,1,0:T(2,128)} %all_to_all.14), calls=%async_computation | async-start | bytes 262144 | tf_op jit(solution)/shard_map/all_to_all | solution.py:141
  13.8 0.0 copy-done.2
  13.8 0.0 copy-done.1
  13.9 0.0 copy-start
  13.9 0.0 copy-start.3
  13.9 5.7 %fusion.5 = f32[64,4,512]{2,1,0:T(4,128)S(1)} fusion(bf16[64,4,128]{2,1,0:T(4,128)(2,1)S(1)} %reshape.102, bf16[64,512,256]{2,1,0:T(8,128)(2,1)} %param.8), kind=kOutput, calls=%fused_computation.7 | convolution fusion | flops 33685504 | bytes 8978432 | tf_op jit(solution)/shard_map/rhc,rbc->rhb/dot_general | solution.py:37
  19.6 2.1 %all-to-all-done = f32[32,2,512]{2,1,0:T(2,128)S(1)} async-done(((f32[32,2,512]{2,1,0:T(2,128)}), f32[32,2,512]{2,1,0:T(2,128)S(1)}, u32[]{:S(2)}, u32[]{:S(2)}) %all-to-all-start) | async-done | bytes 131104 | tf_op jit(solution)/shard_map/all_to_all | solution.py:141
  21.7 0.1 all_to_all.16
  21.8 0.0 copy-done
  21.8 0.0 copy-done.3
  21.8 0.3 broadcast_compare_fusion
  22.1 0.1 maximum_reduce_fusion
  22.2 0.1 fusion.24
  22.3 0.1 copy.36
  22.4 0.3 select_reduce_fusion
  22.7 0.6 fusion.14
  23.2 8.1 %fusion.9 = f32[64,5,256]{2,1,0:T(8,128)S(1)} fusion(bf16[64,512,256]{2,1,0:T(8,128)(2,1)} %param.8, bf16[64,4,512]{2,1,0:T(4,128)(2,1)S(1)} %get-tuple-element.11, bf16[64,1,512]{2,1,0:T(2,128)(2,1)S(1)} %copy.36), kind=kOutput, calls=%fused_computation.11 | convolution fusion | flops 84541440 | bytes 17432576 | tf_op jit(solution)/shard_map/rkb,rbc->rkc/dot_general | solution.py:62
  31.3 0.1 slice.53
  31.4 0.2 fusion.32
  31.6 0.1 convert_convert_fusion
  31.7 0.1 multiply_add_fusion
  31.8 0.1 select_maximum_fusion
  31.9 0.2 fusion.17
  32.1 0.7 %pad_maximum_fusion = f32[64,5,128]{2,1,0:T(8,128)} fusion(f32[64,1,128]{2,1,0:T(1,128)S(1)} %bitcast.38, f32[64,4,128]{2,1,0:T(4,128)S(1)} %fusion.17), kind=kLoop, calls=%fused_computation.19 | loop fusion | flops 40960 | bytes 327680 | tf_op jit(solution)/shard_map/concatenate | solution.py:150
  32.8 5.3 %all-to-all-start.1 = ((f32[64,5,128]{2,1,0:T(8,128)}), f32[64,5,128]{2,1,0:T(8,128)S(1)}, u32[]{:S(2)}, u32[]{:S(2)}) async-start(f32[64,5,128]{2,1,0:T(8,128)} %pad_maximum_fusion), calls=%async_computation.1 | async-start | bytes 524288 | tf_op jit(solution)/shard_map/all_to_all | solution.py:151
  38.2 2.9 %copy.41 = bf16[2048,512]{1,0:T(8,128)(2,1)S(1)} copy(bf16[2048,512]{0,1:T(8,128)(2,1)} %bitcast.28) | data formatting | bytes 4194304 | tf_op jit(solution)/shard_map/dot_general | solution.py:161
  41.0 6.1 %all-to-all-done.1 = f32[64,5,128]{2,1,0:T(8,128)S(1)} async-done(((f32[64,5,128]{2,1,0:T(8,128)}), f32[64,5,128]{2,1,0:T(8,128)S(1)}, u32[]{:S(2)}, u32[]{:S(2)}) %all-to-all-start.1) | async-done | bytes 163872 | tf_op jit(solution)/shard_map/all_to_all | solution.py:151
  47.1 0.1 fusion.53
  47.3 0.1 multiply_reduce_fusion
  47.3 0.1 fusion.16
  47.5 0.1 divide_convert_fusion.1
  47.6 0.6 %convolution_bitcast_fusion = f32[4,2,512]{2,1,0:T(2,128)S(1)} fusion(bf16[2,512,1]{1,0,2:T(2,128)(2,1)S(1)} %reshape.106, bf16[4,512,512]{2,1,0:T(8,128)(2,1)S(1)} %bitcast.27), kind=kOutput, calls=%fused_computation.9 | convolution fusion | flops 4194304 | bytes 2115584 | tf_op jit(solution)/shard_map/dot_general | solution.py:161
  48.2 9.5 %all_to_all.22 = f32[4,2,512]{2,1,0:T(2,128)S(1)} all-to-all(f32[4,2,512]{2,1,0:T(2,128)S(1)} %convolution_bitcast_fusion), channel_id=1, replica_groups=mesh['kv'=32,'hd'=4] {'hd'}, dimensions={0} | all-to-all | bytes 32768 | tf_op jit(solution)/shard_map/all_to_all | solution.py:164
  57.7 0.6 %reduce_sum.63 = bf16[2,512]{1,0:T(2,128)(2,1)} reduce(f32[4,2,512]{2,1,0:T(2,128)S(1)} %all_to_all.22, f32[]{:T(128)} %constant.77.clone.1), dimensions={0}, to_apply=%region_7.8 | reduce | flops 3072 | bytes 18436 | tf_op jit(solution)/shard_map/reduce_sum | solution.py:165
  (13 shorter events, 0.2 us)
Async XLA Ops:
  0.0 13.8 %copy-start.2 = (s32[64]{0:T(128)S(1)}, s32[64]{0:T(128)}, u32[]{:S(2)}) copy-start(s32[64]{0:T(128)} %param.13) | copy-start | bytes 772
  0.0 13.8 %copy-start.1 = (bf16[64,512]{1,0:T(8,128)(2,1)S(1)}, bf16[64,512]{1,0:T(8,128)(2,1)}, u32[]{:S(2)}) copy-start(bf16[64,512]{1,0:T(8,128)(2,1)} %param.14) | copy-start | bytes 196612
  5.4 16.3 %all-to-all-start = ((f32[32,2,512]{2,1,0:T(2,128)}), f32[32,2,512]{2,1,0:T(2,128)S(1)}, u32[]{:S(2)}, u32[]{:S(2)}) async-start(f32[32,2,512]{2,1,0:T(2,128)} %all_to_all.14), calls=%async_computation | async-start | bytes 262144 | tf_op jit(solution)/shard_map/all_to_all | solution.py:141
  13.9 7.9 %copy-start = (f32[64,512]{1,0:T(8,128)S(1)}, f32[64,512]{1,0:T(8,128)}, u32[]{:S(2)}) copy-start(f32[64,512]{1,0:T(8,128)} %param.11) | copy-start | bytes 393220
  13.9 7.9 %copy-start.3 = (s32[64]{0:T(128)S(1)}, s32[64]{0:T(128)}, u32[]{:S(2)}) copy-start(s32[64]{0:T(128)} %param.12) | copy-start | bytes 772
  32.8 14.3 %all-to-all-start.1 = ((f32[64,5,128]{2,1,0:T(8,128)}), f32[64,5,128]{2,1,0:T(8,128)S(1)}, u32[]{:S(2)}, u32[]{:S(2)}) async-start(f32[64,5,128]{2,1,0:T(8,128)} %pad_maximum_fusion), calls=%async_computation.1 | async-start | bytes 524288 | tf_op jit(solution)/shard_map/all_to_all | solution.py:151

commit v10 on v9

--- a/solution.py
+++ b/solution.py
@@ -52,6 +52,7 @@
     has_merged = totals > 0.0
     floored = jnp.maximum(totals, 1.0)
     shares = (weight / floored[:, None]).astype(jnp.bfloat16)
+    raw_qk = scores_qk
     scores_qk = jnp.where(kept_rows[:, None, :], scores_qk, -1e30)
     kept_peaks = jnp.max(scores_qk, axis=-1)
     kept_probs = jnp.where(
@@ -59,22 +60,18 @@
     )
     kept_mass = jnp.sum(kept_probs, axis=-1)
     rows = jnp.concatenate([shares[:, None, :], kept_probs.astype(jnp.bfloat16)], axis=1)
-    products = jnp.einsum("rkb,rbc->rkc", rows, block_data, preferred_element_type=jnp.float32)
-    merged = products[:, 0, :].astype(jnp.bfloat16)
-    kept_weighted = products[:, 1:, head_dim:]
-    merged_score = (
-        jnp.einsum(
-            "rhc,rc->rh", queries_h, merged[:, :head_dim], preferred_element_type=jnp.float32
-        )
-        * factor
+    products = jnp.einsum(
+        "rkb,rbc->rkc", rows, block_data[..., head_dim:], preferred_element_type=jnp.float32
     )
+    merged_value = products[:, 0, :].astype(jnp.bfloat16).astype(jnp.float32)
+    kept_weighted = products[:, 1:, :]
+    merged_score = jnp.sum(shares.astype(jnp.float32)[:, None, :] * raw_qk, axis=-1)
     merged_score = merged_score + jnp.log(floored)[:, None]
     merged_score = jnp.where(has_merged[:, None], merged_score, -1e30)
     peaks = jnp.maximum(kept_peaks, merged_score)
     rescale = jnp.exp(kept_peaks - peaks)
     merged_prob = jnp.where(has_merged[:, None], jnp.exp(merged_score - peaks), 0.0)
     mass = kept_mass * rescale + merged_prob
-    merged_value = merged[:, head_dim:].astype(jnp.float32)
     weighted = (
         kept_weighted * rescale[..., None]
         + merged_prob.astype(jnp.bfloat16).astype(jnp.float32)[..., None] * merged_value[:, None, :]

time: 58.7 us -> 56.6 us (0.964)
  matrix products: 17.1 us -> 13.5 us
  starting transfers between devices: 13.7 us -> 15.2 us
  waiting for transfers between devices: 8.15 us -> 6.72 us
  local copies, waits for them, and re-layouts: 4.45 us -> 5.22 us
  other arithmetic: 5.13 us -> 5.89 us
    dot_general x2 -> x1, matrix products: 8.26 us -> 4.58 us  [block_partial(): jnp.einsum('rkb,rbc->rkc', rows, block_data[..., head_dim:], preferred_el...]
    all_to_all x1, waiting for transfers between devices: 2.09 us -> 0.66 us  [body(): lax.all_to_all(outgoing, 'kv', split_axis=0, concat_axis=0, tiled=True)]
    all_to_all x1, starting transfers between devices: 5.32 us -> 6.74 us  [body(): lax.all_to_all(payload, 'kv', split_axis=0, concat_axis=0, tiled=True)]
    reshape x1, local copies, waits for them, and re-layouts: 0.02 us -> 0.86 us  [body(): queries_h = queries.reshape(requests, -1, head_dim)]
    add x1, other arithmetic: 0.01 us -> 0.67 us  [unpack_slots(): slots = source * capacity + jnp.minimum(position, capacity - 1)]
  transfers between devices with their start and end apart: 2 -> 2, of which waited for: 2 -> 2; matrix products, arithmetic and copies ran while one was open for 15% -> 18% of each run, Pallas kernels for 0% -> 0%
where the time goes in v10:
time: 56.6 us; the launch traced here: 56.1 us
  starting transfers between devices  15.2 us (27%)
  matrix products  13.5 us (24%)
  blocking collectives  9.46 us (17%)
  waiting for transfers between devices  6.72 us (12%)
  other arithmetic  5.89 us (10%)
  local copies, waits for them, and re-layouts  5.22 us (9%)
    all_to_all x1, blocking collectives, body(): lax.all_to_all(pieces, 'hd', split_axis=0, concat_axis=0, tiled=True)  9.46 us
    all_to_all x1, starting transfers between devices, body(): lax.all_to_all(outgoing, 'kv', split_axis=0, concat_axis=0, tiled=True)  8.42 us
    all_to_all x1, starting transfers between devices, body(): lax.all_to_all(payload, 'kv', split_axis=0, concat_axis=0, tiled=True)  6.74 us
    all_to_all x1, waiting for transfers between devices, body(): lax.all_to_all(payload, 'kv', split_axis=0, concat_axis=0, tiled=True)  6.06 us
    dot_general x1, matrix products, raw_scores(): jnp.einsum('rhc,rbc->rhb', queries_h, block_data[..., :head_dim], preferr...  5.65 us
    dot_general x1, matrix products, block_partial(): jnp.einsum('rkb,rbc->rkc', rows, block_data[..., head_dim:], preferred_el...  4.58 us
    dot_general x1, local copies, waits for them, and re-layouts, body(): jnp.dot(attended, out_weight, preferred_element_type=jnp.float32)  2.87 us
    dot_general x1, matrix products, pack_slots(): jnp.dot(match.astype(values.dtype), values, precision=lax.Precision.HIGHEST)  1.21 us
  transfers between devices with their start and end apart: 2, of which 2 were waited for; matrix products, arithmetic and copies ran while one was open for 18% of the time, Pallas kernels for 0%

profile of v10, /device:TPU:0, one launch (start us, length us, event | category | flops | bytes accessed | tf_op | source)
XLA Modules:
  0.0 56.1 jit_solution(9940515241792712963)
XLA Ops:
  0.0 0.0 copy-start.2
  0.0 0.0 copy-start.1
  0.0 0.0 copy-start
  0.0 0.9 %convert_reduce_fusion = s32[64]{0:T(128)S(1)} fusion(s32[64]{0:T(128)} %param.13), kind=kLoop, calls=%fused_computation.51 | loop fusion | flops 20416 | bytes 512 | tf_op jit(solution)/shard_map/reduce_sum | solution.py:86
  1.0 1.0 %shift-right-arithmetic_select_fusion = (s32[64,512]{1,0:T(8,128)S(1)}, s32[64,512]{1,0:T(8,128)S(1)}) fusion(s32[64,512]{1,0:T(8,128)} %param.9, s32[64]{0:T(128)} %bitcast.29), kind=kLoop, calls=%fused_computation.30 | loop fusion | flops 131072 | bytes 393472 | tf_op jit(solution)/shard_map/jit(_where)/select_n | solution.py:22
  2.0 1.1 %fusion.6 = pred[64,16,32]{2,1,0:T(8,128)(4,1)S(1)} fusion(s32[64,512]{1,0:T(8,128)S(1)} %get-tuple-element.19, s32[64,512]{1,0:T(8,128)S(1)} %get-tuple-element.18), kind=kOutput, calls=%fused_computation.8 | convolution fusion | flops 35160064 | bytes 294912 | tf_op jit(solution)/shard_map/rpa,rpb->rab/dot_general | solution.py:27
  3.1 0.3 copy.34
  3.4 0.1 copy.35
  3.5 1.2 %fusion.19 = f32[64,512]{1,0:T(8,128)S(1)} fusion(f32[64,512]{1,0:T(8,128)} %param.11, pred[64,512]{1,0:T(32,128)(4,1)S(1)} %copy.35, s32[512]{0:T(512)S(1)} %iota_add_fusion, s32[64]{0:T(128)} %param.12, s32[64]{0:T(128)} %param.13, s32[64]{0:T(128)S(1)} %and_select_fusion.1, pred[64]{0:T(512)(128)(4,1)S(1)} %broadcast_compare_fusion.3, ...), kind=kOutput, calls=%fused_computation.33 | convolution fusion | flops 25313280 | bytes 297920 | tf_op jit(solution)/shard_map/dot_general | solution.py:103
  4.7 0.7 %all_to_all.14 = f32[32,2,512]{2,1,0:T(2,128)} reshape(f32[64,512]{1,0:T(8,128)S(1)} %fusion.19) | data formatting | bytes 262144 | tf_op jit(solution)/shard_map/all_to_all | solution.py:138
  5.4 8.4 %all-to-all-start = ((f32[32,2,512]{2,1,0:T(2,128)}), f32[32,2,512]{2,1,0:T(2,128)S(1)}, u32[]{:S(2)}, u32[]{:S(2)}) async-start(f32[32,2,512]{2,1,0:T(2,128)} %all_to_all.14), calls=%async_computation | async-start | bytes 262144 | tf_op jit(solution)/shard_map/all_to_all | solution.py:138
  13.9 0.7 %fusion.44 = s32[64]{0:T(128)S(1)} fusion(s32[64]{0:T(128)S(1)} %convert_reduce_fusion, s32[64]{0:T(128)} %param.13, s32[]{:T(128)S(6)} %axis_index.15), kind=kLoop, calls=%fused_computation.84 | loop fusion | flops 960 | bytes 772 | tf_op jit(solution)/shard_map/add | solution.py:108
  14.5 0.9 %reshape.187 = bf16[64,4,128]{2,1,0:T(4,128)(2,1)S(1)} reshape(bf16[64,512]{1,0:T(8,128)(2,1)} %param.14) | data formatting | bytes 131072 | tf_op jit(solution)/shard_map/reshape | solution.py:141
  15.4 5.6 %fusion.7 = f32[64,4,512]{2,1,0:T(4,128)S(1)} fusion(bf16[64,4,128]{2,1,0:T(4,128)(2,1)S(1)} %reshape.187, bf16[64,512,256]{2,1,0:T(8,128)(2,1)} %param.8), kind=kOutput, calls=%fused_computation.9 | convolution fusion | flops 33685504 | bytes 8978432 | tf_op jit(solution)/shard_map/rhc,rbc->rhb/dot_general | solution.py:37
  21.0 0.0 copy-done.2
  21.1 0.7 %all-to-all-done = f32[32,2,512]{2,1,0:T(2,128)S(1)} async-done(((f32[32,2,512]{2,1,0:T(2,128)}), f32[32,2,512]{2,1,0:T(2,128)S(1)}, u32[]{:S(2)}, u32[]{:S(2)}) %all-to-all-start) | async-done | bytes 131104 | tf_op jit(solution)/shard_map/all_to_all | solution.py:138
  21.7 0.1 all_to_all.16
  21.8 0.0 copy-done.1
  21.8 0.0 copy-done
  21.8 0.4 maximum_reduce_fusion
  22.2 0.1 fusion.52
  22.3 0.1 copy.36
  22.4 0.3 select_reduce_fusion
  22.7 0.7 %multiply_reduce_fusion = (f32[64,4]{1,0:T(8,128)S(1)}, f32[64,4]{1,0:T(8,128)S(1)}, bf16[64,4,512]{2,1,0:T(4,128)(2,1)S(1)}) fusion(f32[64,4,512]{2,1,0:T(4,128)S(1)} %fusion.7, f32[64,512]{1,0:T(8,128)S(1)} %get-tuple-element.13, f32[64,4]{1,0:T(8,128)S(1)} %select_reduce_fusion, pred[64,512]{1,0:T(8,128)(4,1)S(1)} %broadcast_compare_fusion), kind=kLoop, calls=%fused_computation.16 | loop fusion | flops 916992 | bytes 953344 | tf_op jit(solution)/shard_map/reduce_sum | solution.py:68
  23.4 0.1 convert_convert_fusion
  23.5 0.1 multiply_add_fusion
  23.6 0.1 select_maximum_fusion
  23.7 4.6 %fusion = f32[64,5,128]{2,1,0:T(8,128)S(1)} fusion(bf16[64,512,256]{2,1,0:T(8,128)(2,1)} %param.8, bf16[64,4,512]{2,1,0:T(4,128)(2,1)S(1)} %get-tuple-element.15, bf16[64,1,512]{2,1,0:T(2,128)(2,1)S(1)} %copy.36), kind=kOutput, calls=%fused_computation | convolution fusion | flops 42598400 | bytes 8880128 | tf_op jit(solution)/shard_map/rkb,rbc->rkc/dot_general | solution.py:63
  28.3 0.2 fusion.18
  28.5 0.8 %pad_maximum_fusion = f32[64,5,128]{2,1,0:T(8,128)} fusion(f32[64,1,128]{2,1,0:T(1,128)S(1)} %bitcast.27, f32[64,4,128]{2,1,0:T(4,128)S(1)} %fusion.18), kind=kLoop, calls=%fused_computation.21 | loop fusion | flops 40960 | bytes 327680 | tf_op jit(solution)/shard_map/concatenate | solution.py:147
  29.2 6.7 %all-to-all-start.1 = ((f32[64,5,128]{2,1,0:T(8,128)}), f32[64,5,128]{2,1,0:T(8,128)S(1)}, u32[]{:S(2)}, u32[]{:S(2)}) async-start(f32[64,5,128]{2,1,0:T(8,128)} %pad_maximum_fusion), calls=%async_computation.1 | async-start | bytes 524288 | tf_op jit(solution)/shard_map/all_to_all | solution.py:148
  36.0 2.9 %copy.39 = bf16[2048,512]{1,0:T(8,128)(2,1)S(1)} copy(bf16[2048,512]{0,1:T(8,128)(2,1)} %bitcast.19) | data formatting | bytes 4194304 | tf_op jit(solution)/shard_map/dot_general | solution.py:158
  38.9 6.1 %all-to-all-done.1 = f32[64,5,128]{2,1,0:T(8,128)S(1)} async-done(((f32[64,5,128]{2,1,0:T(8,128)}), f32[64,5,128]{2,1,0:T(8,128)S(1)}, u32[]{:S(2)}, u32[]{:S(2)}) %all-to-all-start.1) | async-done | bytes 163872 | tf_op jit(solution)/shard_map/all_to_all | solution.py:148
  44.9 0.1 fusion.53
  45.1 0.1 multiply_reduce_fusion.1
  45.2 0.1 fusion.17
  45.3 0.1 divide_convert_fusion.1
  45.4 0.6 %convolution_bitcast_fusion = f32[4,2,512]{2,1,0:T(2,128)S(1)} fusion(bf16[2,512,1]{1,0,2:T(2,128)(2,1)S(1)} %reshape.190, bf16[4,512,512]{2,1,0:T(8,128)(2,1)S(1)} %bitcast.18), kind=kOutput, calls=%fused_computation.11 | convolution fusion | flops 4194304 | bytes 2115584 | tf_op jit(solution)/shard_map/dot_general | solution.py:158
  46.0 9.5 %all_to_all.22 = f32[4,2,512]{2,1,0:T(2,128)S(1)} all-to-all(f32[4,2,512]{2,1,0:T(2,128)S(1)} %convolution_bitcast_fusion), channel_id=1, replica_groups=mesh['kv'=32,'hd'=4] {'hd'}, dimensions={0} | all-to-all | bytes 32768 | tf_op jit(solution)/shard_map/all_to_all | solution.py:161
  55.5 0.6 %reduce_sum.73 = bf16[2,512]{1,0:T(2,128)(2,1)} reduce(f32[4,2,512]{2,1,0:T(2,128)S(1)} %all_to_all.22, f32[]{:T(128)} %constant.76.clone.1), dimensions={0}, to_apply=%region_8.9 | reduce | flops 3072 | bytes 18436 | tf_op jit(solution)/shard_map/reduce_sum | solution.py:162
  (11 shorter events, 0.2 us)
Async XLA Ops:
  0.0 21.0 %copy-start.2 = (s32[64]{0:T(128)S(1)}, s32[64]{0:T(128)}, u32[]{:S(2)}) copy-start(s32[64]{0:T(128)} %param.13) | copy-start | bytes 772
  0.0 21.8 %copy-start.1 = (s32[64]{0:T(128)S(1)}, s32[64]{0:T(128)}, u32[]{:S(2)}) copy-start(s32[64]{0:T(128)} %param.12) | copy-start | bytes 772
  0.0 21.8 %copy-start = (f32[64,512]{1,0:T(8,128)S(1)}, f32[64,512]{1,0:T(8,128)}, u32[]{:S(2)}) copy-start(f32[64,512]{1,0:T(8,128)} %param.11) | copy-start | bytes 393220
  5.4 16.3 %all-to-all-start = ((f32[32,2,512]{2,1,0:T(2,128)}), f32[32,2,512]{2,1,0:T(2,128)S(1)}, u32[]{:S(2)}, u32[]{:S(2)}) async-start(f32[32,2,512]{2,1,0:T(2,128)} %all_to_all.14), calls=%async_computation | async-start | bytes 262144 | tf_op jit(solution)/shard_map/all_to_all | solution.py:138
  29.2 15.7 %all-to-all-start.1 = ((f32[64,5,128]{2,1,0:T(8,128)}), f32[64,5,128]{2,1,0:T(8,128)S(1)}, u32[]{:S(2)}, u32[]{:S(2)}) async-start(f32[64,5,128]{2,1,0:T(8,128)} %pad_maximum_fusion), calls=%async_computation.1 | async-start | bytes 524288 | tf_op jit(solution)/shard_map/all_to_all | solution.py:148

commit v11 on v10

--- a/solution.py
+++ b/solution.py
@@ -45,35 +45,27 @@
 
 def block_partial(block_data, codes, queries_h, scores_qk):
     head_dim = queries_h.shape[-1]
-    factor = 1.0 / math.sqrt(head_dim)
     kept_rows = codes < 0.0
     weight = jnp.maximum(codes, 0.0)
     totals = jnp.sum(weight, axis=1)
     has_merged = totals > 0.0
     floored = jnp.maximum(totals, 1.0)
     shares = (weight / floored[:, None]).astype(jnp.bfloat16)
-    raw_qk = scores_qk
+    merged_score = jnp.sum(shares.astype(jnp.float32)[:, None, :] * scores_qk, axis=-1)
+    merged_score = merged_score + jnp.log(floored)[:, None]
+    merged_score = jnp.where(has_merged[:, None], merged_score, -1e30)
     scores_qk = jnp.where(kept_rows[:, None, :], scores_qk, -1e30)
-    kept_peaks = jnp.max(scores_qk, axis=-1)
-    kept_probs = jnp.where(
-        kept_rows[:, None, :], jnp.exp(scores_qk - kept_peaks[..., None]), 0.0
-    )
-    kept_mass = jnp.sum(kept_probs, axis=-1)
-    rows = jnp.concatenate([shares[:, None, :], kept_probs.astype(jnp.bfloat16)], axis=1)
+    peaks = jnp.maximum(jnp.max(scores_qk, axis=-1), merged_score)
+    probs = jnp.where(kept_rows[:, None, :], jnp.exp(scores_qk - peaks[..., None]), 0.0)
+    merged_prob = jnp.where(has_merged[:, None], jnp.exp(merged_score - peaks), 0.0)
+    mass = jnp.sum(probs, axis=-1) + merged_prob
+    rows = jnp.concatenate([shares[:, None, :], probs.astype(jnp.bfloat16)], axis=1)
     products = jnp.einsum(
         "rkb,rbc->rkc", rows, block_data[..., head_dim:], preferred_element_type=jnp.float32
     )
     merged_value = products[:, 0, :].astype(jnp.bfloat16).astype(jnp.float32)
-    kept_weighted = products[:, 1:, :]
-    merged_score = jnp.sum(shares.astype(jnp.float32)[:, None, :] * raw_qk, axis=-1)
-    merged_score = merged_score + jnp.log(floored)[:, None]
-    merged_score = jnp.where(has_merged[:, None], merged_score, -1e30)
-    peaks = jnp.maximum(kept_peaks, merged_score)
-    rescale = jnp.exp(kept_peaks - peaks)
-    merged_prob = jnp.where(has_merged[:, None], jnp.exp(merged_score - peaks), 0.0)
-    mass = kept_mass * rescale + merged_prob
     weighted = (
-        kept_weighted * rescale[..., None]
+        products[:, 1:, :]
         + merged_prob.astype(jnp.bfloat16).astype(jnp.float32)[..., None] * merged_value[:, None, :]
     )
     return (peaks, mass, weighted)

time: 56.6 us -> 56.6 us (level)
  no operation moved by 1% of the time
where the time goes in v11:
time: 56.6 us; the launch traced here: 56.1 us
  starting transfers between devices  15.2 us (27%)
  matrix products  13.5 us (24%)
  blocking collectives  9.46 us (17%)
  waiting for transfers between devices  6.72 us (12%)
  other arithmetic  5.86 us (10%)
  local copies, waits for them, and re-layouts  5.22 us (9%)
    all_to_all x1, blocking collectives, body(): lax.all_to_all(pieces, 'hd', split_axis=0, concat_axis=0, tiled=True)  9.46 us
    all_to_all x1, starting transfers between devices, body(): lax.all_to_all(outgoing, 'kv', split_axis=0, concat_axis=0, tiled=True)  8.42 us
    all_to_all x1, starting transfers between devices, body(): lax.all_to_all(payload, 'kv', split_axis=0, concat_axis=0, tiled=True)  6.74 us
    all_to_all x1, waiting for transfers between devices, body(): lax.all_to_all(payload, 'kv', split_axis=0, concat_axis=0, tiled=True)  6.06 us
    dot_general x1, matrix products, raw_scores(): jnp.einsum('rhc,rbc->rhb', queries_h, block_data[..., :head_dim], preferr...  5.65 us
    dot_general x1, matrix products, block_partial(): jnp.einsum('rkb,rbc->rkc', rows, block_data[..., head_dim:], preferred_el...  4.58 us
    dot_general x1, local copies, waits for them, and re-layouts, body(): jnp.dot(attended, out_weight, preferred_element_type=jnp.float32)  2.87 us
    dot_general x1, matrix products, pack_slots(): jnp.dot(match.astype(values.dtype), values, precision=lax.Precision.HIGHEST)  1.21 us
  transfers between devices with their start and end apart: 2, of which 2 were waited for; matrix products, arithmetic and copies ran while one was open for 18% of the time, Pallas kernels for 0%

profile of v11, /device:TPU:0, one launch (start us, length us, event | category | flops | bytes accessed | tf_op | source)
XLA Modules:
  0.0 56.1 jit_solution(1991669424034504178)
XLA Ops:
  0.0 0.0 copy-start.2
  0.0 0.0 copy-start.1
  0.0 0.0 copy-start
  0.0 0.9 %convert_reduce_fusion = s32[64]{0:T(128)S(1)} fusion(s32[64]{0:T(128)} %param.13), kind=kLoop, calls=%fused_computation.48 | loop fusion | flops 20416 | bytes 512 | tf_op jit(solution)/shard_map/reduce_sum | solution.py:78
  1.0 1.0 %shift-right-arithmetic_select_fusion = (s32[64,512]{1,0:T(8,128)S(1)}, s32[64,512]{1,0:T(8,128)S(1)}) fusion(s32[64,512]{1,0:T(8,128)} %param.9, s32[64]{0:T(128)} %bitcast.29), kind=kLoop, calls=%fused_computation.29 | loop fusion | flops 131072 | bytes 393472 | tf_op jit(solution)/shard_map/jit(_where)/select_n | solution.py:22
  2.0 1.1 %fusion.6 = pred[64,16,32]{2,1,0:T(8,128)(4,1)S(1)} fusion(s32[64,512]{1,0:T(8,128)S(1)} %get-tuple-element.16, s32[64,512]{1,0:T(8,128)S(1)} %get-tuple-element.15), kind=kOutput, calls=%fused_computation.8 | convolution fusion | flops 35160064 | bytes 294912 | tf_op jit(solution)/shard_map/rpa,rpb->rab/dot_general | solution.py:27
  3.1 0.3 copy.33
  3.4 0.1 copy.34
  3.5 1.2 %fusion.18 = f32[64,512]{1,0:T(8,128)S(1)} fusion(f32[64,512]{1,0:T(8,128)} %param.11, pred[64,512]{1,0:T(32,128)(4,1)S(1)} %copy.34, s32[512]{0:T(512)S(1)} %iota_add_fusion, s32[64]{0:T(128)} %param.12, s32[64]{0:T(128)} %param.13, s32[64]{0:T(128)S(1)} %and_select_fusion.1, pred[64]{0:T(512)(128)(4,1)S(1)} %broadcast_compare_fusion.3, ...), kind=kOutput, calls=%fused_computation.32 | convolution fusion | flops 25313280 | bytes 297920 | tf_op jit(solution)/shard_map/dot_general | solution.py:95
  4.7 0.7 %all_to_all.14 = f32[32,2,512]{2,1,0:T(2,128)} reshape(f32[64,512]{1,0:T(8,128)S(1)} %fusion.18) | data formatting | bytes 262144 | tf_op jit(solution)/shard_map/all_to_all | solution.py:130
  5.4 8.4 %all-to-all-start = ((f32[32,2,512]{2,1,0:T(2,128)}), f32[32,2,512]{2,1,0:T(2,128)S(1)}, u32[]{:S(2)}, u32[]{:S(2)}) async-start(f32[32,2,512]{2,1,0:T(2,128)} %all_to_all.14), calls=%async_computation | async-start | bytes 262144 | tf_op jit(solution)/shard_map/all_to_all | solution.py:130
  13.9 0.7 %fusion.43 = s32[64]{0:T(128)S(1)} fusion(s32[64]{0:T(128)S(1)} %convert_reduce_fusion, s32[64]{0:T(128)} %param.13, s32[]{:T(128)S(6)} %axis_index.15), kind=kLoop, calls=%fused_computation.81 | loop fusion | flops 960 | bytes 772 | tf_op jit(solution)/shard_map/add | solution.py:100
  14.5 0.9 %reshape.184 = bf16[64,4,128]{2,1,0:T(4,128)(2,1)S(1)} reshape(bf16[64,512]{1,0:T(8,128)(2,1)} %param.14) | data formatting | bytes 131072 | tf_op jit(solution)/shard_map/reshape | solution.py:133
  15.4 5.6 %fusion.7 = f32[64,4,512]{2,1,0:T(4,128)S(1)} fusion(bf16[64,4,128]{2,1,0:T(4,128)(2,1)S(1)} %reshape.184, bf16[64,512,256]{2,1,0:T(8,128)(2,1)} %param.8), kind=kOutput, calls=%fused_computation.9 | convolution fusion | flops 33685504 | bytes 8978432 | tf_op jit(solution)/shard_map/rhc,rbc->rhb/dot_general | solution.py:37
  21.0 0.0 copy-done.2
  21.1 0.7 %all-to-all-done = f32[32,2,512]{2,1,0:T(2,128)S(1)} async-done(((f32[32,2,512]{2,1,0:T(2,128)}), f32[32,2,512]{2,1,0:T(2,128)S(1)}, u32[]{:S(2)}, u32[]{:S(2)}) %all-to-all-start) | async-done | bytes 131104 | tf_op jit(solution)/shard_map/all_to_all | solution.py:130
  21.7 0.1 all_to_all.16
  21.8 0.0 copy-done.1
  21.8 0.0 copy-done
  21.8 0.4 maximum_reduce_fusion
  22.2 0.1 fusion.51
  22.3 0.1 copy.35
  22.4 0.5 multiply_reduce_fusion
  22.9 0.1 fusion.32
  23.0 0.6 fusion.15
  23.5 0.1 convert_convert_fusion
  23.6 0.1 select_maximum_fusion
  23.7 4.6 %fusion = f32[64,5,128]{2,1,0:T(8,128)S(1)} fusion(bf16[64,512,256]{2,1,0:T(8,128)(2,1)} %param.8, bf16[64,4,512]{2,1,0:T(4,128)(2,1)S(1)} %get-tuple-element.11, bf16[64,1,512]{2,1,0:T(2,128)(2,1)S(1)} %copy.35), kind=kOutput, calls=%fused_computation | convolution fusion | flops 42598400 | bytes 8880128 | tf_op jit(solution)/shard_map/rkb,rbc->rkc/dot_general | solution.py:63
  28.3 0.1 slice_add_fusion
  28.5 0.8 %pad_maximum_fusion = f32[64,5,128]{2,1,0:T(8,128)} fusion(f32[64,1,128]{2,1,0:T(1,128)S(1)} %bitcast.28, f32[64,4,128]{2,1,0:T(4,128)S(1)} %slice_add_fusion), kind=kLoop, calls=%fused_computation.21 | loop fusion | flops 40960 | bytes 327680 | tf_op jit(solution)/shard_map/concatenate | solution.py:139
  29.2 6.7 %all-to-all-start.1 = ((f32[64,5,128]{2,1,0:T(8,128)}), f32[64,5,128]{2,1,0:T(8,128)S(1)}, u32[]{:S(2)}, u32[]{:S(2)}) async-start(f32[64,5,128]{2,1,0:T(8,128)} %pad_maximum_fusion), calls=%async_computation.1 | async-start | bytes 524288 | tf_op jit(solution)/shard_map/all_to_all | solution.py:140
  36.0 2.9 %copy.38 = bf16[2048,512]{1,0:T(8,128)(2,1)S(1)} copy(bf16[2048,512]{0,1:T(8,128)(2,1)} %bitcast.19) | data formatting | bytes 4194304 | tf_op jit(solution)/shard_map/dot_general | solution.py:150
  38.8 6.1 %all-to-all-done.1 = f32[64,5,128]{2,1,0:T(8,128)S(1)} async-done(((f32[64,5,128]{2,1,0:T(8,128)}), f32[64,5,128]{2,1,0:T(8,128)S(1)}, u32[]{:S(2)}, u32[]{:S(2)}) %all-to-all-start.1) | async-done | bytes 163872 | tf_op jit(solution)/shard_map/all_to_all | solution.py:140
  44.9 0.1 fusion.52
  45.1 0.1 multiply_reduce_fusion.1
  45.1 0.1 fusion.17
  45.3 0.1 divide_convert_fusion.1
  45.4 0.6 %convolution_bitcast_fusion = f32[4,2,512]{2,1,0:T(2,128)S(1)} fusion(bf16[2,512,1]{1,0,2:T(2,128)(2,1)S(1)} %reshape.187, bf16[4,512,512]{2,1,0:T(8,128)(2,1)S(1)} %bitcast.18), kind=kOutput, calls=%fused_computation.11 | convolution fusion | flops 4194304 | bytes 2115584 | tf_op jit(solution)/shard_map/dot_general | solution.py:150
  46.0 9.5 %all_to_all.22 = f32[4,2,512]{2,1,0:T(2,128)S(1)} all-to-all(f32[4,2,512]{2,1,0:T(2,128)S(1)} %convolution_bitcast_fusion), channel_id=1, replica_groups=mesh['kv'=32,'hd'=4] {'hd'}, dimensions={0} | all-to-all | bytes 32768 | tf_op jit(solution)/shard_map/all_to_all | solution.py:153
  55.5 0.6 %reduce_sum.73 = bf16[2,512]{1,0:T(2,128)(2,1)} reduce(f32[4,2,512]{2,1,0:T(2,128)S(1)} %all_to_all.22, f32[]{:T(128)} %constant.76.clone.1), dimensions={0}, to_apply=%region_8.9 | reduce | flops 3072 | bytes 18436 | tf_op jit(solution)/shard_map/reduce_sum | solution.py:154
  (11 shorter events, 0.2 us)
Async XLA Ops:
  0.0 21.0 %copy-start.2 = (s32[64]{0:T(128)S(1)}, s32[64]{0:T(128)}, u32[]{:S(2)}) copy-start(s32[64]{0:T(128)} %param.13) | copy-start | bytes 772
  0.0 21.8 %copy-start.1 = (s32[64]{0:T(128)S(1)}, s32[64]{0:T(128)}, u32[]{:S(2)}) copy-start(s32[64]{0:T(128)} %param.12) | copy-start | bytes 772
  0.0 21.8 %copy-start = (f32[64,512]{1,0:T(8,128)S(1)}, f32[64,512]{1,0:T(8,128)}, u32[]{:S(2)}) copy-start(f32[64,512]{1,0:T(8,128)} %param.11) | copy-start | bytes 393220
  5.4 16.3 %all-to-all-start = ((f32[32,2,512]{2,1,0:T(2,128)}), f32[32,2,512]{2,1,0:T(2,128)S(1)}, u32[]{:S(2)}, u32[]{:S(2)}) async-start(f32[32,2,512]{2,1,0:T(2,128)} %all_to_all.14), calls=%async_computation | async-start | bytes 262144 | tf_op jit(solution)/shard_map/all_to_all | solution.py:130
  29.2 15.7 %all-to-all-start.1 = ((f32[64,5,128]{2,1,0:T(8,128)}), f32[64,5,128]{2,1,0:T(8,128)S(1)}, u32[]{:S(2)}, u32[]{:S(2)}) async-start(f32[64,5,128]{2,1,0:T(8,128)} %pad_maximum_fusion), calls=%async_computation.1 | async-start | bytes 524288 | tf_op jit(solution)/shard_map/all_to_all | solution.py:140

commit v12 on v11

--- a/solution.py
+++ b/solution.py
@@ -149,9 +149,15 @@
     attended = (upper / lower[..., None]).astype(jnp.bfloat16).reshape(per_device, -1)
     partial_out = jnp.dot(attended, out_weight, preferred_element_type=jnp.float32)
     groups = lax.axis_size("hd")
+    group = lax.axis_index("hd")
     pieces = partial_out.reshape(per_device, groups, -1).transpose(1, 0, 2)
-    pieces = lax.all_to_all(pieces, "hd", split_axis=0, concat_axis=0, tiled=True)
-    return jnp.sum(pieces, axis=0).astype(jnp.bfloat16)
+    total = lax.dynamic_index_in_dim(pieces, group, 0, keepdims=False)
+    for shift in range(1, groups):
+        target = (group + shift) % groups
+        piece = lax.dynamic_index_in_dim(pieces, target, 0, keepdims=False)
+        pairs = [(i, (i + shift) % groups) for i in range(groups)]
+        total = total + lax.ppermute(piece, "hd", pairs)
+    return total.astype(jnp.bfloat16)
 
 
 def solution(mesh):

time: 56.6 us -> 55 us (0.972)
  blocking collectives: 9.46 us -> 0 us
  starting transfers between devices: 15.2 us -> 20.8 us
  waiting for transfers between devices: 6.72 us -> 8.83 us
    all_to_all x1 -> x0, blocking collectives: 9.46 us -> none  [body(): lax.all_to_all(pieces, 'hd', split_axis=0, concat_axis=0, tiled=True)]
    ppermute x0 -> x3, starting transfers between devices: none -> 5.67 us  [body(): total = total + lax.ppermute(piece, 'hd', pairs)]
    ppermute x0 -> x3, waiting for transfers between devices: none -> 2.17 us  [body(): total = total + lax.ppermute(piece, 'hd', pairs)]
    reduce_sum x1 -> x0, other arithmetic: 0.59 us -> none  [body(): return jnp.sum(pieces, axis=0).astype(jnp.bfloat16)]
    convert_element_type x0 -> x1, other arithmetic: none -> 0.59 us  [body(): return total.astype(jnp.bfloat16)]
  transfers between devices with their start and end apart: 2 -> 5, of which waited for: 2 -> 4; matrix products, arithmetic and copies ran while one was open for 18% -> 18% of each run, Pallas kernels for 0% -> 0%
where the time goes in v12:
time: 55 us; the launch traced here: 54.5 us
  starting transfers between devices  20.8 us (38%)
  matrix products  13.5 us (25%)
  waiting for transfers between devices  8.83 us (16%)
  other arithmetic  5.86 us (11%)
  local copies, waits for them, and re-layouts  5.22 us (9%)
    all_to_all x1, starting transfers between devices, body(): lax.all_to_all(outgoing, 'kv', split_axis=0, concat_axis=0, tiled=True)  8.42 us
    all_to_all x1, starting transfers between devices, body(): lax.all_to_all(payload, 'kv', split_axis=0, concat_axis=0, tiled=True)  6.74 us
    all_to_all x1, waiting for transfers between devices, body(): lax.all_to_all(payload, 'kv', split_axis=0, concat_axis=0, tiled=True)  6.01 us
    ppermute x3, starting transfers between devices, body(): total = total + lax.ppermute(piece, 'hd', pairs)  5.67 us
    dot_general x1, matrix products, raw_scores(): jnp.einsum('rhc,rbc->rhb', queries_h, block_data[..., :head_dim], preferr...  5.65 us
    dot_general x1, matrix products, block_partial(): jnp.einsum('rkb,rbc->rkc', rows, block_data[..., head_dim:], preferred_el...  4.58 us
    dot_general x1, local copies, waits for them, and re-layouts, body(): jnp.dot(attended, out_weight, preferred_element_type=jnp.float32)  2.87 us
    ppermute x3, waiting for transfers between devices, body(): total = total + lax.ppermute(piece, 'hd', pairs)  2.17 us
  transfers between devices with their start and end apart: 5, of which 4 were waited for; matrix products, arithmetic and copies ran while one was open for 18% of the time, Pallas kernels for 0%

profile of v12, /device:TPU:0, one launch (start us, length us, event | category | flops | bytes accessed | tf_op | source)
XLA Modules:
  0.0 54.5 jit_solution(5816785308484130374)
XLA Ops:
  0.0 0.0 copy-start.2
  0.0 0.0 copy-start
  0.0 0.0 copy-start.1
  0.1 1.0 %shift-right-arithmetic_select_fusion = (s32[64,512]{1,0:T(8,128)S(1)}, s32[64,512]{1,0:T(8,128)S(1)}) fusion(s32[64,512]{1,0:T(8,128)} %param.9, s32[64]{0:T(128)} %bitcast.41), kind=kLoop, calls=%fused_computation.28 | loop fusion | flops 131072 | bytes 393472 | tf_op jit(solution)/shard_map/jit(_where)/select_n | solution.py:22
  1.1 1.1 %fusion.6 = pred[64,16,32]{2,1,0:T(8,128)(4,1)S(1)} fusion(s32[64,512]{1,0:T(8,128)S(1)} %get-tuple-element.16, s32[64,512]{1,0:T(8,128)S(1)} %get-tuple-element.15), kind=kOutput, calls=%fused_computation.8 | convolution fusion | flops 35160064 | bytes 294912 | tf_op jit(solution)/shard_map/rpa,rpb->rab/dot_general | solution.py:27
  2.1 0.3 copy.33
  2.4 0.1 copy.34
  2.6 0.9 %convert_reduce_fusion = s32[64]{0:T(128)S(1)} fusion(s32[64]{0:T(128)} %param.13), kind=kLoop, calls=%fused_computation.47 | loop fusion | flops 20416 | bytes 512 | tf_op jit(solution)/shard_map/reduce_sum | solution.py:78
  3.5 1.2 %fusion.18 = f32[64,512]{1,0:T(8,128)S(1)} fusion(f32[64,512]{1,0:T(8,128)} %param.11, pred[64,512]{1,0:T(32,128)(4,1)S(1)} %copy.34, s32[512]{0:T(512)S(1)} %iota_add_fusion, s32[64]{0:T(128)} %param.12, s32[64]{0:T(128)} %param.13, s32[64]{0:T(128)S(1)} %and_select_fusion.1, pred[64]{0:T(512)(128)(4,1)S(1)} %get-tuple-element.27, ...), kind=kOutput, calls=%fused_computation.31 | convolution fusion | flops 25313280 | bytes 297920 | tf_op jit(solution)/shard_map/dot_general | solution.py:95
  4.7 0.7 %all_to_all.11 = f32[32,2,512]{2,1,0:T(2,128)} reshape(f32[64,512]{1,0:T(8,128)S(1)} %fusion.18) | data formatting | bytes 262144 | tf_op jit(solution)/shard_map/all_to_all | solution.py:130
  5.4 8.4 %all-to-all-start = ((f32[32,2,512]{2,1,0:T(2,128)}), f32[32,2,512]{2,1,0:T(2,128)S(1)}, u32[]{:S(2)}, u32[]{:S(2)}) async-start(f32[32,2,512]{2,1,0:T(2,128)} %all_to_all.11), calls=%async_computation | async-start | bytes 262144 | tf_op jit(solution)/shard_map/all_to_all | solution.py:130
  13.9 0.7 %fusion.46 = s32[64]{0:T(128)S(1)} fusion(s32[64]{0:T(128)S(1)} %convert_reduce_fusion, s32[64]{0:T(128)} %param.13, s32[]{:T(128)S(6)} %axis_index.23), kind=kLoop, calls=%fused_computation.87 | loop fusion | flops 960 | bytes 772 | tf_op jit(solution)/shard_map/add | solution.py:100
  14.5 0.9 %reshape.192 = bf16[64,4,128]{2,1,0:T(4,128)(2,1)S(1)} reshape(bf16[64,512]{1,0:T(8,128)(2,1)} %param.14) | data formatting | bytes 131072 | tf_op jit(solution)/shard_map/reshape | solution.py:133
  15.4 5.6 %fusion.7 = f32[64,4,512]{2,1,0:T(4,128)S(1)} fusion(bf16[64,4,128]{2,1,0:T(4,128)(2,1)S(1)} %reshape.192, bf16[64,512,256]{2,1,0:T(8,128)(2,1)} %param.8), kind=kOutput, calls=%fused_computation.9 | convolution fusion | flops 33685504 | bytes 8978432 | tf_op jit(solution)/shard_map/rhc,rbc->rhb/dot_general | solution.py:37
  21.0 0.0 copy-done.2
  21.1 0.7 %all-to-all-done = f32[32,2,512]{2,1,0:T(2,128)S(1)} async-done(((f32[32,2,512]{2,1,0:T(2,128)}), f32[32,2,512]{2,1,0:T(2,128)S(1)}, u32[]{:S(2)}, u32[]{:S(2)}) %all-to-all-start) | async-done | bytes 131104 | tf_op jit(solution)/shard_map/all_to_all | solution.py:130
  21.7 0.1 all_to_all.13
  21.8 0.0 copy-done
  21.8 0.0 copy-done.1
  21.8 0.4 maximum_reduce_fusion
  22.2 0.1 fusion.54
  22.3 0.5 multiply_reduce_fusion
  22.8 0.1 fusion.32
  22.9 0.6 %fusion.15 = (bf16[64,4,512]{2,1,0:T(4,128)(2,1)S(1)}, f32[64,4]{1,0:T(8,128)S(1)}) fusion(f32[64,4,512]{2,1,0:T(4,128)S(1)} %fusion.7, f32[64,4]{1,0:T(8,128)S(1)} %fusion.32, pred[64,512]{1,0:T(8,128)(4,1)S(1)} %broadcast_compare_fusion), kind=kLoop, calls=%fused_computation.19 | loop fusion | flops 655104 | bytes 821248 | tf_op jit(solution)/shard_map/convert_element_type | solution.py:62
  23.4 0.1 copy.35
  23.5 4.6 %fusion = f32[64,5,128]{2,1,0:T(8,128)S(1)} fusion(bf16[64,512,256]{2,1,0:T(8,128)(2,1)} %param.8, bf16[64,4,512]{2,1,0:T(4,128)(2,1)S(1)} %get-tuple-element.11, bf16[64,1,512]{2,1,0:T(2,128)(2,1)S(1)} %copy.35), kind=kOutput, calls=%fused_computation | convolution fusion | flops 42598400 | bytes 8880128 | tf_op jit(solution)/shard_map/rkb,rbc->rkc/dot_general | solution.py:63
  28.2 0.1 convert_convert_fusion
  28.3 0.1 select_maximum_fusion
  28.3 0.1 slice_add_fusion
  28.5 0.8 %pad_maximum_fusion = f32[64,5,128]{2,1,0:T(8,128)} fusion(f32[64,1,128]{2,1,0:T(1,128)S(1)} %bitcast.40, f32[64,4,128]{2,1,0:T(4,128)S(1)} %slice_add_fusion), kind=kLoop, calls=%fused_computation.20 | loop fusion | flops 40960 | bytes 327680 | tf_op jit(solution)/shard_map/concatenate | solution.py:139
  29.2 6.7 %all-to-all-start.1 = ((f32[64,5,128]{2,1,0:T(8,128)}), f32[64,5,128]{2,1,0:T(8,128)S(1)}, u32[]{:S(2)}, u32[]{:S(2)}) async-start(f32[64,5,128]{2,1,0:T(8,128)} %pad_maximum_fusion), calls=%async_computation.1 | async-start | bytes 524288 | tf_op jit(solution)/shard_map/all_to_all | solution.py:140
  36.0 2.9 %copy.38 = bf16[2048,512]{1,0:T(8,128)(2,1)S(1)} copy(bf16[2048,512]{0,1:T(8,128)(2,1)} %bitcast.31) | data formatting | bytes 4194304 | tf_op jit(solution)/shard_map/dot_general | solution.py:150
  38.9 6.0 %all-to-all-done.1 = f32[64,5,128]{2,1,0:T(8,128)S(1)} async-done(((f32[64,5,128]{2,1,0:T(8,128)}), f32[64,5,128]{2,1,0:T(8,128)S(1)}, u32[]{:S(2)}, u32[]{:S(2)}) %all-to-all-start.1) | async-done | bytes 163872 | tf_op jit(solution)/shard_map/all_to_all | solution.py:140
  44.9 0.1 fusion.55
  45.1 0.1 multiply_reduce_fusion.1
  45.2 0.1 fusion.17
  45.3 0.1 divide_convert_fusion.1
  45.4 0.6 %fusion.56 = f32[2,4,512]{2,0,1:T(2,128)S(1)} fusion(bf16[2,512,1]{1,0,2:T(2,128)(2,1)S(1)} %reshape.195, bf16[4,512,512]{2,1,0:T(8,128)(2,1)S(1)} %bitcast.30), kind=kOutput, calls=%fused_computation.102 | convolution fusion | flops 4194304 | bytes 2115584 | tf_op jit(solution)/shard_map/dot_general | solution.py:150
  46.0 1.5 %collective-permute-start = (f32[2,512]{1,0:T(2,128)S(1)}, f32[2,512]{1,0:T(2,128)S(1)}, u32[]{:S(2)}, u32[]{:S(2)}) collective-permute-start(f32[2,512]{1,0:T(2,128)S(1)} %get-tuple-element.19), channel_id=1, source_target_pairs={{0,1},{1,2},{2,3},{3,0},{4,5},{5,6},{6,7},{7,4},{8,9},{9,10},{10,1... | collective-permute-start | bytes 12296 | tf_op jit(solution)/shard_map/ppermute | solution.py:159
  47.5 2.7 %collective-permute-start.1 = (f32[2,512]{1,0:T(2,128)S(1)}, f32[2,512]{1,0:T(2,128)S(1)}, u32[]{:S(2)}, u32[]{:S(2)}) collective-permute-start(f32[2,512]{1,0:T(2,128)S(1)} %get-tuple-element.21), channel_id=1, source_target_pairs={{0,2},{1,3},{2,0},{3,1},{4,6},{5,7},{6,4},{7,5},{8,10},{9,11},{10,... | collective-permute-start | bytes 12296 | tf_op jit(solution)/shard_map/ppermute | solution.py:159
  50.3 1.4 %collective-permute-start.2 = (f32[2,512]{1,0:T(2,128)S(1)}, f32[2,512]{1,0:T(2,128)S(1)}, u32[]{:S(2)}, u32[]{:S(2)}) collective-permute-start(f32[2,512]{1,0:T(2,128)S(1)} %get-tuple-element.20), channel_id=1, source_target_pairs={{0,3},{1,0},{2,1},{3,2},{4,7},{5,4},{6,5},{7,6},{8,11},{9,8},{10,9... | collective-permute-start | bytes 12296 | tf_op jit(solution)/shard_map/ppermute | solution.py:159
  51.7 0.0 collective-permute-done
  51.7 0.9 %collective-permute-done.1 = f32[2,512]{1,0:T(2,128)S(1)} collective-permute-done((f32[2,512]{1,0:T(2,128)S(1)}, f32[2,512]{1,0:T(2,128)S(1)}, u32[]{:S(2)}, u32[]{:S(2)}) %collective-permute-start.1) | collective-permute-done | bytes 4128 | tf_op jit(solution)/shard_map/ppermute | solution.py:159
  52.7 1.2 %collective-permute-done.2 = f32[2,512]{1,0:T(2,128)S(1)} collective-permute-done((f32[2,512]{1,0:T(2,128)S(1)}, f32[2,512]{1,0:T(2,128)S(1)}, u32[]{:S(2)}, u32[]{:S(2)}) %collective-permute-start.2) | collective-permute-done | bytes 4128 | tf_op jit(solution)/shard_map/ppermute | solution.py:159
  53.9 0.6 %fusion.42 = bf16[2,512]{1,0:T(2,128)(2,1)} fusion(f32[2,512]{1,0:T(2,128)S(1)} %collective-permute-done.2, f32[2,512]{1,0:T(2,128)S(1)} %collective-permute-done.1, f32[2,512]{1,0:T(2,128)S(1)} %collective-permute-done, f32[2,4,512]{2,0,1:T(2,128)S(1)} %fusion.56, s32[]{:T(128)S(6)} %select_n.118), kind=kLoop, calls=%fused_computation.67 | loop fusion | flops 4096 | bytes 18436 | tf_op jit(solution)/shard_map/convert_element_type | solution.py:160
  (12 shorter events, 0.2 us)
Async XLA Ops:
  0.0 21.0 %copy-start.2 = (s32[64]{0:T(128)S(1)}, s32[64]{0:T(128)}, u32[]{:S(2)}) copy-start(s32[64]{0:T(128)} %param.13) | copy-start | bytes 772
  0.0 21.8 %copy-start = (f32[64,512]{1,0:T(8,128)S(1)}, f32[64,512]{1,0:T(8,128)}, u32[]{:S(2)}) copy-start(f32[64,512]{1,0:T(8,128)} %param.11) | copy-start | bytes 393220
  0.0 21.8 %copy-start.1 = (s32[64]{0:T(128)S(1)}, s32[64]{0:T(128)}, u32[]{:S(2)}) copy-start(s32[64]{0:T(128)} %param.12) | copy-start | bytes 772
  5.4 16.3 %all-to-all-start = ((f32[32,2,512]{2,1,0:T(2,128)}), f32[32,2,512]{2,1,0:T(2,128)S(1)}, u32[]{:S(2)}, u32[]{:S(2)}) async-start(f32[32,2,512]{2,1,0:T(2,128)} %all_to_all.11), calls=%async_computation | async-start | bytes 262144 | tf_op jit(solution)/shard_map/all_to_all | solution.py:130
  29.2 15.7 %all-to-all-start.1 = ((f32[64,5,128]{2,1,0:T(8,128)}), f32[64,5,128]{2,1,0:T(8,128)S(1)}, u32[]{:S(2)}, u32[]{:S(2)}) async-start(f32[64,5,128]{2,1,0:T(8,128)} %pad_maximum_fusion), calls=%async_computation.1 | async-start | bytes 524288 | tf_op jit(solution)/shard_map/all_to_all | solution.py:140
  46.0 5.7 %collective-permute-start = (f32[2,512]{1,0:T(2,128)S(1)}, f32[2,512]{1,0:T(2,128)S(1)}, u32[]{:S(2)}, u32[]{:S(2)}) collective-permute-start(f32[2,512]{1,0:T(2,128)S(1)} %get-tuple-element.19), channel_id=1, source_target_pairs={{0,1},{1,2},{2,3},{3,0},{4,5},{5,6},{6,7},{7,4},{8,9},{9,10},{10,1... | collective-permute-start | bytes 12296 | tf_op jit(solution)/shard_map/ppermute | solution.py:159
  47.5 5.1 %collective-permute-start.1 = (f32[2,512]{1,0:T(2,128)S(1)}, f32[2,512]{1,0:T(2,128)S(1)}, u32[]{:S(2)}, u32[]{:S(2)}) collective-permute-start(f32[2,512]{1,0:T(2,128)S(1)} %get-tuple-element.21), channel_id=1, source_target_pairs={{0,2},{1,3},{2,0},{3,1},{4,6},{5,7},{6,4},{7,5},{8,10},{9,11},{10,... | collective-permute-start | bytes 12296 | tf_op jit(solution)/shard_map/ppermute | solution.py:159
  50.3 3.6 %collective-permute-start.2 = (f32[2,512]{1,0:T(2,128)S(1)}, f32[2,512]{1,0:T(2,128)S(1)}, u32[]{:S(2)}, u32[]{:S(2)}) collective-permute-start(f32[2,512]{1,0:T(2,128)S(1)} %get-tuple-element.20), channel_id=1, source_target_pairs={{0,3},{1,0},{2,1},{3,2},{4,7},{5,4},{6,5},{7,6},{8,11},{9,8},{10,9... | collective-permute-start | bytes 12296 | tf_op jit(solution)/shard_map/ppermute | solution.py:159

commit v13 on v11

--- a/solution.py
+++ b/solution.py
@@ -149,9 +149,28 @@
     attended = (upper / lower[..., None]).astype(jnp.bfloat16).reshape(per_device, -1)
     partial_out = jnp.dot(attended, out_weight, preferred_element_type=jnp.float32)
     groups = lax.axis_size("hd")
+    group = lax.axis_index("hd")
     pieces = partial_out.reshape(per_device, groups, -1).transpose(1, 0, 2)
-    pieces = lax.all_to_all(pieces, "hd", split_axis=0, concat_axis=0, tiled=True)
-    return jnp.sum(pieces, axis=0).astype(jnp.bfloat16)
+    return halving_sum(pieces, group, groups, "hd").astype(jnp.bfloat16)
+
+
+def halving_sum(pieces, group, groups, axis):
+    if groups & (groups - 1):
+        total = lax.dynamic_index_in_dim(pieces, group, 0, keepdims=False)
+        for shift in range(1, groups):
+            piece = lax.dynamic_index_in_dim(pieces, (group + shift) % groups, 0, keepdims=False)
+            pairs = [(i, (i + shift) % groups) for i in range(groups)]
+            total = total + lax.ppermute(piece, axis, pairs)
+        return total
+    width = groups
+    while width > 1:
+        width //= 2
+        pairs = [(i, i ^ width) for i in range(groups)]
+        own = (group & width) // width
+        keep = lax.dynamic_slice_in_dim(pieces, own * width, width, 0)
+        send = lax.dynamic_slice_in_dim(pieces, (1 - own) * width, width, 0)
+        pieces = keep + lax.ppermute(send, axis, pairs)
+    return pieces[0]
 
 
 def solution(mesh):

time: 56.6 us -> 56 us (0.989)
  blocking collectives: 9.46 us -> 0 us
  starting transfers between devices: 15.2 us -> 19.8 us
  waiting for transfers between devices: 6.72 us -> 11 us
    all_to_all x1 -> x0, blocking collectives: 9.46 us -> none  [body(): lax.all_to_all(pieces, 'hd', split_axis=0, concat_axis=0, tiled=True)]
    ppermute x0 -> x2, starting transfers between devices: none -> 4.6 us  [halving_sum(): pieces = keep + lax.ppermute(send, axis, pairs)]
    ppermute x0 -> x2, waiting for transfers between devices: none -> 4.26 us  [halving_sum(): pieces = keep + lax.ppermute(send, axis, pairs)]
    reduce_sum x1 -> x0, other arithmetic: 0.59 us -> none  [body(): return jnp.sum(pieces, axis=0).astype(jnp.bfloat16)]
    convert_element_type x0 -> x1, other arithmetic: none -> 0.58 us  [body(): return halving_sum(pieces, group, groups, 'hd').astype(jnp.bfloat16)]
  transfers between devices with their start and end apart: 2 -> 4, of which waited for: 2 -> 4; matrix products, arithmetic and copies ran while one was open for 18% -> 18% of each run, Pallas kernels for 0% -> 0%
where the time goes in v13:
time: 56 us; the launch traced here: 55.5 us
  starting transfers between devices  19.8 us (35%)
  matrix products  13.5 us (24%)
  waiting for transfers between devices  11 us (20%)
  other arithmetic  5.86 us (10%)
  local copies, waits for them, and re-layouts  5.23 us (9%)
    all_to_all x1, starting transfers between devices, body(): lax.all_to_all(outgoing, 'kv', split_axis=0, concat_axis=0, tiled=True)  8.42 us
    all_to_all x1, starting transfers between devices, body(): lax.all_to_all(payload, 'kv', split_axis=0, concat_axis=0, tiled=True)  6.74 us
    all_to_all x1, waiting for transfers between devices, body(): lax.all_to_all(payload, 'kv', split_axis=0, concat_axis=0, tiled=True)  6.04 us
    dot_general x1, matrix products, raw_scores(): jnp.einsum('rhc,rbc->rhb', queries_h, block_data[..., :head_dim], preferr...  5.65 us
    ppermute x2, starting transfers between devices, halving_sum(): pieces = keep + lax.ppermute(send, axis, pairs)  4.6 us
    dot_general x1, matrix products, block_partial(): jnp.einsum('rkb,rbc->rkc', rows, block_data[..., head_dim:], preferred_el...  4.58 us
    ppermute x2, waiting for transfers between devices, halving_sum(): pieces = keep + lax.ppermute(send, axis, pairs)  4.26 us
    dot_general x1, local copies, waits for them, and re-layouts, body(): jnp.dot(attended, out_weight, preferred_element_type=jnp.float32)  2.87 us
  transfers between devices with their start and end apart: 4, of which 4 were waited for; matrix products, arithmetic and copies ran while one was open for 18% of the time, Pallas kernels for 0%

profile of v13, /device:TPU:0, one launch (start us, length us, event | category | flops | bytes accessed | tf_op | source)
XLA Modules:
  0.0 55.5 jit_solution(17184335382466409969)
XLA Ops:
  0.0 0.0 copy-start.2
  0.0 0.0 copy-start
  0.0 0.0 copy-start.1
  0.1 1.0 %shift-right-arithmetic_select_fusion = (s32[64,512]{1,0:T(8,128)S(1)}, s32[64,512]{1,0:T(8,128)S(1)}) fusion(s32[64,512]{1,0:T(8,128)} %param.9, s32[64]{0:T(128)} %bitcast.33), kind=kLoop, calls=%fused_computation.28 | loop fusion | flops 131072 | bytes 393472 | tf_op jit(solution)/shard_map/jit(_where)/select_n | solution.py:22
  1.1 1.1 %fusion.6 = pred[64,16,32]{2,1,0:T(8,128)(4,1)S(1)} fusion(s32[64,512]{1,0:T(8,128)S(1)} %get-tuple-element.16, s32[64,512]{1,0:T(8,128)S(1)} %get-tuple-element.15), kind=kOutput, calls=%fused_computation.8 | convolution fusion | flops 35160064 | bytes 294912 | tf_op jit(solution)/shard_map/rpa,rpb->rab/dot_general | solution.py:27
  2.1 0.3 copy.33
  2.4 0.1 copy.34
  2.6 0.9 %convert_reduce_fusion = s32[64]{0:T(128)S(1)} fusion(s32[64]{0:T(128)} %param.13), kind=kLoop, calls=%fused_computation.47 | loop fusion | flops 20416 | bytes 512 | tf_op jit(solution)/shard_map/reduce_sum | solution.py:78
  3.5 1.2 %fusion.18 = f32[64,512]{1,0:T(8,128)S(1)} fusion(f32[64,512]{1,0:T(8,128)} %param.11, pred[64,512]{1,0:T(32,128)(4,1)S(1)} %copy.34, s32[512]{0:T(512)S(1)} %iota_add_fusion, s32[64]{0:T(128)} %param.12, s32[64]{0:T(128)} %param.13, s32[64]{0:T(128)S(1)} %and_select_fusion.1, pred[64]{0:T(512)(128)(4,1)S(1)} %get-tuple-element.24, ...), kind=kOutput, calls=%fused_computation.31 | convolution fusion | flops 25313280 | bytes 297920 | tf_op jit(solution)/shard_map/dot_general | solution.py:95
  4.7 0.7 %all_to_all.11 = f32[32,2,512]{2,1,0:T(2,128)} reshape(f32[64,512]{1,0:T(8,128)S(1)} %fusion.18) | data formatting | bytes 262144 | tf_op jit(solution)/shard_map/all_to_all | solution.py:130
  5.4 8.4 %all-to-all-start = ((f32[32,2,512]{2,1,0:T(2,128)}), f32[32,2,512]{2,1,0:T(2,128)S(1)}, u32[]{:S(2)}, u32[]{:S(2)}) async-start(f32[32,2,512]{2,1,0:T(2,128)} %all_to_all.11), calls=%async_computation | async-start | bytes 262144 | tf_op jit(solution)/shard_map/all_to_all | solution.py:130
  13.9 0.7 %fusion.44 = s32[64]{0:T(128)S(1)} fusion(s32[64]{0:T(128)S(1)} %convert_reduce_fusion, s32[64]{0:T(128)} %param.13, s32[]{:T(128)S(6)} %axis_index.23), kind=kLoop, calls=%fused_computation.85 | loop fusion | flops 960 | bytes 772 | tf_op jit(solution)/shard_map/add | solution.py:100
  14.5 0.9 %reshape.185 = bf16[64,4,128]{2,1,0:T(4,128)(2,1)S(1)} reshape(bf16[64,512]{1,0:T(8,128)(2,1)} %param.14) | data formatting | bytes 131072 | tf_op jit(solution)/shard_map/reshape | solution.py:133
  15.4 5.6 %fusion.7 = f32[64,4,512]{2,1,0:T(4,128)S(1)} fusion(bf16[64,4,128]{2,1,0:T(4,128)(2,1)S(1)} %reshape.185, bf16[64,512,256]{2,1,0:T(8,128)(2,1)} %param.8), kind=kOutput, calls=%fused_computation.9 | convolution fusion | flops 33685504 | bytes 8978432 | tf_op jit(solution)/shard_map/rhc,rbc->rhb/dot_general | solution.py:37
  21.0 0.0 copy-done.2
  21.1 0.7 %all-to-all-done = f32[32,2,512]{2,1,0:T(2,128)S(1)} async-done(((f32[32,2,512]{2,1,0:T(2,128)}), f32[32,2,512]{2,1,0:T(2,128)S(1)}, u32[]{:S(2)}, u32[]{:S(2)}) %all-to-all-start) | async-done | bytes 131104 | tf_op jit(solution)/shard_map/all_to_all | solution.py:130
  21.7 0.1 all_to_all.13
  21.8 0.0 copy-done
  21.8 0.0 copy-done.1
  21.8 0.4 maximum_reduce_fusion
  22.2 0.1 fusion.52
  22.3 0.5 multiply_reduce_fusion
  22.8 0.1 fusion.32
  22.9 0.6 fusion.15
  23.4 0.1 copy.35
  23.5 4.6 %fusion = f32[64,5,128]{2,1,0:T(8,128)S(1)} fusion(bf16[64,512,256]{2,1,0:T(8,128)(2,1)} %param.8, bf16[64,4,512]{2,1,0:T(4,128)(2,1)S(1)} %get-tuple-element.11, bf16[64,1,512]{2,1,0:T(2,128)(2,1)S(1)} %copy.35), kind=kOutput, calls=%fused_computation | convolution fusion | flops 42598400 | bytes 8880128 | tf_op jit(solution)/shard_map/rkb,rbc->rkc/dot_general | solution.py:63
  28.2 0.1 convert_convert_fusion
  28.3 0.1 select_maximum_fusion
  28.3 0.1 slice_add_fusion
  28.5 0.8 %pad_maximum_fusion = f32[64,5,128]{2,1,0:T(8,128)} fusion(f32[64,1,128]{2,1,0:T(1,128)S(1)} %bitcast.32, f32[64,4,128]{2,1,0:T(4,128)S(1)} %slice_add_fusion), kind=kLoop, calls=%fused_computation.20 | loop fusion | flops 40960 | bytes 327680 | tf_op jit(solution)/shard_map/concatenate | solution.py:139
  29.2 6.7 %all-to-all-start.1 = ((f32[64,5,128]{2,1,0:T(8,128)}), f32[64,5,128]{2,1,0:T(8,128)S(1)}, u32[]{:S(2)}, u32[]{:S(2)}) async-start(f32[64,5,128]{2,1,0:T(8,128)} %pad_maximum_fusion), calls=%async_computation.1 | async-start | bytes 524288 | tf_op jit(solution)/shard_map/all_to_all | solution.py:140
  36.0 2.9 %copy.38 = bf16[2048,512]{1,0:T(8,128)(2,1)S(1)} copy(bf16[2048,512]{0,1:T(8,128)(2,1)} %bitcast.23) | data formatting | bytes 4194304 | tf_op jit(solution)/shard_map/dot_general | solution.py:150
  38.9 6.0 %all-to-all-done.1 = f32[64,5,128]{2,1,0:T(8,128)S(1)} async-done(((f32[64,5,128]{2,1,0:T(8,128)}), f32[64,5,128]{2,1,0:T(8,128)S(1)}, u32[]{:S(2)}, u32[]{:S(2)}) %all-to-all-start.1) | async-done | bytes 163872 | tf_op jit(solution)/shard_map/all_to_all | solution.py:140
  44.9 0.1 fusion.53
  45.1 0.1 multiply_reduce_fusion.1
  45.2 0.1 fusion.17
  45.3 0.1 divide_convert_fusion.1
  45.4 0.6 %fusion.54 = f32[2,4,512]{2,0,1:T(2,128)S(1)} fusion(bf16[2,512,1]{1,0,2:T(2,128)(2,1)S(1)} %reshape.188, bf16[4,512,512]{2,1,0:T(8,128)(2,1)S(1)} %bitcast.22), kind=kOutput, calls=%fused_computation.100 | convolution fusion | flops 4194304 | bytes 2115584 | tf_op jit(solution)/shard_map/dot_general | solution.py:150
  46.0 3.0 %collective-permute-start = (f32[2,2,512]{2,1,0:T(2,128)S(1)}, f32[2,2,512]{2,1,0:T(2,128)S(1)}, u32[]{:S(2)}, u32[]{:S(2)}) collective-permute-start(f32[2,2,512]{2,1,0:T(2,128)S(1)} %dynamic-slice_bitcast_fusion), channel_id=1, source_target_pairs={{0,2},{1,3},{2,0},{3,1},{4,6},{5,7},{6,4},{7,5},{8,10},{9,11},{10,... | collective-permute-start | bytes 24584 | tf_op jit(solution)/shard_map/ppermute | solution.py:172
  49.1 2.1 %collective-permute-done = f32[2,2,512]{2,1,0:T(2,128)S(1)} collective-permute-done((f32[2,2,512]{2,1,0:T(2,128)S(1)}, f32[2,2,512]{2,1,0:T(2,128)S(1)}, u32[]{:S(2)}, u32[]{:S(2)}) %collective-permute-start) | collective-permute-done | bytes 8224 | tf_op jit(solution)/shard_map/ppermute | solution.py:172
  51.2 1.6 %collective-permute-start.1 = (f32[1,2,512]{2,1,0:T(2,128)S(1)}, f32[1,2,512]{2,1,0:T(2,128)S(1)}, u32[]{:S(2)}, u32[]{:S(2)}) collective-permute-start(f32[1,2,512]{2,1,0:T(2,128)S(1)} %constant_dynamic-slice_fusion), channel_id=1, source_target_pairs={{0,1},{1,0},{2,3},{3,2},{4,5},{5,4},{6,7},{7,6},{8,9},{9,8},{10,11... | collective-permute-start | bytes 12296 | tf_op jit(solution)/shard_map/ppermute | solution.py:172
  52.8 2.1 %collective-permute-done.1 = f32[1,2,512]{2,1,0:T(2,128)S(1)} collective-permute-done((f32[1,2,512]{2,1,0:T(2,128)S(1)}, f32[1,2,512]{2,1,0:T(2,128)S(1)}, u32[]{:S(2)}, u32[]{:S(2)}) %collective-permute-start.1) | collective-permute-done | bytes 4128 | tf_op jit(solution)/shard_map/ppermute | solution.py:172
  54.9 0.6 %fusion.40 = bf16[2,512]{1,0:T(2,128)(2,1)} fusion(f32[1,2,512]{2,1,0:T(2,128)S(1)} %collective-permute-done.1, f32[2,2,512]{2,1,0:T(2,128)S(1)} %bitcast_add_fusion, s32[]{:T(128)S(6)} %select_n.111), kind=kLoop, calls=%fused_computation.72 | loop fusion | flops 2048 | bytes 10244 | tf_op jit(solution)/shard_map/convert_element_type | solution.py:154
  (14 shorter events, 0.2 us)
Async XLA Ops:
  0.0 21.0 %copy-start.2 = (s32[64]{0:T(128)S(1)}, s32[64]{0:T(128)}, u32[]{:S(2)}) copy-start(s32[64]{0:T(128)} %param.13) | copy-start | bytes 772
  0.0 21.8 %copy-start = (f32[64,512]{1,0:T(8,128)S(1)}, f32[64,512]{1,0:T(8,128)}, u32[]{:S(2)}) copy-start(f32[64,512]{1,0:T(8,128)} %param.11) | copy-start | bytes 393220
  0.0 21.8 %copy-start.1 = (s32[64]{0:T(128)S(1)}, s32[64]{0:T(128)}, u32[]{:S(2)}) copy-start(s32[64]{0:T(128)} %param.12) | copy-start | bytes 772
  5.4 16.3 %all-to-all-start = ((f32[32,2,512]{2,1,0:T(2,128)}), f32[32,2,512]{2,1,0:T(2,128)S(1)}, u32[]{:S(2)}, u32[]{:S(2)}) async-start(f32[32,2,512]{2,1,0:T(2,128)} %all_to_all.11), calls=%async_computation | async-start | bytes 262144 | tf_op jit(solution)/shard_map/all_to_all | solution.py:130
  29.2 15.7 %all-to-all-start.1 = ((f32[64,5,128]{2,1,0:T(8,128)}), f32[64,5,128]{2,1,0:T(8,128)S(1)}, u32[]{:S(2)}, u32[]{:S(2)}) async-start(f32[64,5,128]{2,1,0:T(8,128)} %pad_maximum_fusion), calls=%async_computation.1 | async-start | bytes 524288 | tf_op jit(solution)/shard_map/all_to_all | solution.py:140
  46.0 5.2 %collective-permute-start = (f32[2,2,512]{2,1,0:T(2,128)S(1)}, f32[2,2,512]{2,1,0:T(2,128)S(1)}, u32[]{:S(2)}, u32[]{:S(2)}) collective-permute-start(f32[2,2,512]{2,1,0:T(2,128)S(1)} %dynamic-slice_bitcast_fusion), channel_id=1, source_target_pairs={{0,2},{1,3},{2,0},{3,1},{4,6},{5,7},{6,4},{7,5},{8,10},{9,11},{10,... | collective-permute-start | bytes 24584 | tf_op jit(solution)/shard_map/ppermute | solution.py:172
  51.2 3.7 %collective-permute-start.1 = (f32[1,2,512]{2,1,0:T(2,128)S(1)}, f32[1,2,512]{2,1,0:T(2,128)S(1)}, u32[]{:S(2)}, u32[]{:S(2)}) collective-permute-start(f32[1,2,512]{2,1,0:T(2,128)S(1)} %constant_dynamic-slice_fusion), channel_id=1, source_target_pairs={{0,1},{1,0},{2,3},{3,2},{4,5},{5,4},{6,7},{7,6},{8,9},{9,8},{10,11... | collective-permute-start | bytes 12296 | tf_op jit(solution)/shard_map/ppermute | solution.py:172

commit v14 on v12

--- a/solution.py
+++ b/solution.py
@@ -152,7 +152,7 @@
     group = lax.axis_index("hd")
     pieces = partial_out.reshape(per_device, groups, -1).transpose(1, 0, 2)
     total = lax.dynamic_index_in_dim(pieces, group, 0, keepdims=False)
-    for shift in range(1, groups):
+    for shift in sorted(range(1, groups), key=lambda s: -min(s, groups - s)):
         target = (group + shift) % groups
         piece = lax.dynamic_index_in_dim(pieces, target, 0, keepdims=False)
         pairs = [(i, (i + shift) % groups) for i in range(groups)]

time: 55 us -> 55.4 us (level)
  starting transfers between devices: 20.8 us -> 21.4 us
  waiting for transfers between devices: 8.83 us -> 8.24 us
    ppermute x3, starting transfers between devices: 5.67 us -> 6.27 us  [body(): total = total + lax.ppermute(piece, 'hd', pairs)]
    ppermute x3, waiting for transfers between devices: 2.17 us -> 1.58 us  [body(): total = total + lax.ppermute(piece, 'hd', pairs)]
  transfers between devices with their start and end apart: 5 -> 5, of which waited for: 4 -> 3; matrix products, arithmetic and copies ran while one was open for 18% -> 18% of each run, Pallas kernels for 0% -> 0%
where the time goes in v14:
time: 55.4 us; the launch traced here: 54.5 us
  starting transfers between devices  21.4 us (39%)
  matrix products  13.5 us (24%)
  waiting for transfers between devices  8.24 us (15%)
  other arithmetic  5.86 us (11%)
  local copies, waits for them, and re-layouts  5.22 us (9%)
    all_to_all x1, starting transfers between devices, body(): lax.all_to_all(outgoing, 'kv', split_axis=0, concat_axis=0, tiled=True)  8.42 us
    all_to_all x1, starting transfers between devices, body(): lax.all_to_all(payload, 'kv', split_axis=0, concat_axis=0, tiled=True)  6.74 us
    ppermute x3, starting transfers between devices, body(): total = total + lax.ppermute(piece, 'hd', pairs)  6.27 us
    all_to_all x1, waiting for transfers between devices, body(): lax.all_to_all(payload, 'kv', split_axis=0, concat_axis=0, tiled=True)  6.01 us
    dot_general x1, matrix products, raw_scores(): jnp.einsum('rhc,rbc->rhb', queries_h, block_data[..., :head_dim], preferr...  5.65 us
    dot_general x1, matrix products, block_partial(): jnp.einsum('rkb,rbc->rkc', rows, block_data[..., head_dim:], preferred_el...  4.58 us
    dot_general x1, local copies, waits for them, and re-layouts, body(): jnp.dot(attended, out_weight, preferred_element_type=jnp.float32)  2.87 us
    ppermute x3, waiting for transfers between devices, body(): total = total + lax.ppermute(piece, 'hd', pairs)  1.58 us
  transfers between devices with their start and end apart: 5, of which 3 were waited for; matrix products, arithmetic and copies ran while one was open for 18% of the time, Pallas kernels for 0%

profile of v14, /device:TPU:0, one launch (start us, length us, event | category | flops | bytes accessed | tf_op | source)
XLA Modules:
  0.0 54.5 jit_solution(567388587700789375)
XLA Ops:
  0.0 0.0 copy-start.2
  0.0 0.0 copy-start
  0.0 0.0 copy-start.1
  0.1 1.0 %shift-right-arithmetic_select_fusion = (s32[64,512]{1,0:T(8,128)S(1)}, s32[64,512]{1,0:T(8,128)S(1)}) fusion(s32[64,512]{1,0:T(8,128)} %param.9, s32[64]{0:T(128)} %bitcast.41), kind=kLoop, calls=%fused_computation.28 | loop fusion | flops 131072 | bytes 393472 | tf_op jit(solution)/shard_map/jit(_where)/select_n | solution.py:22
  1.1 1.1 %fusion.6 = pred[64,16,32]{2,1,0:T(8,128)(4,1)S(1)} fusion(s32[64,512]{1,0:T(8,128)S(1)} %get-tuple-element.16, s32[64,512]{1,0:T(8,128)S(1)} %get-tuple-element.15), kind=kOutput, calls=%fused_computation.8 | convolution fusion | flops 35160064 | bytes 294912 | tf_op jit(solution)/shard_map/rpa,rpb->rab/dot_general | solution.py:27
  2.1 0.3 copy.33
  2.4 0.1 copy.34
  2.6 0.9 %convert_reduce_fusion = s32[64]{0:T(128)S(1)} fusion(s32[64]{0:T(128)} %param.13), kind=kLoop, calls=%fused_computation.47 | loop fusion | flops 20416 | bytes 512 | tf_op jit(solution)/shard_map/reduce_sum | solution.py:78
  3.5 1.2 %fusion.18 = f32[64,512]{1,0:T(8,128)S(1)} fusion(f32[64,512]{1,0:T(8,128)} %param.11, pred[64,512]{1,0:T(32,128)(4,1)S(1)} %copy.34, s32[512]{0:T(512)S(1)} %iota_add_fusion, s32[64]{0:T(128)} %param.12, s32[64]{0:T(128)} %param.13, s32[64]{0:T(128)S(1)} %and_select_fusion.1, pred[64]{0:T(512)(128)(4,1)S(1)} %get-tuple-element.27, ...), kind=kOutput, calls=%fused_computation.31 | convolution fusion | flops 25313280 | bytes 297920 | tf_op jit(solution)/shard_map/dot_general | solution.py:95
  4.7 0.7 %all_to_all.11 = f32[32,2,512]{2,1,0:T(2,128)} reshape(f32[64,512]{1,0:T(8,128)S(1)} %fusion.18) | data formatting | bytes 262144 | tf_op jit(solution)/shard_map/all_to_all | solution.py:130
  5.4 8.4 %all-to-all-start = ((f32[32,2,512]{2,1,0:T(2,128)}), f32[32,2,512]{2,1,0:T(2,128)S(1)}, u32[]{:S(2)}, u32[]{:S(2)}) async-start(f32[32,2,512]{2,1,0:T(2,128)} %all_to_all.11), calls=%async_computation | async-start | bytes 262144 | tf_op jit(solution)/shard_map/all_to_all | solution.py:130
  13.9 0.7 %fusion.46 = s32[64]{0:T(128)S(1)} fusion(s32[64]{0:T(128)S(1)} %convert_reduce_fusion, s32[64]{0:T(128)} %param.13, s32[]{:T(128)S(6)} %axis_index.23), kind=kLoop, calls=%fused_computation.87 | loop fusion | flops 960 | bytes 772 | tf_op jit(solution)/shard_map/add | solution.py:100
  14.5 0.9 %reshape.192 = bf16[64,4,128]{2,1,0:T(4,128)(2,1)S(1)} reshape(bf16[64,512]{1,0:T(8,128)(2,1)} %param.14) | data formatting | bytes 131072 | tf_op jit(solution)/shard_map/reshape | solution.py:133
  15.4 5.6 %fusion.7 = f32[64,4,512]{2,1,0:T(4,128)S(1)} fusion(bf16[64,4,128]{2,1,0:T(4,128)(2,1)S(1)} %reshape.192, bf16[64,512,256]{2,1,0:T(8,128)(2,1)} %param.8), kind=kOutput, calls=%fused_computation.9 | convolution fusion | flops 33685504 | bytes 8978432 | tf_op jit(solution)/shard_map/rhc,rbc->rhb/dot_general | solution.py:37
  21.0 0.0 copy-done.2
  21.1 0.7 %all-to-all-done = f32[32,2,512]{2,1,0:T(2,128)S(1)} async-done(((f32[32,2,512]{2,1,0:T(2,128)}), f32[32,2,512]{2,1,0:T(2,128)S(1)}, u32[]{:S(2)}, u32[]{:S(2)}) %all-to-all-start) | async-done | bytes 131104 | tf_op jit(solution)/shard_map/all_to_all | solution.py:130
  21.7 0.1 all_to_all.13
  21.8 0.0 copy-done
  21.8 0.0 copy-done.1
  21.8 0.4 maximum_reduce_fusion
  22.2 0.1 fusion.54
  22.3 0.5 multiply_reduce_fusion
  22.8 0.1 fusion.32
  22.9 0.6 %fusion.15 = (bf16[64,4,512]{2,1,0:T(4,128)(2,1)S(1)}, f32[64,4]{1,0:T(8,128)S(1)}) fusion(f32[64,4,512]{2,1,0:T(4,128)S(1)} %fusion.7, f32[64,4]{1,0:T(8,128)S(1)} %fusion.32, pred[64,512]{1,0:T(8,128)(4,1)S(1)} %broadcast_compare_fusion), kind=kLoop, calls=%fused_computation.19 | loop fusion | flops 655104 | bytes 821248 | tf_op jit(solution)/shard_map/convert_element_type | solution.py:62
  23.4 0.1 copy.35
  23.5 4.6 %fusion = f32[64,5,128]{2,1,0:T(8,128)S(1)} fusion(bf16[64,512,256]{2,1,0:T(8,128)(2,1)} %param.8, bf16[64,4,512]{2,1,0:T(4,128)(2,1)S(1)} %get-tuple-element.11, bf16[64,1,512]{2,1,0:T(2,128)(2,1)S(1)} %copy.35), kind=kOutput, calls=%fused_computation | convolution fusion | flops 42598400 | bytes 8880128 | tf_op jit(solution)/shard_map/rkb,rbc->rkc/dot_general | solution.py:63
  28.2 0.1 convert_convert_fusion
  28.3 0.1 select_maximum_fusion
  28.3 0.1 slice_add_fusion
  28.5 0.8 %pad_maximum_fusion = f32[64,5,128]{2,1,0:T(8,128)} fusion(f32[64,1,128]{2,1,0:T(1,128)S(1)} %bitcast.40, f32[64,4,128]{2,1,0:T(4,128)S(1)} %slice_add_fusion), kind=kLoop, calls=%fused_computation.20 | loop fusion | flops 40960 | bytes 327680 | tf_op jit(solution)/shard_map/concatenate | solution.py:139
  29.2 6.7 %all-to-all-start.1 = ((f32[64,5,128]{2,1,0:T(8,128)}), f32[64,5,128]{2,1,0:T(8,128)S(1)}, u32[]{:S(2)}, u32[]{:S(2)}) async-start(f32[64,5,128]{2,1,0:T(8,128)} %pad_maximum_fusion), calls=%async_computation.1 | async-start | bytes 524288 | tf_op jit(solution)/shard_map/all_to_all | solution.py:140
  36.0 2.9 %copy.38 = bf16[2048,512]{1,0:T(8,128)(2,1)S(1)} copy(bf16[2048,512]{0,1:T(8,128)(2,1)} %bitcast.31) | data formatting | bytes 4194304 | tf_op jit(solution)/shard_map/dot_general | solution.py:150
  38.9 6.0 %all-to-all-done.1 = f32[64,5,128]{2,1,0:T(8,128)S(1)} async-done(((f32[64,5,128]{2,1,0:T(8,128)}), f32[64,5,128]{2,1,0:T(8,128)S(1)}, u32[]{:S(2)}, u32[]{:S(2)}) %all-to-all-start.1) | async-done | bytes 163872 | tf_op jit(solution)/shard_map/all_to_all | solution.py:140
  44.9 0.1 fusion.55
  45.1 0.1 multiply_reduce_fusion.1
  45.2 0.1 fusion.17
  45.3 0.1 divide_convert_fusion.1
  45.4 0.6 %fusion.56 = f32[2,4,512]{2,0,1:T(2,128)S(1)} fusion(bf16[2,512,1]{1,0,2:T(2,128)(2,1)S(1)} %reshape.195, bf16[4,512,512]{2,1,0:T(8,128)(2,1)S(1)} %bitcast.30), kind=kOutput, calls=%fused_computation.102 | convolution fusion | flops 4194304 | bytes 2115584 | tf_op jit(solution)/shard_map/dot_general | solution.py:150
  46.0 3.0 %collective-permute-start = (f32[2,512]{1,0:T(2,128)S(1)}, f32[2,512]{1,0:T(2,128)S(1)}, u32[]{:S(2)}, u32[]{:S(2)}) collective-permute-start(f32[2,512]{1,0:T(2,128)S(1)} %get-tuple-element.19), channel_id=1, source_target_pairs={{0,2},{1,3},{2,0},{3,1},{4,6},{5,7},{6,4},{7,5},{8,10},{9,11},{10,... | collective-permute-start | bytes 12296 | tf_op jit(solution)/shard_map/ppermute | solution.py:159
  49.1 0.6 %collective-permute-start.1 = (f32[2,512]{1,0:T(2,128)S(1)}, f32[2,512]{1,0:T(2,128)S(1)}, u32[]{:S(2)}, u32[]{:S(2)}) collective-permute-start(f32[2,512]{1,0:T(2,128)S(1)} %get-tuple-element.21), channel_id=1, source_target_pairs={{0,1},{1,2},{2,3},{3,0},{4,5},{5,6},{6,7},{7,4},{8,9},{9,10},{10,1... | collective-permute-start | bytes 12296 | tf_op jit(solution)/shard_map/ppermute | solution.py:159
  49.7 2.6 %collective-permute-start.2 = (f32[2,512]{1,0:T(2,128)S(1)}, f32[2,512]{1,0:T(2,128)S(1)}, u32[]{:S(2)}, u32[]{:S(2)}) collective-permute-start(f32[2,512]{1,0:T(2,128)S(1)} %get-tuple-element.20), channel_id=1, source_target_pairs={{0,3},{1,0},{2,1},{3,2},{4,7},{5,4},{6,5},{7,6},{8,11},{9,8},{10,9... | collective-permute-start | bytes 12296 | tf_op jit(solution)/shard_map/ppermute | solution.py:159
  52.3 0.0 collective-permute-done
  52.3 1.6 %collective-permute-done.1 = f32[2,512]{1,0:T(2,128)S(1)} collective-permute-done((f32[2,512]{1,0:T(2,128)S(1)}, f32[2,512]{1,0:T(2,128)S(1)}, u32[]{:S(2)}, u32[]{:S(2)}) %collective-permute-start.1) | collective-permute-done | bytes 4128 | tf_op jit(solution)/shard_map/ppermute | solution.py:159
  53.9 0.0 collective-permute-done.2
  53.9 0.6 %fusion.42 = bf16[2,512]{1,0:T(2,128)(2,1)} fusion(f32[2,512]{1,0:T(2,128)S(1)} %collective-permute-done.2, f32[2,512]{1,0:T(2,128)S(1)} %collective-permute-done.1, f32[2,512]{1,0:T(2,128)S(1)} %collective-permute-done, f32[2,4,512]{2,0,1:T(2,128)S(1)} %fusion.56, s32[]{:T(128)S(6)} %select_n.118), kind=kLoop, calls=%fused_computation.67 | loop fusion | flops 4096 | bytes 18436 | tf_op jit(solution)/shard_map/convert_element_type | solution.py:160
  (12 shorter events, 0.2 us)
Async XLA Ops:
  0.0 21.0 %copy-start.2 = (s32[64]{0:T(128)S(1)}, s32[64]{0:T(128)}, u32[]{:S(2)}) copy-start(s32[64]{0:T(128)} %param.13) | copy-start | bytes 772
  0.0 21.8 %copy-start = (f32[64,512]{1,0:T(8,128)S(1)}, f32[64,512]{1,0:T(8,128)}, u32[]{:S(2)}) copy-start(f32[64,512]{1,0:T(8,128)} %param.11) | copy-start | bytes 393220
  0.0 21.8 %copy-start.1 = (s32[64]{0:T(128)S(1)}, s32[64]{0:T(128)}, u32[]{:S(2)}) copy-start(s32[64]{0:T(128)} %param.12) | copy-start | bytes 772
  5.4 16.3 %all-to-all-start = ((f32[32,2,512]{2,1,0:T(2,128)}), f32[32,2,512]{2,1,0:T(2,128)S(1)}, u32[]{:S(2)}, u32[]{:S(2)}) async-start(f32[32,2,512]{2,1,0:T(2,128)} %all_to_all.11), calls=%async_computation | async-start | bytes 262144 | tf_op jit(solution)/shard_map/all_to_all | solution.py:130
  29.2 15.7 %all-to-all-start.1 = ((f32[64,5,128]{2,1,0:T(8,128)}), f32[64,5,128]{2,1,0:T(8,128)S(1)}, u32[]{:S(2)}, u32[]{:S(2)}) async-start(f32[64,5,128]{2,1,0:T(8,128)} %pad_maximum_fusion), calls=%async_computation.1 | async-start | bytes 524288 | tf_op jit(solution)/shard_map/all_to_all | solution.py:140
  46.0 6.3 %collective-permute-start = (f32[2,512]{1,0:T(2,128)S(1)}, f32[2,512]{1,0:T(2,128)S(1)}, u32[]{:S(2)}, u32[]{:S(2)}) collective-permute-start(f32[2,512]{1,0:T(2,128)S(1)} %get-tuple-element.19), channel_id=1, source_target_pairs={{0,2},{1,3},{2,0},{3,1},{4,6},{5,7},{6,4},{7,5},{8,10},{9,11},{10,... | collective-permute-start | bytes 12296 | tf_op jit(solution)/shard_map/ppermute | solution.py:159
  49.1 4.8 %collective-permute-start.1 = (f32[2,512]{1,0:T(2,128)S(1)}, f32[2,512]{1,0:T(2,128)S(1)}, u32[]{:S(2)}, u32[]{:S(2)}) collective-permute-start(f32[2,512]{1,0:T(2,128)S(1)} %get-tuple-element.21), channel_id=1, source_target_pairs={{0,1},{1,2},{2,3},{3,0},{4,5},{5,6},{6,7},{7,4},{8,9},{9,10},{10,1... | collective-permute-start | bytes 12296 | tf_op jit(solution)/shard_map/ppermute | solution.py:159
  49.7 4.2 %collective-permute-start.2 = (f32[2,512]{1,0:T(2,128)S(1)}, f32[2,512]{1,0:T(2,128)S(1)}, u32[]{:S(2)}, u32[]{:S(2)}) collective-permute-start(f32[2,512]{1,0:T(2,128)S(1)} %get-tuple-element.20), channel_id=1, source_target_pairs={{0,3},{1,0},{2,1},{3,2},{4,7},{5,4},{6,5},{7,6},{8,11},{9,8},{10,9... | collective-permute-start | bytes 12296 | tf_op jit(solution)/shard_map/ppermute | solution.py:159

commit v15 on v12

--- a/solution.py
+++ b/solution.py
@@ -81,26 +81,29 @@
 
 def pack_slots(values, offsets, device, devices, capacity):
     requests = offsets.shape[0]
+    depth = 8
     index = jnp.arange(requests, dtype=jnp.int32)
-    slot_ids = jnp.arange(devices * capacity, dtype=jnp.int32)
-    amount = (slot_ids // capacity - device) % devices
-    second = (slot_ids % capacity) == 1
+    slot_ids = jnp.arange(devices * depth, dtype=jnp.int32)
+    amount = (slot_ids // depth - device) % devices
+    slot = slot_ids % depth
     same = offsets[:, None] == offsets[None, :]
     earlier = jnp.sum((same & (index[None, :] < index[:, None])).astype(jnp.int32), axis=1)
     match = (
         (offsets[None, :] == amount[:, None])
-        & (amount != 0)[:, None]
-        & ((earlier[None, :] == 1) == second[:, None])
+        & ((amount != 0) & (slot < capacity))[:, None]
+        & (earlier[None, :] == slot[:, None])
     )
-    return jnp.dot(match.astype(values.dtype), values, precision=lax.Precision.HIGHEST)
+    sent = jnp.dot(match.astype(values.dtype), values, precision=lax.Precision.HIGHEST)
+    return sent.reshape(devices, depth, -1)
 
 
 def unpack_slots(received, values, offsets, position, device, devices, capacity):
     source = (device - offsets) % devices
-    slots = source * capacity + jnp.minimum(position, capacity - 1)
+    depth = received.shape[1]
+    slots = source * depth + jnp.minimum(position, capacity - 1)
     moving = offsets != 0
-    flat = received.reshape(devices * capacity, -1)
-    picks = (slots[:, None] == jnp.arange(devices * capacity, dtype=jnp.int32)[None, :]) & moving[:, None]
+    flat = received.reshape(devices * depth, -1)
+    picks = (slots[:, None] == jnp.arange(devices * depth, dtype=jnp.int32)[None, :]) & moving[:, None]
     taken = jnp.dot(picks.astype(values.dtype), flat, precision=lax.Precision.HIGHEST)
     return taken + jnp.where(moving[:, None], jnp.zeros((), values.dtype), values)
 

time: 55 us -> 55.8 us (1.015)
  waiting for transfers between devices: 8.83 us -> 12.8 us
  starting transfers between devices: 20.8 us -> 18.2 us
  matrix products: 13.5 us -> 14.5 us
  local copies, waits for them, and re-layouts: 5.22 us -> 4.43 us
  other arithmetic: 5.86 us -> 5.19 us
    all_to_all x1, waiting for transfers between devices: 0.66 us -> 4.63 us  [body(): lax.all_to_all(outgoing, 'kv', split_axis=0, concat_axis=0, tiled=True)]
    all_to_all x1, starting transfers between devices: 6.74 us -> 4.06 us  [body(): lax.all_to_all(payload, 'kv', split_axis=0, concat_axis=0, tiled=True)]
    dot_general x1, matrix products: 1.21 us -> 2.17 us  [pack_slots(): jnp.dot(match.astype(values.dtype), values, precision=lax.Precision.HIGHEST)]
    all_to_all x2 -> x0, local copies, waits for them, and re-layouts: 0.8 us -> none  [body(): lax.all_to_all(outgoing, 'kv', split_axis=0, concat_axis=0, tiled=True)]
    add x1, other arithmetic: 0.67 us -> 0.01 us  [unpack_slots(): slots = source * depth + jnp.minimum(position, capacity - 1)]
  transfers between devices with their start and end apart: 5 -> 5, of which waited for: 4 -> 4; matrix products, arithmetic and copies ran while one was open for 18% -> 17% of each run, Pallas kernels for 0% -> 0%
where the time goes in v15:
time: 55.8 us; the launch traced here: 55.3 us
  starting transfers between devices  18.2 us (33%)
  matrix products  14.5 us (26%)
  waiting for transfers between devices  12.8 us (23%)
  other arithmetic  5.19 us (9%)
  local copies, waits for them, and re-layouts  4.43 us (8%)
    all_to_all x1, starting transfers between devices, body(): lax.all_to_all(outgoing, 'kv', split_axis=0, concat_axis=0, tiled=True)  8.42 us
    all_to_all x1, waiting for transfers between devices, body(): lax.all_to_all(payload, 'kv', split_axis=0, concat_axis=0, tiled=True)  6.01 us
    ppermute x3, starting transfers between devices, body(): total = total + lax.ppermute(piece, 'hd', pairs)  5.66 us
    dot_general x1, matrix products, raw_scores(): jnp.einsum('rhc,rbc->rhb', queries_h, block_data[..., :head_dim], preferr...  5.65 us
    all_to_all x1, waiting for transfers between devices, body(): lax.all_to_all(outgoing, 'kv', split_axis=0, concat_axis=0, tiled=True)  4.63 us
    dot_general x1, matrix products, block_partial(): jnp.einsum('rkb,rbc->rkc', rows, block_data[..., head_dim:], preferred_el...  4.58 us
    all_to_all x1, starting transfers between devices, body(): lax.all_to_all(payload, 'kv', split_axis=0, concat_axis=0, tiled=True)  4.06 us
    dot_general x1, local copies, waits for them, and re-layouts, body(): jnp.dot(attended, out_weight, preferred_element_type=jnp.float32)  2.87 us
  transfers between devices with their start and end apart: 5, of which 4 were waited for; matrix products, arithmetic and copies ran while one was open for 17% of the time, Pallas kernels for 0%

profile of v15, /device:TPU:0, one launch (start us, length us, event | category | flops | bytes accessed | tf_op | source)
XLA Modules:
  0.0 55.3 jit_solution(15728766968610970395)
XLA Ops:
  0.0 0.0 copy-start.2
  0.0 0.0 copy-start
  0.0 0.0 copy-start.1
  0.1 1.0 %shift-right-arithmetic_select_fusion = (s32[64,512]{1,0:T(8,128)S(1)}, s32[64,512]{1,0:T(8,128)S(1)}) fusion(s32[64,512]{1,0:T(8,128)} %param.9, s32[64]{0:T(128)} %bitcast.47), kind=kLoop, calls=%fused_computation.30 | loop fusion | flops 131072 | bytes 393472 | tf_op jit(solution)/shard_map/jit(_where)/select_n | solution.py:22
  1.1 1.1 %fusion.6 = pred[64,16,32]{2,1,0:T(8,128)(4,1)S(1)} fusion(s32[64,512]{1,0:T(8,128)S(1)} %get-tuple-element.16, s32[64,512]{1,0:T(8,128)S(1)} %get-tuple-element.15), kind=kOutput, calls=%fused_computation.9 | convolution fusion | flops 35160064 | bytes 294912 | tf_op jit(solution)/shard_map/rpa,rpb->rab/dot_general | solution.py:27
  2.1 0.3 copy.33
  2.4 0.1 copy.34
  2.6 0.9 %convert_reduce_fusion = s32[64]{0:T(128)S(1)} fusion(s32[64]{0:T(128)} %param.13), kind=kLoop, calls=%fused_computation.59 | loop fusion | flops 20416 | bytes 512 | tf_op jit(solution)/shard_map/reduce_sum | solution.py:78
  3.5 2.2 %convolution_bitcast_fusion = f32[32,8,512]{2,1,0:T(8,128)} fusion(f32[64,512]{1,0:T(8,128)} %param.11, pred[64,512]{1,0:T(32,128)(4,1)S(1)} %copy.34, s32[512]{0:T(512)S(1)} %iota_add_fusion, s32[64]{0:T(128)S(1)} %convert_reduce_fusion, s32[64]{0:T(128)} %param.13, s32[64]{0:T(128)} %param.12, s32[256]{0:T(256)S(1)} %get-tuple-element.26, ...), kind=kOutput, calls=%fused_computation.8 | convolution fusion | flops 100859904 | bytes 693248 | tf_op jit(solution)/shard_map/dot_general | solution.py:96
  5.7 8.4 %all-to-all-start = ((f32[32,8,512]{2,1,0:T(8,128)}), f32[32,8,512]{2,1,0:T(8,128)S(1)}, u32[]{:S(2)}, u32[]{:S(2)}) async-start(f32[32,8,512]{2,1,0:T(8,128)} %convolution_bitcast_fusion), calls=%async_computation | async-start | bytes 1048576 | tf_op jit(solution)/shard_map/all_to_all | solution.py:133
  14.1 0.9 %reshape.197 = bf16[64,4,128]{2,1,0:T(4,128)(2,1)S(1)} reshape(bf16[64,512]{1,0:T(8,128)(2,1)} %param.14) | data formatting | bytes 131072 | tf_op jit(solution)/shard_map/reshape | solution.py:136
  15.0 5.6 %fusion.7 = f32[64,4,512]{2,1,0:T(4,128)S(1)} fusion(bf16[64,4,128]{2,1,0:T(4,128)(2,1)S(1)} %reshape.197, bf16[64,512,256]{2,1,0:T(8,128)(2,1)} %param.8), kind=kOutput, calls=%fused_computation.10 | convolution fusion | flops 33685504 | bytes 8978432 | tf_op jit(solution)/shard_map/rhc,rbc->rhb/dot_general | solution.py:37
  20.6 0.0 copy-done.2
  20.6 4.6 %all-to-all-done = f32[32,8,512]{2,1,0:T(8,128)S(1)} async-done(((f32[32,8,512]{2,1,0:T(8,128)}), f32[32,8,512]{2,1,0:T(8,128)S(1)}, u32[]{:S(2)}, u32[]{:S(2)}) %all-to-all-start) | async-done | bytes 524320 | tf_op jit(solution)/shard_map/all_to_all | solution.py:133
  25.3 0.0 copy-done
  25.3 0.0 copy-done.1
  25.3 0.4 maximum_reduce_fusion
  25.8 0.1 fusion.55
  25.9 0.5 multiply_reduce_fusion
  26.3 0.1 fusion.39
  26.4 0.6 %fusion.16 = (bf16[64,4,512]{2,1,0:T(4,128)(2,1)S(1)}, f32[64,4]{1,0:T(8,128)S(1)}) fusion(f32[64,4,512]{2,1,0:T(4,128)S(1)} %fusion.7, f32[64,4]{1,0:T(8,128)S(1)} %fusion.39, pred[64,512]{1,0:T(8,128)(4,1)S(1)} %broadcast_compare_fusion), kind=kLoop, calls=%fused_computation.21 | loop fusion | flops 655104 | bytes 821248 | tf_op jit(solution)/shard_map/convert_element_type | solution.py:62
  27.0 0.1 copy.35
  27.1 4.6 %fusion = f32[64,5,128]{2,1,0:T(8,128)S(1)} fusion(bf16[64,512,256]{2,1,0:T(8,128)(2,1)} %param.8, bf16[64,4,512]{2,1,0:T(4,128)(2,1)S(1)} %get-tuple-element.11, bf16[64,1,512]{2,1,0:T(2,128)(2,1)S(1)} %copy.35), kind=kOutput, calls=%fused_computation | convolution fusion | flops 42598400 | bytes 8880128 | tf_op jit(solution)/shard_map/rkb,rbc->rkc/dot_general | solution.py:63
  31.7 0.1 convert_convert_fusion
  31.8 0.1 select_maximum_fusion
  31.9 0.1 slice_add_fusion
  32.0 0.8 %pad_maximum_fusion = f32[64,5,128]{2,1,0:T(8,128)} fusion(f32[64,1,128]{2,1,0:T(1,128)S(1)} %bitcast.46, f32[64,4,128]{2,1,0:T(4,128)S(1)} %slice_add_fusion), kind=kLoop, calls=%fused_computation.22 | loop fusion | flops 40960 | bytes 327680 | tf_op jit(solution)/shard_map/concatenate | solution.py:142
  32.8 4.1 %all-to-all-start.1 = ((f32[64,5,128]{2,1,0:T(8,128)}), f32[64,5,128]{2,1,0:T(8,128)S(1)}, u32[]{:S(2)}, u32[]{:S(2)}) async-start(f32[64,5,128]{2,1,0:T(8,128)} %pad_maximum_fusion), calls=%async_computation.1 | async-start | bytes 524288 | tf_op jit(solution)/shard_map/all_to_all | solution.py:143
  36.9 2.9 %copy.38 = bf16[2048,512]{1,0:T(8,128)(2,1)S(1)} copy(bf16[2048,512]{0,1:T(8,128)(2,1)} %bitcast.37) | data formatting | bytes 4194304 | tf_op jit(solution)/shard_map/dot_general | solution.py:153
  39.8 6.0 %all-to-all-done.1 = f32[64,5,128]{2,1,0:T(8,128)S(1)} async-done(((f32[64,5,128]{2,1,0:T(8,128)}), f32[64,5,128]{2,1,0:T(8,128)S(1)}, u32[]{:S(2)}, u32[]{:S(2)}) %all-to-all-start.1) | async-done | bytes 163872 | tf_op jit(solution)/shard_map/all_to_all | solution.py:143
  45.8 0.1 fusion.56
  46.0 0.1 multiply_reduce_fusion.1
  46.0 0.1 fusion.18
  46.2 0.1 divide_convert_fusion.1
  46.2 0.6 %fusion.57 = f32[2,4,512]{2,0,1:T(2,128)S(1)} fusion(bf16[2,512,1]{1,0,2:T(2,128)(2,1)S(1)} %reshape.200, bf16[4,512,512]{2,1,0:T(8,128)(2,1)S(1)} %bitcast.36), kind=kOutput, calls=%fused_computation.103 | convolution fusion | flops 4194304 | bytes 2115584 | tf_op jit(solution)/shard_map/dot_general | solution.py:153
  46.9 1.5 %collective-permute-start = (f32[2,512]{1,0:T(2,128)S(1)}, f32[2,512]{1,0:T(2,128)S(1)}, u32[]{:S(2)}, u32[]{:S(2)}) collective-permute-start(f32[2,512]{1,0:T(2,128)S(1)} %get-tuple-element.19), channel_id=1, source_target_pairs={{0,1},{1,2},{2,3},{3,0},{4,5},{5,6},{6,7},{7,4},{8,9},{9,10},{10,1... | collective-permute-start | bytes 12296 | tf_op jit(solution)/shard_map/ppermute | solution.py:162
  48.4 2.7 %collective-permute-start.1 = (f32[2,512]{1,0:T(2,128)S(1)}, f32[2,512]{1,0:T(2,128)S(1)}, u32[]{:S(2)}, u32[]{:S(2)}) collective-permute-start(f32[2,512]{1,0:T(2,128)S(1)} %get-tuple-element.21), channel_id=1, source_target_pairs={{0,2},{1,3},{2,0},{3,1},{4,6},{5,7},{6,4},{7,5},{8,10},{9,11},{10,... | collective-permute-start | bytes 12296 | tf_op jit(solution)/shard_map/ppermute | solution.py:162
  51.1 1.4 %collective-permute-start.2 = (f32[2,512]{1,0:T(2,128)S(1)}, f32[2,512]{1,0:T(2,128)S(1)}, u32[]{:S(2)}, u32[]{:S(2)}) collective-permute-start(f32[2,512]{1,0:T(2,128)S(1)} %get-tuple-element.20), channel_id=1, source_target_pairs={{0,3},{1,0},{2,1},{3,2},{4,7},{5,4},{6,5},{7,6},{8,11},{9,8},{10,9... | collective-permute-start | bytes 12296 | tf_op jit(solution)/shard_map/ppermute | solution.py:162
  52.6 0.0 collective-permute-done
  52.6 0.9 %collective-permute-done.1 = f32[2,512]{1,0:T(2,128)S(1)} collective-permute-done((f32[2,512]{1,0:T(2,128)S(1)}, f32[2,512]{1,0:T(2,128)S(1)}, u32[]{:S(2)}, u32[]{:S(2)}) %collective-permute-start.1) | collective-permute-done | bytes 4128 | tf_op jit(solution)/shard_map/ppermute | solution.py:162
  53.5 1.2 %collective-permute-done.2 = f32[2,512]{1,0:T(2,128)S(1)} collective-permute-done((f32[2,512]{1,0:T(2,128)S(1)}, f32[2,512]{1,0:T(2,128)S(1)}, u32[]{:S(2)}, u32[]{:S(2)}) %collective-permute-start.2) | collective-permute-done | bytes 4128 | tf_op jit(solution)/shard_map/ppermute | solution.py:162
  54.7 0.6 %fusion.42 = bf16[2,512]{1,0:T(2,128)(2,1)} fusion(f32[2,512]{1,0:T(2,128)S(1)} %collective-permute-done.2, f32[2,512]{1,0:T(2,128)S(1)} %collective-permute-done.1, f32[2,512]{1,0:T(2,128)S(1)} %collective-permute-done, f32[2,4,512]{2,0,1:T(2,128)S(1)} %fusion.57, s32[]{:T(128)S(6)} %select_n.125), kind=kLoop, calls=%fused_computation.68 | loop fusion | flops 4096 | bytes 18436 | tf_op jit(solution)/shard_map/convert_element_type | solution.py:163
  (12 shorter events, 0.2 us)
Async XLA Ops:
  0.0 20.6 %copy-start.2 = (s32[64]{0:T(128)S(1)}, s32[64]{0:T(128)}, u32[]{:S(2)}) copy-start(s32[64]{0:T(128)} %param.13) | copy-start | bytes 772
  0.0 25.3 %copy-start = (f32[64,512]{1,0:T(8,128)S(1)}, f32[64,512]{1,0:T(8,128)}, u32[]{:S(2)}) copy-start(f32[64,512]{1,0:T(8,128)} %param.11) | copy-start | bytes 393220
  0.0 25.3 %copy-start.1 = (s32[64]{0:T(128)S(1)}, s32[64]{0:T(128)}, u32[]{:S(2)}) copy-start(s32[64]{0:T(128)} %param.12) | copy-start | bytes 772
  5.7 19.6 %all-to-all-start = ((f32[32,8,512]{2,1,0:T(8,128)}), f32[32,8,512]{2,1,0:T(8,128)S(1)}, u32[]{:S(2)}, u32[]{:S(2)}) async-start(f32[32,8,512]{2,1,0:T(8,128)} %convolution_bitcast_fusion), calls=%async_computation | async-start | bytes 1048576 | tf_op jit(solution)/shard_map/all_to_all | solution.py:133
  32.8 13.0 %all-to-all-start.1 = ((f32[64,5,128]{2,1,0:T(8,128)}), f32[64,5,128]{2,1,0:T(8,128)S(1)}, u32[]{:S(2)}, u32[]{:S(2)}) async-start(f32[64,5,128]{2,1,0:T(8,128)} %pad_maximum_fusion), calls=%async_computation.1 | async-start | bytes 524288 | tf_op jit(solution)/shard_map/all_to_all | solution.py:143
  46.9 5.7 %collective-permute-start = (f32[2,512]{1,0:T(2,128)S(1)}, f32[2,512]{1,0:T(2,128)S(1)}, u32[]{:S(2)}, u32[]{:S(2)}) collective-permute-start(f32[2,512]{1,0:T(2,128)S(1)} %get-tuple-element.19), channel_id=1, source_target_pairs={{0,1},{1,2},{2,3},{3,0},{4,5},{5,6},{6,7},{7,4},{8,9},{9,10},{10,1... | collective-permute-start | bytes 12296 | tf_op jit(solution)/shard_map/ppermute | solution.py:162
  48.4 5.1 %collective-permute-start.1 = (f32[2,512]{1,0:T(2,128)S(1)}, f32[2,512]{1,0:T(2,128)S(1)}, u32[]{:S(2)}, u32[]{:S(2)}) collective-permute-start(f32[2,512]{1,0:T(2,128)S(1)} %get-tuple-element.21), channel_id=1, source_target_pairs={{0,2},{1,3},{2,0},{3,1},{4,6},{5,7},{6,4},{7,5},{8,10},{9,11},{10,... | collective-permute-start | bytes 12296 | tf_op jit(solution)/shard_map/ppermute | solution.py:162
  51.1 3.6 %collective-permute-start.2 = (f32[2,512]{1,0:T(2,128)S(1)}, f32[2,512]{1,0:T(2,128)S(1)}, u32[]{:S(2)}, u32[]{:S(2)}) collective-permute-start(f32[2,512]{1,0:T(2,128)S(1)} %get-tuple-element.20), channel_id=1, source_target_pairs={{0,3},{1,0},{2,1},{3,2},{4,7},{5,4},{6,5},{7,6},{8,11},{9,8},{10,9... | collective-permute-start | bytes 12296 | tf_op jit(solution)/shard_map/ppermute | solution.py:162

commit v16 on v12

--- a/solution.py
+++ b/solution.py
@@ -19,11 +19,11 @@
     low = 32
     high = block_rows // low
     places = jnp.arange(block_rows, dtype=jnp.int32)[None, :]
-    counted_hi = jnp.where(places < count_block[:, None], keep_block >> 5, -1)
-    upper = (counted_hi[..., None] == jnp.arange(high, dtype=jnp.int32)).astype(jnp.bfloat16)
-    lower = ((keep_block & (low - 1))[..., None] == jnp.arange(low, dtype=jnp.int32)).astype(
-        jnp.bfloat16
-    )
+    counted = (places < count_block[:, None])[..., None]
+    starts = low * jnp.arange(high, dtype=jnp.int32)
+    keep = keep_block[..., None]
+    upper = ((keep >= starts) & (keep < starts + low) & counted).astype(jnp.bfloat16)
+    lower = (((keep - jnp.arange(low, dtype=jnp.int32)) & (low - 1)) == 0).astype(jnp.bfloat16)
     kept = jnp.einsum("rpa,rpb->rab", upper, lower, preferred_element_type=jnp.float32)
     kept_rows = kept.reshape(requests, block_rows) > 0.5
     position = block_index * block_rows + jnp.arange(block_rows, dtype=jnp.int32)

time: 55 us -> 53.2 us (0.967)
  other arithmetic: 5.86 us -> 4.24 us
  starting transfers between devices: 20.8 us -> 19.3 us
  waiting for transfers between devices: 8.83 us -> 10.3 us
  local copies, waits for them, and re-layouts: 5.22 us -> 4.39 us
  matrix products: 13.5 us -> 14.2 us
    dot_general x1, matrix products: 1.05 us -> 2.65 us  [codes_for(): jnp.einsum('rpa,rpb->rab', upper, lower, preferred_element_type=jnp.float32)]
    all_to_all x1, waiting for transfers between devices: 0.66 us -> 2.16 us  [body(): lax.all_to_all(outgoing, 'kv', split_axis=0, concat_axis=0, tiled=True)]
    all_to_all x1, starting transfers between devices: 6.74 us -> 5.25 us  [body(): lax.all_to_all(payload, 'kv', split_axis=0, concat_axis=0, tiled=True)]
    select_n x1 -> x0, other arithmetic: 1.03 us -> none  [codes_for(): counted_hi = jnp.where(places < count_block[:, None], keep_block >> 5, -1)]
    dot_general x1, matrix products: 1.21 us -> 0.31 us  [pack_slots(): jnp.dot(match.astype(values.dtype), values, precision=lax.Precision.HIGHEST)]
    reshape x1, local copies, waits for them, and re-layouts: 0.86 us -> 0.02 us  [body(): queries_h = queries.reshape(requests, -1, head_dim)]
    lt x0 -> x1, other arithmetic: none -> 0.8 us  [codes_for(): counted = (places < count_block[:, None])[..., None]]
    reduce_sum x1, other arithmetic: 0.91 us -> 0.17 us  [route_tables(): jnp.sum((same & (index[None, :] < index[:, None])).astype(jnp.int32), axi...]
  transfers between devices with their start and end apart: 5 -> 5, of which waited for: 4 -> 4; matrix products, arithmetic and copies ran while one was open for 18% -> 16% of each run, Pallas kernels for 0% -> 0%
where the time goes in v16:
time: 53.2 us; the launch traced here: 52.7 us
  starting transfers between devices  19.3 us (36%)
  matrix products  14.2 us (27%)
  waiting for transfers between devices  10.3 us (19%)
  local copies, waits for them, and re-layouts  4.39 us (8%)
  other arithmetic  4.24 us (8%)
    all_to_all x1, starting transfers between devices, body(): lax.all_to_all(outgoing, 'kv', split_axis=0, concat_axis=0, tiled=True)  8.42 us
    all_to_all x1, waiting for transfers between devices, body(): lax.all_to_all(payload, 'kv', split_axis=0, concat_axis=0, tiled=True)  6.01 us
    ppermute x3, starting transfers between devices, body(): total = total + lax.ppermute(piece, 'hd', pairs)  5.67 us
    dot_general x1, matrix products, raw_scores(): jnp.einsum('rhc,rbc->rhb', queries_h, block_data[..., :head_dim], preferr...  5.65 us
    all_to_all x1, starting transfers between devices, body(): lax.all_to_all(payload, 'kv', split_axis=0, concat_axis=0, tiled=True)  5.25 us
    dot_general x1, matrix products, block_partial(): jnp.einsum('rkb,rbc->rkc', rows, block_data[..., head_dim:], preferred_el...  4.58 us
    dot_general x1, local copies, waits for them, and re-layouts, body(): jnp.dot(attended, out_weight, preferred_element_type=jnp.float32)  2.87 us
    dot_general x1, matrix products, codes_for(): jnp.einsum('rpa,rpb->rab', upper, lower, preferred_element_type=jnp.float32)  2.65 us
  transfers between devices with their start and end apart: 5, of which 4 were waited for; matrix products, arithmetic and copies ran while one was open for 16% of the time, Pallas kernels for 0%

profile of v16, /device:TPU:0, one launch (start us, length us, event | category | flops | bytes accessed | tf_op | source)
XLA Modules:
  0.0 52.7 jit_solution(14993113835013261344)
XLA Ops:
  0.0 0.0 copy-start.3
  0.0 0.0 copy-start
  0.0 0.0 copy-start.2
  0.0 0.0 copy-start.1
  0.1 0.8 %iota_compare_fusion = pred[64,512]{1,0:T(8,128)(4,1)S(1)} fusion(s32[64]{0:T(128)} %bitcast.41), kind=kLoop, calls=%fused_computation.36 | loop fusion | flops 32768 | bytes 33024 | tf_op jit(solution)/shard_map/lt | solution.py:22
  0.9 2.7 %fusion.15 = pred[64,16,32]{2,1,0:T(8,128)(4,1)S(1)} fusion(s32[64,512]{1,0:T(8,128)} %param.9, s32[16]{0:T(128)S(1)} %get-tuple-element.25, s32[16]{0:T(128)S(1)} %get-tuple-element.24, pred[64,512]{1,0:T(8,128)(4,1)S(1)} %iota_compare_fusion), kind=kOutput, calls=%fused_computation.14 | convolution fusion | flops 38830080 | bytes 196736 | tf_op jit(solution)/shard_map/rpa,rpb->rab/dot_general | solution.py:27
  3.5 0.3 copy.33
  3.8 0.1 copy.34
  4.0 0.0 copy-done.3
  4.0 0.2 convert_reduce_fusion
  4.2 0.0 copy-done
  4.2 0.0 copy-done.2
  4.2 0.3 fusion.29
  4.5 0.7 %all_to_all.11 = f32[32,2,512]{2,1,0:T(2,128)} reshape(f32[64,512]{1,0:T(8,128)S(1)} %fusion.29) | data formatting | bytes 262144 | tf_op jit(solution)/shard_map/all_to_all | solution.py:130
  5.2 8.4 %all-to-all-start = ((f32[32,2,512]{2,1,0:T(2,128)}), f32[32,2,512]{2,1,0:T(2,128)S(1)}, u32[]{:S(2)}, u32[]{:S(2)}) async-start(f32[32,2,512]{2,1,0:T(2,128)} %all_to_all.11), calls=%async_computation | async-start | bytes 262144 | tf_op jit(solution)/shard_map/all_to_all | solution.py:130
  13.7 0.0 copy-done.1
  13.7 5.6 %fusion.12 = f32[64,4,512]{2,1,0:T(4,128)S(1)} fusion(bf16[64,4,128]{2,1,0:T(4,128)(2,1)S(1)} %reshape.220, bf16[64,512,256]{2,1,0:T(8,128)(2,1)} %param.8), kind=kOutput, calls=%fused_computation.13 | convolution fusion | flops 33685504 | bytes 8978432 | tf_op jit(solution)/shard_map/rhc,rbc->rhb/dot_general | solution.py:37
  19.3 2.2 %all-to-all-done = f32[32,2,512]{2,1,0:T(2,128)S(1)} async-done(((f32[32,2,512]{2,1,0:T(2,128)}), f32[32,2,512]{2,1,0:T(2,128)S(1)}, u32[]{:S(2)}, u32[]{:S(2)}) %all-to-all-start) | async-done | bytes 131104 | tf_op jit(solution)/shard_map/all_to_all | solution.py:130
  21.5 0.1 all_to_all.13
  21.6 0.4 maximum_reduce_fusion
  22.0 0.1 fusion.67
  22.1 0.5 multiply_reduce_fusion
  22.6 0.1 fusion.43
  22.6 0.6 %fusion.26 = (bf16[64,4,512]{2,1,0:T(4,128)(2,1)S(1)}, f32[64,4]{1,0:T(8,128)S(1)}) fusion(f32[64,4,512]{2,1,0:T(4,128)S(1)} %fusion.12, f32[64,4]{1,0:T(8,128)S(1)} %fusion.43, pred[64,512]{1,0:T(8,128)(4,1)S(1)} %broadcast_compare_fusion), kind=kLoop, calls=%fused_computation.27 | loop fusion | flops 655104 | bytes 821248 | tf_op jit(solution)/shard_map/convert_element_type | solution.py:62
  23.2 0.1 copy.35
  23.3 4.6 %fusion = f32[64,5,128]{2,1,0:T(8,128)S(1)} fusion(bf16[64,512,256]{2,1,0:T(8,128)(2,1)} %param.8, bf16[64,4,512]{2,1,0:T(4,128)(2,1)S(1)} %get-tuple-element.11, bf16[64,1,512]{2,1,0:T(2,128)(2,1)S(1)} %copy.35), kind=kOutput, calls=%fused_computation | convolution fusion | flops 42598400 | bytes 8880128 | tf_op jit(solution)/shard_map/rkb,rbc->rkc/dot_general | solution.py:63
  27.9 0.1 convert_convert_fusion
  28.0 0.1 select_maximum_fusion
  28.1 0.1 slice_add_fusion
  28.2 0.8 %pad_maximum_fusion = f32[64,5,128]{2,1,0:T(8,128)} fusion(f32[64,1,128]{2,1,0:T(1,128)S(1)} %bitcast.40, f32[64,4,128]{2,1,0:T(4,128)S(1)} %slice_add_fusion), kind=kLoop, calls=%fused_computation.28 | loop fusion | flops 40960 | bytes 327680 | tf_op jit(solution)/shard_map/concatenate | solution.py:139
  29.0 5.3 %all-to-all-start.1 = ((f32[64,5,128]{2,1,0:T(8,128)}), f32[64,5,128]{2,1,0:T(8,128)S(1)}, u32[]{:S(2)}, u32[]{:S(2)}) async-start(f32[64,5,128]{2,1,0:T(8,128)} %pad_maximum_fusion), calls=%async_computation.1 | async-start | bytes 524288 | tf_op jit(solution)/shard_map/all_to_all | solution.py:140
  34.3 2.9 %copy.38 = bf16[2048,512]{1,0:T(8,128)(2,1)S(1)} copy(bf16[2048,512]{0,1:T(8,128)(2,1)} %bitcast.31) | data formatting | bytes 4194304 | tf_op jit(solution)/shard_map/dot_general | solution.py:150
  37.2 6.0 %all-to-all-done.1 = f32[64,5,128]{2,1,0:T(8,128)S(1)} async-done(((f32[64,5,128]{2,1,0:T(8,128)}), f32[64,5,128]{2,1,0:T(8,128)S(1)}, u32[]{:S(2)}, u32[]{:S(2)}) %all-to-all-start.1) | async-done | bytes 163872 | tf_op jit(solution)/shard_map/all_to_all | solution.py:140
  43.2 0.1 fusion.68
  43.4 0.1 multiply_reduce_fusion.1
  43.4 0.1 fusion.28
  43.6 0.1 divide_convert_fusion.1
  43.7 0.6 %fusion.69 = f32[2,4,512]{2,0,1:T(2,128)S(1)} fusion(bf16[2,512,1]{1,0,2:T(2,128)(2,1)S(1)} %reshape.223, bf16[4,512,512]{2,1,0:T(8,128)(2,1)S(1)} %bitcast.30), kind=kOutput, calls=%fused_computation.112 | convolution fusion | flops 4194304 | bytes 2115584 | tf_op jit(solution)/shard_map/dot_general | solution.py:150
  44.3 1.5 %collective-permute-start = (f32[2,512]{1,0:T(2,128)S(1)}, f32[2,512]{1,0:T(2,128)S(1)}, u32[]{:S(2)}, u32[]{:S(2)}) collective-permute-start(f32[2,512]{1,0:T(2,128)S(1)} %get-tuple-element.17), channel_id=1, source_target_pairs={{0,1},{1,2},{2,3},{3,0},{4,5},{5,6},{6,7},{7,4},{8,9},{9,10},{10,1... | collective-permute-start | bytes 12296 | tf_op jit(solution)/shard_map/ppermute | solution.py:159
  45.8 2.7 %collective-permute-start.1 = (f32[2,512]{1,0:T(2,128)S(1)}, f32[2,512]{1,0:T(2,128)S(1)}, u32[]{:S(2)}, u32[]{:S(2)}) collective-permute-start(f32[2,512]{1,0:T(2,128)S(1)} %get-tuple-element.19), channel_id=1, source_target_pairs={{0,2},{1,3},{2,0},{3,1},{4,6},{5,7},{6,4},{7,5},{8,10},{9,11},{10,... | collective-permute-start | bytes 12296 | tf_op jit(solution)/shard_map/ppermute | solution.py:159
  48.6 1.4 %collective-permute-start.2 = (f32[2,512]{1,0:T(2,128)S(1)}, f32[2,512]{1,0:T(2,128)S(1)}, u32[]{:S(2)}, u32[]{:S(2)}) collective-permute-start(f32[2,512]{1,0:T(2,128)S(1)} %get-tuple-element.18), channel_id=1, source_target_pairs={{0,3},{1,0},{2,1},{3,2},{4,7},{5,4},{6,5},{7,6},{8,11},{9,8},{10,9... | collective-permute-start | bytes 12296 | tf_op jit(solution)/shard_map/ppermute | solution.py:159
  50.0 0.0 collective-permute-done
  50.0 0.9 %collective-permute-done.1 = f32[2,512]{1,0:T(2,128)S(1)} collective-permute-done((f32[2,512]{1,0:T(2,128)S(1)}, f32[2,512]{1,0:T(2,128)S(1)}, u32[]{:S(2)}, u32[]{:S(2)}) %collective-permute-start.1) | collective-permute-done | bytes 4128 | tf_op jit(solution)/shard_map/ppermute | solution.py:159
  50.9 1.2 %collective-permute-done.2 = f32[2,512]{1,0:T(2,128)S(1)} collective-permute-done((f32[2,512]{1,0:T(2,128)S(1)}, f32[2,512]{1,0:T(2,128)S(1)}, u32[]{:S(2)}, u32[]{:S(2)}) %collective-permute-start.2) | collective-permute-done | bytes 4128 | tf_op jit(solution)/shard_map/ppermute | solution.py:159
  52.2 0.6 %fusion.53 = bf16[2,512]{1,0:T(2,128)(2,1)} fusion(f32[2,512]{1,0:T(2,128)S(1)} %collective-permute-done.2, f32[2,512]{1,0:T(2,128)S(1)} %collective-permute-done.1, f32[2,512]{1,0:T(2,128)S(1)} %collective-permute-done, f32[2,4,512]{2,0,1:T(2,128)S(1)} %fusion.69, s32[]{:T(128)S(6)} %select_n.113), kind=kLoop, calls=%fused_computation.73 | loop fusion | flops 4096 | bytes 18436 | tf_op jit(solution)/shard_map/convert_element_type | solution.py:160
  (15 shorter events, 0.2 us)
Async XLA Ops:
  0.0 4.0 %copy-start.3 = (s32[64]{0:T(128)S(1)}, s32[64]{0:T(128)}, u32[]{:S(2)}) copy-start(s32[64]{0:T(128)} %param.13) | copy-start | bytes 772
  0.0 4.2 %copy-start = (f32[64,512]{1,0:T(8,128)S(1)}, f32[64,512]{1,0:T(8,128)}, u32[]{:S(2)}) copy-start(f32[64,512]{1,0:T(8,128)} %param.11) | copy-start | bytes 393220
  0.0 4.2 %copy-start.2 = (s32[64]{0:T(128)S(1)}, s32[64]{0:T(128)}, u32[]{:S(2)}) copy-start(s32[64]{0:T(128)} %param.12) | copy-start | bytes 772
  0.0 13.6 %copy-start.1 = (bf16[64,512]{1,0:T(8,128)(2,1)S(1)}, bf16[64,512]{1,0:T(8,128)(2,1)}, u32[]{:S(2)}) copy-start(bf16[64,512]{1,0:T(8,128)(2,1)} %param.14) | copy-start | bytes 196612
  5.2 16.3 %all-to-all-start = ((f32[32,2,512]{2,1,0:T(2,128)}), f32[32,2,512]{2,1,0:T(2,128)S(1)}, u32[]{:S(2)}, u32[]{:S(2)}) async-start(f32[32,2,512]{2,1,0:T(2,128)} %all_to_all.11), calls=%async_computation | async-start | bytes 262144 | tf_op jit(solution)/shard_map/all_to_all | solution.py:130
  29.0 14.2 %all-to-all-start.1 = ((f32[64,5,128]{2,1,0:T(8,128)}), f32[64,5,128]{2,1,0:T(8,128)S(1)}, u32[]{:S(2)}, u32[]{:S(2)}) async-start(f32[64,5,128]{2,1,0:T(8,128)} %pad_maximum_fusion), calls=%async_computation.1 | async-start | bytes 524288 | tf_op jit(solution)/shard_map/all_to_all | solution.py:140
  44.3 5.7 %collective-permute-start = (f32[2,512]{1,0:T(2,128)S(1)}, f32[2,512]{1,0:T(2,128)S(1)}, u32[]{:S(2)}, u32[]{:S(2)}) collective-permute-start(f32[2,512]{1,0:T(2,128)S(1)} %get-tuple-element.17), channel_id=1, source_target_pairs={{0,1},{1,2},{2,3},{3,0},{4,5},{5,6},{6,7},{7,4},{8,9},{9,10},{10,1... | collective-permute-start | bytes 12296 | tf_op jit(solution)/shard_map/ppermute | solution.py:159
  45.8 5.1 %collective-permute-start.1 = (f32[2,512]{1,0:T(2,128)S(1)}, f32[2,512]{1,0:T(2,128)S(1)}, u32[]{:S(2)}, u32[]{:S(2)}) collective-permute-start(f32[2,512]{1,0:T(2,128)S(1)} %get-tuple-element.19), channel_id=1, source_target_pairs={{0,2},{1,3},{2,0},{3,1},{4,6},{5,7},{6,4},{7,5},{8,10},{9,11},{10,... | collective-permute-start | bytes 12296 | tf_op jit(solution)/shard_map/ppermute | solution.py:159
  48.6 3.6 %collective-permute-start.2 = (f32[2,512]{1,0:T(2,128)S(1)}, f32[2,512]{1,0:T(2,128)S(1)}, u32[]{:S(2)}, u32[]{:S(2)}) collective-permute-start(f32[2,512]{1,0:T(2,128)S(1)} %get-tuple-element.18), channel_id=1, source_target_pairs={{0,3},{1,0},{2,1},{3,2},{4,7},{5,4},{6,5},{7,6},{8,11},{9,8},{10,9... | collective-permute-start | bytes 12296 | tf_op jit(solution)/shard_map/ppermute | solution.py:159

commit v17 on v16

--- a/solution.py
+++ b/solution.py
@@ -97,10 +97,14 @@
 
 def unpack_slots(received, values, offsets, position, device, devices, capacity):
     source = (device - offsets) % devices
-    slots = source * capacity + jnp.minimum(position, capacity - 1)
     moving = offsets != 0
     flat = received.reshape(devices * capacity, -1)
-    picks = (slots[:, None] == jnp.arange(devices * capacity, dtype=jnp.int32)[None, :]) & moving[:, None]
+    slot_ids = jnp.arange(devices * capacity, dtype=jnp.int32)[None, :]
+    picks = (
+        (source[:, None] == slot_ids // capacity)
+        & ((position[:, None] == 1) == (slot_ids % capacity == 1))
+        & moving[:, None]
+    )
     taken = jnp.dot(picks.astype(values.dtype), flat, precision=lax.Precision.HIGHEST)
     return taken + jnp.where(moving[:, None], jnp.zeros((), values.dtype), values)
 

time: 53.2 us -> 53.2 us (level)
  no operation moved by 1% of the time
where the time goes in v17:
time: 53.2 us; the launch traced here: 52.8 us
  starting transfers between devices  19.3 us (36%)
  matrix products  14.2 us (27%)
  waiting for transfers between devices  10.3 us (19%)
  local copies, waits for them, and re-layouts  4.39 us (8%)
  other arithmetic  4.23 us (8%)
    all_to_all x1, starting transfers between devices, body(): lax.all_to_all(outgoing, 'kv', split_axis=0, concat_axis=0, tiled=True)  8.42 us
    all_to_all x1, waiting for transfers between devices, body(): lax.all_to_all(payload, 'kv', split_axis=0, concat_axis=0, tiled=True)  6.01 us
    ppermute x3, starting transfers between devices, body(): total = total + lax.ppermute(piece, 'hd', pairs)  5.67 us
    dot_general x1, matrix products, raw_scores(): jnp.einsum('rhc,rbc->rhb', queries_h, block_data[..., :head_dim], preferr...  5.65 us
    all_to_all x1, starting transfers between devices, body(): lax.all_to_all(payload, 'kv', split_axis=0, concat_axis=0, tiled=True)  5.25 us
    dot_general x1, matrix products, block_partial(): jnp.einsum('rkb,rbc->rkc', rows, block_data[..., head_dim:], preferred_el...  4.58 us
    dot_general x1, local copies, waits for them, and re-layouts, body(): jnp.dot(attended, out_weight, preferred_element_type=jnp.float32)  2.87 us
    dot_general x1, matrix products, codes_for(): jnp.einsum('rpa,rpb->rab', upper, lower, preferred_element_type=jnp.float32)  2.65 us
  transfers between devices with their start and end apart: 5, of which 4 were waited for; matrix products, arithmetic and copies ran while one was open for 16% of the time, Pallas kernels for 0%

profile of v17, /device:TPU:0, one launch (start us, length us, event | category | flops | bytes accessed | tf_op | source)
XLA Modules:
  0.0 52.8 jit_solution(3951394847880178552)
XLA Ops:
  0.0 0.0 copy-start.2
  0.0 0.0 copy-start
  0.0 0.0 copy-start.3
  0.0 0.0 copy-start.1
  0.1 0.8 %iota_compare_fusion = pred[64,512]{1,0:T(8,128)(4,1)S(1)} fusion(s32[64]{0:T(128)} %bitcast.41), kind=kLoop, calls=%fused_computation.36 | loop fusion | flops 32768 | bytes 33024 | tf_op jit(solution)/shard_map/lt | solution.py:22
  0.9 2.7 %fusion.15 = pred[64,16,32]{2,1,0:T(8,128)(4,1)S(1)} fusion(s32[64,512]{1,0:T(8,128)} %param.9, s32[16]{0:T(128)S(1)} %get-tuple-element.25, s32[16]{0:T(128)S(1)} %get-tuple-element.24, pred[64,512]{1,0:T(8,128)(4,1)S(1)} %iota_compare_fusion), kind=kOutput, calls=%fused_computation.14 | convolution fusion | flops 38830080 | bytes 196736 | tf_op jit(solution)/shard_map/rpa,rpb->rab/dot_general | solution.py:27
  3.5 0.3 copy.33
  3.8 0.1 copy.34
  4.0 0.0 copy-done.2
  4.0 0.2 convert_reduce_fusion
  4.2 0.0 copy-done
  4.2 0.0 copy-done.3
  4.2 0.3 fusion.29
  4.5 0.7 %all_to_all.11 = f32[32,2,512]{2,1,0:T(2,128)} reshape(f32[64,512]{1,0:T(8,128)S(1)} %fusion.29) | data formatting | bytes 262144 | tf_op jit(solution)/shard_map/all_to_all | solution.py:134
  5.2 8.4 %all-to-all-start = ((f32[32,2,512]{2,1,0:T(2,128)}), f32[32,2,512]{2,1,0:T(2,128)S(1)}, u32[]{:S(2)}, u32[]{:S(2)}) async-start(f32[32,2,512]{2,1,0:T(2,128)} %all_to_all.11), calls=%async_computation | async-start | bytes 262144 | tf_op jit(solution)/shard_map/all_to_all | solution.py:134
  13.7 0.0 copy-done.1
  13.7 5.6 %fusion.12 = f32[64,4,512]{2,1,0:T(4,128)S(1)} fusion(bf16[64,4,128]{2,1,0:T(4,128)(2,1)S(1)} %reshape.278, bf16[64,512,256]{2,1,0:T(8,128)(2,1)} %param.8), kind=kOutput, calls=%fused_computation.13 | convolution fusion | flops 33685504 | bytes 8978432 | tf_op jit(solution)/shard_map/rhc,rbc->rhb/dot_general | solution.py:37
  19.3 2.2 %all-to-all-done = f32[32,2,512]{2,1,0:T(2,128)S(1)} async-done(((f32[32,2,512]{2,1,0:T(2,128)}), f32[32,2,512]{2,1,0:T(2,128)S(1)}, u32[]{:S(2)}, u32[]{:S(2)}) %all-to-all-start) | async-done | bytes 131104 | tf_op jit(solution)/shard_map/all_to_all | solution.py:134
  21.5 0.1 all_to_all.13
  21.6 0.4 maximum_reduce_fusion
  22.0 0.1 fusion.69
  22.1 0.5 multiply_reduce_fusion
  22.6 0.1 fusion.45
  22.6 0.6 %fusion.26 = (bf16[64,4,512]{2,1,0:T(4,128)(2,1)S(1)}, f32[64,4]{1,0:T(8,128)S(1)}) fusion(f32[64,4,512]{2,1,0:T(4,128)S(1)} %fusion.12, f32[64,4]{1,0:T(8,128)S(1)} %fusion.45, pred[64,512]{1,0:T(8,128)(4,1)S(1)} %broadcast_compare_fusion), kind=kLoop, calls=%fused_computation.27 | loop fusion | flops 655104 | bytes 821248 | tf_op jit(solution)/shard_map/convert_element_type | solution.py:62
  23.2 0.1 copy.35
  23.3 4.6 %fusion = f32[64,5,128]{2,1,0:T(8,128)S(1)} fusion(bf16[64,512,256]{2,1,0:T(8,128)(2,1)} %param.8, bf16[64,4,512]{2,1,0:T(4,128)(2,1)S(1)} %get-tuple-element.11, bf16[64,1,512]{2,1,0:T(2,128)(2,1)S(1)} %copy.35), kind=kOutput, calls=%fused_computation | convolution fusion | flops 42598400 | bytes 8880128 | tf_op jit(solution)/shard_map/rkb,rbc->rkc/dot_general | solution.py:63
  27.9 0.1 convert_convert_fusion
  28.0 0.1 select_maximum_fusion
  28.1 0.1 slice_add_fusion
  28.2 0.8 %pad_maximum_fusion = f32[64,5,128]{2,1,0:T(8,128)} fusion(f32[64,1,128]{2,1,0:T(1,128)S(1)} %bitcast.40, f32[64,4,128]{2,1,0:T(4,128)S(1)} %slice_add_fusion), kind=kLoop, calls=%fused_computation.28 | loop fusion | flops 40960 | bytes 327680 | tf_op jit(solution)/shard_map/concatenate | solution.py:143
  29.0 5.3 %all-to-all-start.1 = ((f32[64,5,128]{2,1,0:T(8,128)}), f32[64,5,128]{2,1,0:T(8,128)S(1)}, u32[]{:S(2)}, u32[]{:S(2)}) async-start(f32[64,5,128]{2,1,0:T(8,128)} %pad_maximum_fusion), calls=%async_computation.1 | async-start | bytes 524288 | tf_op jit(solution)/shard_map/all_to_all | solution.py:144
  34.3 2.9 %copy.38 = bf16[2048,512]{1,0:T(8,128)(2,1)S(1)} copy(bf16[2048,512]{0,1:T(8,128)(2,1)} %bitcast.31) | data formatting | bytes 4194304 | tf_op jit(solution)/shard_map/dot_general | solution.py:154
  37.2 6.0 %all-to-all-done.1 = f32[64,5,128]{2,1,0:T(8,128)S(1)} async-done(((f32[64,5,128]{2,1,0:T(8,128)}), f32[64,5,128]{2,1,0:T(8,128)S(1)}, u32[]{:S(2)}, u32[]{:S(2)}) %all-to-all-start.1) | async-done | bytes 163872 | tf_op jit(solution)/shard_map/all_to_all | solution.py:144
  43.2 0.1 fusion.70
  43.4 0.1 multiply_reduce_fusion.1
  43.4 0.1 fusion.28
  43.6 0.1 divide_convert_fusion.1
  43.7 0.6 %fusion.71 = f32[2,4,512]{2,0,1:T(2,128)S(1)} fusion(bf16[2,512,1]{1,0,2:T(2,128)(2,1)S(1)} %reshape.281, bf16[4,512,512]{2,1,0:T(8,128)(2,1)S(1)} %bitcast.30), kind=kOutput, calls=%fused_computation.114 | convolution fusion | flops 4194304 | bytes 2115584 | tf_op jit(solution)/shard_map/dot_general | solution.py:154
  44.3 1.5 %collective-permute-start = (f32[2,512]{1,0:T(2,128)S(1)}, f32[2,512]{1,0:T(2,128)S(1)}, u32[]{:S(2)}, u32[]{:S(2)}) collective-permute-start(f32[2,512]{1,0:T(2,128)S(1)} %get-tuple-element.17), channel_id=1, source_target_pairs={{0,1},{1,2},{2,3},{3,0},{4,5},{5,6},{6,7},{7,4},{8,9},{9,10},{10,1... | collective-permute-start | bytes 12296 | tf_op jit(solution)/shard_map/ppermute | solution.py:163
  45.8 2.7 %collective-permute-start.1 = (f32[2,512]{1,0:T(2,128)S(1)}, f32[2,512]{1,0:T(2,128)S(1)}, u32[]{:S(2)}, u32[]{:S(2)}) collective-permute-start(f32[2,512]{1,0:T(2,128)S(1)} %get-tuple-element.19), channel_id=1, source_target_pairs={{0,2},{1,3},{2,0},{3,1},{4,6},{5,7},{6,4},{7,5},{8,10},{9,11},{10,... | collective-permute-start | bytes 12296 | tf_op jit(solution)/shard_map/ppermute | solution.py:163
  48.6 1.4 %collective-permute-start.2 = (f32[2,512]{1,0:T(2,128)S(1)}, f32[2,512]{1,0:T(2,128)S(1)}, u32[]{:S(2)}, u32[]{:S(2)}) collective-permute-start(f32[2,512]{1,0:T(2,128)S(1)} %get-tuple-element.18), channel_id=1, source_target_pairs={{0,3},{1,0},{2,1},{3,2},{4,7},{5,4},{6,5},{7,6},{8,11},{9,8},{10,9... | collective-permute-start | bytes 12296 | tf_op jit(solution)/shard_map/ppermute | solution.py:163
  50.0 0.0 collective-permute-done
  50.0 0.9 %collective-permute-done.1 = f32[2,512]{1,0:T(2,128)S(1)} collective-permute-done((f32[2,512]{1,0:T(2,128)S(1)}, f32[2,512]{1,0:T(2,128)S(1)}, u32[]{:S(2)}, u32[]{:S(2)}) %collective-permute-start.1) | collective-permute-done | bytes 4128 | tf_op jit(solution)/shard_map/ppermute | solution.py:163
  50.9 1.2 %collective-permute-done.2 = f32[2,512]{1,0:T(2,128)S(1)} collective-permute-done((f32[2,512]{1,0:T(2,128)S(1)}, f32[2,512]{1,0:T(2,128)S(1)}, u32[]{:S(2)}, u32[]{:S(2)}) %collective-permute-start.2) | collective-permute-done | bytes 4128 | tf_op jit(solution)/shard_map/ppermute | solution.py:163
  52.2 0.6 %fusion.58 = bf16[2,512]{1,0:T(2,128)(2,1)} fusion(f32[2,512]{1,0:T(2,128)S(1)} %collective-permute-done.2, f32[2,512]{1,0:T(2,128)S(1)} %collective-permute-done.1, f32[2,512]{1,0:T(2,128)S(1)} %collective-permute-done, f32[2,4,512]{2,0,1:T(2,128)S(1)} %fusion.71, s32[]{:T(128)S(6)} %select_n.134), kind=kLoop, calls=%fused_computation.78 | loop fusion | flops 4096 | bytes 18436 | tf_op jit(solution)/shard_map/convert_element_type | solution.py:164
  (15 shorter events, 0.2 us)
Async XLA Ops:
  0.0 4.0 %copy-start.2 = (s32[64]{0:T(128)S(1)}, s32[64]{0:T(128)}, u32[]{:S(2)}) copy-start(s32[64]{0:T(128)} %param.13) | copy-start | bytes 772
  0.0 4.2 %copy-start = (f32[64,512]{1,0:T(8,128)S(1)}, f32[64,512]{1,0:T(8,128)}, u32[]{:S(2)}) copy-start(f32[64,512]{1,0:T(8,128)} %param.11) | copy-start | bytes 393220
  0.0 4.2 %copy-start.3 = (s32[64]{0:T(128)S(1)}, s32[64]{0:T(128)}, u32[]{:S(2)}) copy-start(s32[64]{0:T(128)} %param.12) | copy-start | bytes 772
  0.0 13.6 %copy-start.1 = (bf16[64,512]{1,0:T(8,128)(2,1)S(1)}, bf16[64,512]{1,0:T(8,128)(2,1)}, u32[]{:S(2)}) copy-start(bf16[64,512]{1,0:T(8,128)(2,1)} %param.14) | copy-start | bytes 196612
  5.2 16.3 %all-to-all-start = ((f32[32,2,512]{2,1,0:T(2,128)}), f32[32,2,512]{2,1,0:T(2,128)S(1)}, u32[]{:S(2)}, u32[]{:S(2)}) async-start(f32[32,2,512]{2,1,0:T(2,128)} %all_to_all.11), calls=%async_computation | async-start | bytes 262144 | tf_op jit(solution)/shard_map/all_to_all | solution.py:134
  29.0 14.2 %all-to-all-start.1 = ((f32[64,5,128]{2,1,0:T(8,128)}), f32[64,5,128]{2,1,0:T(8,128)S(1)}, u32[]{:S(2)}, u32[]{:S(2)}) async-start(f32[64,5,128]{2,1,0:T(8,128)} %pad_maximum_fusion), calls=%async_computation.1 | async-start | bytes 524288 | tf_op jit(solution)/shard_map/all_to_all | solution.py:144
  44.3 5.7 %collective-permute-start = (f32[2,512]{1,0:T(2,128)S(1)}, f32[2,512]{1,0:T(2,128)S(1)}, u32[]{:S(2)}, u32[]{:S(2)}) collective-permute-start(f32[2,512]{1,0:T(2,128)S(1)} %get-tuple-element.17), channel_id=1, source_target_pairs={{0,1},{1,2},{2,3},{3,0},{4,5},{5,6},{6,7},{7,4},{8,9},{9,10},{10,1... | collective-permute-start | bytes 12296 | tf_op jit(solution)/shard_map/ppermute | solution.py:163
  45.8 5.1 %collective-permute-start.1 = (f32[2,512]{1,0:T(2,128)S(1)}, f32[2,512]{1,0:T(2,128)S(1)}, u32[]{:S(2)}, u32[]{:S(2)}) collective-permute-start(f32[2,512]{1,0:T(2,128)S(1)} %get-tuple-element.19), channel_id=1, source_target_pairs={{0,2},{1,3},{2,0},{3,1},{4,6},{5,7},{6,4},{7,5},{8,10},{9,11},{10,... | collective-permute-start | bytes 12296 | tf_op jit(solution)/shard_map/ppermute | solution.py:163
  48.6 3.6 %collective-permute-start.2 = (f32[2,512]{1,0:T(2,128)S(1)}, f32[2,512]{1,0:T(2,128)S(1)}, u32[]{:S(2)}, u32[]{:S(2)}) collective-permute-start(f32[2,512]{1,0:T(2,128)S(1)} %get-tuple-element.18), channel_id=1, source_target_pairs={{0,3},{1,0},{2,1},{3,2},{4,7},{5,4},{6,5},{7,6},{8,11},{9,8},{10,9... | collective-permute-start | bytes 12296 | tf_op jit(solution)/shard_map/ppermute | solution.py:163
